TPU v7x, 512 devices: a whole 4x4x16 slice. The times are simulated.
512 devices in a mesh: wide: 64 (over z_hi, x, y, core), narrow: 8 (over z_lo).
Axes of the slice: x: 4, y: 4, z: 16 (z_hi: 2, z_lo: 8; z = z_hi * 8 + z_lo), core: 2. Of those that a mesh axis runs over, the one named last changes fastest.
Arguments:
- adjoint_start: float32 [2, 20, 1024, 4096], P(None, None, 'wide', 'narrow'), may hold values from -6 to 6
- velocity: float32 [2, 20, 1024, 4096], P(None, None, 'wide', 'narrow'), may hold values from -6 to 6
- coupling: float32 [19, 1024, 4096], P(None, 'wide', 'narrow'), may hold values from 30 to 300
- friction: float32 [1024, 4096], P('wide', 'narrow'), may hold values from 0.1 to 10
- horiz: float32 [1024, 4096], P('wide', 'narrow'), may hold values from 0.1 to 1
- ice_mask: int32 [1024, 4096], P('wide', 'narrow'), may hold values 0 or 1
- obs_owner: int32 [8, 262144, 1], P('narrow', 'wide'), may hold values from 0 to 63; in each aligned block of 4096 rows (0 to 4095, 4096 to 8191, ..., all dimensions but the last counted through in order) at most 128 rows name the same one
- obs_cell: int32 [8, 262144], P('narrow', 'wide'), may hold values from 0 to 8191
- obs_value: float32 [2, 8, 262144], P(None, 'narrow', 'wide'), may hold values from -6 to 6
- obs_weight: float32 [8, 262144], P('narrow', 'wide'), may hold values from 0.1 to 1
Outputs:
- adjoint: float32 [2, 20, 1024, 4096], P(None, None, 'wide', 'narrow')
- direction: float32 [1024, 4096], P('wide', 'narrow')
- misfit: float32 [], replicated
Inputs may be any that keep to these rules, and one draw needn't show every extreme that they name: `obs_owner`: among the 4096 observations of one device, at most 128 name the same owner.
All inputs are finite; a program needn't handle non-finite values. No bound on the sum of `ice_mask` on one device may be relied on, other than what follows from the above.
Results may differ from a plain program's by a relative error of at most 0.0003.
Values sent between devices are 32-bit elements; how exact they have to be, the bound alone decides.
No kernel may reach another device: no remote copies, remote signals or barrier semaphores. Data moves between devices by JAX's collectives and lax.ppermute only.
A program may use at most 128 MiB of HBM per device.

v0:
```python
import jax
import jax.numpy as jnp
from jax import lax
from jax.experimental import pallas as pl
from jax.experimental.pallas import tpu as pltpu
from jax.sharding import PartitionSpec as P

ITERS = 2
KAPPA = 1024


def neighbour_sum(value):
    edges = []
    for axis, dim in (("wide", 2), ("narrow", 3)):
        peers, length = (lax.axis_size(axis), value.shape[dim])
        up = [(i, i + 1) for i in range(peers - 1)]
        down = [(j, i) for i, j in up]
        last = lax.slice_in_dim(value, length - 1, length, axis=dim)
        first = lax.slice_in_dim(value, 0, 1, axis=dim)
        before = lax.ppermute(last, axis, up)
        after = lax.ppermute(first, axis, down)
        inner_next = lax.slice_in_dim(value, 1, length, axis=dim)
        inner_prev = lax.slice_in_dim(value, 0, length - 1, axis=dim)
        edges.append(jnp.concatenate([inner_next, after], axis=dim))
        edges.append(jnp.concatenate([before, inner_prev], axis=dim))
    return edges[0] + edges[1] + edges[2] + edges[3]


def thomas(coupling, diagonal, right_side):
    layers = diagonal.shape[0]
    pivots = diagonal[0]
    ratios = [coupling[0] / pivots]
    partial_sol = [right_side[:, 0] / pivots]
    for level in range(1, layers):
        pivots = diagonal[level] - coupling[level - 1] * ratios[level - 1]
        if level < layers - 1:
            ratios.append(coupling[level] / pivots)
        partial_sol.append(
            (right_side[:, level] + coupling[level - 1] * partial_sol[level - 1]) / pivots
        )
    result = [partial_sol[layers - 1]]
    for level in range(layers - 2, -1, -1):
        result.append(partial_sol[level] + ratios[level] * result[-1])
    ordered = result[::-1]
    return jnp.stack(ordered, axis=1)


def make_diagonal(coupling, friction, horiz):
    zeros_row = jnp.zeros_like(coupling[:1])
    below = jnp.concatenate([zeros_row, coupling], axis=0)
    above = jnp.concatenate([coupling, zeros_row], axis=0)
    diagonal = 0.5 + 4.0 * horiz[None] + below + above
    return diagonal.at[0].add(friction)


def relax(beside_all, coupling, diagonal, horiz, ice_float, force):
    right_side = horiz * beside_all
    right_side = right_side.at[:, -1].add(force)
    return ice_float * thomas(coupling, diagonal, right_side)


def column_kernel(beside_ref, coupling_ref, friction_ref, horiz_ref, ice_ref, force_ref, out_ref, ratio_ref, partial_ref):
    comps, layers = beside_ref.shape[0], beside_ref.shape[1]
    horiz = horiz_ref[...]
    base = 0.5 + 4.0 * horiz

    def diagonal(level):
        value = base
        if level > 0:
            value = value + coupling_ref[level - 1]
        if level < layers - 1:
            value = value + coupling_ref[level]
        if level == 0:
            value = value + friction_ref[...]
        return value

    def right_side(comp, level):
        value = horiz * beside_ref[comp, level]
        if level == layers - 1:
            value = value + force_ref[comp]
        return value

    pivots = diagonal(0)
    ratio_ref[0] = coupling_ref[0] / pivots
    for comp in range(comps):
        partial_ref[comp, 0] = right_side(comp, 0) / pivots
    for level in range(1, layers):
        below = coupling_ref[level - 1]
        pivots = diagonal(level) - below * ratio_ref[level - 1]
        if level < layers - 1:
            ratio_ref[level] = coupling_ref[level] / pivots
        for comp in range(comps):
            partial_ref[comp, level] = (
                right_side(comp, level) + below * partial_ref[comp, level - 1]
            ) / pivots
    ice = ice_ref[...]
    for comp in range(comps):
        result = partial_ref[comp, layers - 1]
        out_ref[comp, layers - 1] = ice * result
        for level in range(layers - 2, -1, -1):
            result = partial_ref[comp, level] + ratio_ref[level] * result
            out_ref[comp, level] = ice * result


def column_solve(beside, coupling, friction, horiz, ice_float, force):
    comps, layers, rows_x, rows_y = beside.shape
    cells = rows_x * rows_y
    return pl.pallas_call(
        column_kernel,
        out_shape=jax.ShapeDtypeStruct(beside.shape, jnp.float32),
        scratch_shapes=[
            pltpu.VMEM((layers - 1, rows_x, rows_y), jnp.float32),
            pltpu.VMEM(beside.shape, jnp.float32),
        ],
        cost_estimate=pl.CostEstimate(
            flops=12 * comps * layers * cells,
            transcendentals=0,
            bytes_accessed=4 * cells * (2 * comps * layers + layers + 4),
        ),
    )(beside, coupling, friction, horiz, ice_float, force)


def cosine_table(length):
    block = 32
    freq = lax.broadcasted_iota(jnp.int32, (1, length), 1)
    coarse = lax.broadcasted_iota(jnp.int32, (length // block, 1), 0)
    fine = lax.broadcasted_iota(jnp.int32, (block, 1), 0)
    period = 4 * length
    scale = jnp.pi / (2.0 * length)
    coarse_angle = ((2 * block * coarse * freq) % period).astype(jnp.float32) * scale
    fine_angle = (((2 * fine + 1) * freq) % period).astype(jnp.float32) * scale
    table = (
        jnp.cos(coarse_angle)[:, None, :] * jnp.cos(fine_angle)[None, :, :]
        - jnp.sin(coarse_angle)[:, None, :] * jnp.sin(fine_angle)[None, :, :]
    ).reshape(length, length)
    norm_factor = jnp.where(freq == 0, jnp.sqrt(1.0 / length), jnp.sqrt(2.0 / length))
    return table * norm_factor.astype(jnp.float32)


def smooth_lines(lines, kappa_val):
    length = lines.shape[1]
    table = cosine_table(length)
    modes = lax.iota(jnp.int32, length).astype(jnp.float32)
    spectrum = 1.0 + kappa_val * (2.0 - 2.0 * jnp.cos(jnp.pi * modes / length))
    coefficients = jnp.dot(
        lines, table, precision=lax.Precision.HIGHEST, preferred_element_type=jnp.float32
    )
    coefficients = coefficients / spectrum[None, :]
    return lax.dot_general(
        coefficients,
        table,
        (((1,), (1,)), ((), ())),
        precision=lax.Precision.HIGHEST,
        preferred_element_type=jnp.float32,
    )


def split_parts(value):
    high = lax.reduce_precision(value, exponent_bits=8, mantissa_bits=7)
    rest = value - high
    middle = lax.reduce_precision(rest, exponent_bits=8, mantissa_bits=7)
    low = rest - middle
    return jnp.concatenate([high, middle, low], axis=0).astype(jnp.bfloat16)


def exact_dot(value, selector, contract):
    rows = value.shape[0]
    parts = lax.dot_general(
        split_parts(value),
        selector,
        (((1,), (contract,)), ((), ())),
        preferred_element_type=jnp.float32,
    )
    parts = parts.reshape(3, rows, parts.shape[-1])
    return (parts[0] + parts[1]) + parts[2]


def owner_ranks(owner_hot):
    count, peers = owner_hot.shape
    block = 128
    blocks = count // block
    hot = owner_hot.astype(jnp.bfloat16).reshape(blocks, block, peers)
    lower = (
        lax.broadcasted_iota(jnp.int32, (block, block), 0)
        >= lax.broadcasted_iota(jnp.int32, (block, block), 1)
    ).astype(jnp.bfloat16)
    within = jnp.einsum("ij,bjw->biw", lower, hot, preferred_element_type=jnp.float32)
    totals = within[:, -1, :].astype(jnp.bfloat16)
    strict = (
        lax.broadcasted_iota(jnp.int32, (blocks, blocks), 0)
        > lax.broadcasted_iota(jnp.int32, (blocks, blocks), 1)
    ).astype(jnp.bfloat16)
    before = jnp.dot(strict, totals, preferred_element_type=jnp.float32)
    counts = within + before[:, None, :]
    mine = jnp.where(owner_hot.reshape(blocks, block, peers), counts, 0.0)
    return jnp.sum(mine, axis=-1).reshape(count) - 1.0


def on_device(
    adjoint_start,
    velocity,
    coupling,
    friction,
    horiz,
    ice_mask,
    obs_owner,
    obs_cell,
    obs_value,
    obs_weight,
):
    wide_count = lax.axis_size("wide")
    rows_x, rows_y = friction.shape
    owners = obs_owner[0, :, 0]
    cell_ids = obs_cell[0]
    how_many = owners.shape[0]
    capacity = 2 * how_many // wide_count
    owner_hot = owners[:, None] == jnp.arange(wide_count, dtype=jnp.int32)[None, :]
    ranking = owner_ranks(owner_hot)
    rank_hot = (
        ranking[:, None] == jnp.arange(capacity, dtype=jnp.float32)[None, :]
    ).astype(jnp.bfloat16)
    payload = jnp.stack(
        [obs_value[0, 0], obs_value[1, 0], obs_weight[0], cell_ids.astype(jnp.float32)], axis=0
    )
    spread = jnp.where(owner_hot.T[None, :, :], payload[:, None, :], 0.0)
    packed = exact_dot(spread.reshape(4 * wide_count, how_many), rank_hot, 0)
    packed = packed.reshape(4, wide_count, capacity)
    arrived = lax.all_to_all(packed, "wide", split_axis=1, concat_axis=1, tiled=True).reshape(4, -1)
    target = arrived[3].astype(jnp.int32)
    slots = target.shape[0]
    column_hot = (
        jnp.arange(rows_y, dtype=jnp.int32)[:, None] == (target % rows_y)[None, :]
    ).astype(jnp.bfloat16)
    row_hot = jnp.arange(rows_x, dtype=jnp.int32)[:, None] == (target // rows_y)[None, :]
    top = velocity[:, -1].reshape(2 * rows_x, rows_y)
    picked = exact_dot(top, column_hot, 0).reshape(2, rows_x, slots)
    surface = jnp.sum(jnp.where(row_hot[None], picked, 0.0), axis=1)
    residual = surface - arrived[:2]
    weights = arrived[2]
    weighted = weights * residual
    placed = jnp.where(row_hot[None], weighted[:, None, :], 0.0).reshape(2 * rows_x, slots)
    force = exact_dot(placed, column_hot, 1).reshape(2, rows_x, rows_y)
    local_misfit = 0.5 * jnp.sum(weights * jnp.sum(residual * residual, axis=0))
    ice_float = ice_mask.astype(jnp.float32)
    adjoint = adjoint_start
    for sweep_no in range(ITERS):
        adjoint = column_solve(neighbour_sum(adjoint), coupling, friction, horiz, ice_float, force)
    grad = -friction * ice_float * jnp.sum(adjoint[:, 0] * velocity[:, 0], axis=0)
    misfit_column = jnp.broadcast_to(local_misfit, (rows_y, 1))
    sent = jnp.concatenate([grad.T, misfit_column], axis=1)
    lines = lax.all_to_all(sent, "wide", split_axis=0, concat_axis=1, tiled=True)
    width = lines.shape[0]
    lines = lines.reshape(width, wide_count, rows_x + 1)
    wide_misfit = jnp.sum(lines[0, :, rows_x])
    lines = lines[:, :, :rows_x].reshape(width, wide_count * rows_x)
    smooth = smooth_lines(lines, float(KAPPA))
    local_square = jnp.sum(smooth * smooth)
    square_column = jnp.broadcast_to(local_square, (width, wide_count, 1))
    returned = jnp.concatenate([smooth.reshape(width, wide_count, rows_x), square_column], axis=2)
    returned = returned.reshape(width, wide_count * (rows_x + 1))
    back = lax.all_to_all(returned, "wide", split_axis=1, concat_axis=0, tiled=True)
    wide_square = jnp.sum(back[::width, rows_x])
    back = back[:, :rows_x].T
    totals = lax.psum(jnp.stack([wide_square, wide_misfit]), "narrow")
    cell_total = wide_count * rows_x * rows_y * lax.axis_size("narrow")
    direction = back * lax.rsqrt(totals[0] / cell_total + 1e-06)
    return (adjoint, direction, totals[1])


def solution(mesh):
    in_specs = (
        P(None, None, "wide", "narrow"),
        P(None, None, "wide", "narrow"),
        P(None, "wide", "narrow"),
        P("wide", "narrow"),
        P("wide", "narrow"),
        P("wide", "narrow"),
        P("narrow", "wide", None),
        P("narrow", "wide"),
        P(None, "narrow", "wide"),
        P("narrow", "wide"),
    )
    out_specs = (P(None, None, "wide", "narrow"), P("wide", "narrow"), P())
    return jax.shard_map(
        on_device, mesh=mesh, in_specs=in_specs, out_specs=out_specs, check_vma=False
    )
```

profile of v0, /device:TPU:6, one launch (start us, length us, event | category | flops | bytes accessed | tf_op | source)
XLA Modules:
  0.0 214.1 jit_solution(7657856855985007942)
XLA Ops:
  7.6 21.3 %all-to-all-start = ((f32[4,64,128]{2,0,1:T(4,128)}), f32[4,64,128]{2,0,1:T(4,128)S(1)}, u32[]{:S(2)}, u32[]{:S(2)}) async-start(f32[4,64,128]{2,0,1:T(4,128)} %copy.18), calls=%async_computation | async-start | bytes 262144 | tf_op jit(solution)/shard_map/all_to_all | solution.py:228
  30.4 4.6 %collective-permute-start.3 = (f32[2,20,16,1]{3,2,1,0:T(8,128)S(1)}, f32[2,20,16,1]{3,2,1,0:T(8,128)S(1)}, u32[]{:S(2)}, u32[]{:S(2)}) collective-permute-start(f32[2,20,16,1]{3,2,1,0:T(8,128)S(1)} %get-tuple-element.20), channel_id=1, source_target_pairs={{0,1},{1,2},{2,3},{3,4},{4,5},{5,6},{6,7},{8,9},{9,10},{10,11},{11... | collective-permute-start | bytes 7688 | tf_op jit(solution)/shard_map/ppermute | solution.py:20
  35.1 4.1 %collective-permute-start = (f32[2,20,1,512]{3,2,1,0:T(1,128)S(1)}, f32[2,20,1,512]{3,2,1,0:T(1,128)S(1)}, u32[]{:S(2)}, u32[]{:S(2)}) collective-permute-start(f32[2,20,1,512]{3,2,1,0:T(1,128)S(1)} %get-tuple-element.25), channel_id=1, source_target_pairs={{8,0},{16,8},{24,16},{32,24},{40,32},{48,40},{56,48},{64,56},{72,6... | collective-permute-start | bytes 245768 | tf_op jit(solution)/shard_map/ppermute | solution.py:21
  39.2 2.1 collective-permute-start.1
  42.9 4.4 %multiply_subtract_fusion = (f32[32,32,1024]{2,1,0:T(8,128)}, f32[32,32,1024]{2,1,0:T(8,128)}) fusion(f32[32,1024]{1,0:T(8,128)S(1)} %get-tuple-element.47, f32[32,1024]{1,0:T(8,128)S(1)} %get-tuple-element.50, f32[32,1024]{1,0:T(8,128)S(1)} %get-tuple-element.46, f32[32,1024]{1,0:T(8,128)S(1)} %get-tuple-element.51, f32[1024]{0:T(1024)S(1)} %fusion.57), kind=kLoop, calls=%fused_computation.17 | loop fusion | flops 4194304 | bytes 8916992 | tf_op jit(solution)/shard_map/sub | solution.py:133
  48.7 2.0 fusion.17.beside_ref
  50.9 3.2 %fusion.1 = f32[96,8192]{1,0:T(8,128)S(1)} fusion(s32[8192]{0:T(1024)S(1)} %get-tuple-element.39, bf16[32,512]{1,0:T(8,128)(2,1)S(1)} %get-tuple-element.36, bf16[32,512]{1,0:T(8,128)(2,1)S(1)} %get-tuple-element.37, bf16[32,512]{1,0:T(8,128)(2,1)S(1)} %get-tuple-element.35), kind=kOutput, calls=%fused_computation.2 | convolution fusion | flops 809795584 | bytes 3276800 | tf_op jit(solution)/shard_map/dot_general | solution.py:168
  55.6 3.2 %fusion = f32[96,512]{1,0:T(8,128)S(1)} fusion(s32[8192]{0:T(1024)S(1)} %get-tuple-element.39, bf16[32,8192]{1,0:T(8,128)(2,1)S(1)} %get-tuple-element.29, bf16[32,8192]{1,0:T(8,128)(2,1)S(1)} %get-tuple-element.30, bf16[32,8192]{1,0:T(8,128)(2,1)S(1)} %get-tuple-element.28), kind=kOutput, calls=%fused_computation.1 | convolution fusion | flops 814219264 | bytes 1802240 | tf_op jit(solution)/shard_map/dot_general | solution.py:168
  59.5 3.2 %shard_map.121 = f32[2,20,16,512]{3,2,1,0:T(8,128)} custom-call(f32[2,20,16,512]{3,2,1,0:T(8,128)} %fusion.17.beside_ref, f32[19,16,512]{2,1,0:T(8,128)} %coupling_ref.3, f32[16,512]{1,0:T(8,128)} %friction_ref.3, f32[16,512]{1,0:T(8,128)} %horiz_ref.3, f32[16,512]{1,0:T(8,128)} %convert_element_type.63.ice_ref, f32[2,16,512]{2,1,0:T(8,128)} %bitcast.86), custom_call_target="tpu_custom_call" | custom-call | flops 3932160 | bytes 3407872 | tf_op jit(solution)/shard_map/pallas_call | solution.py:108
  62.6 2.4 %fusion.62 = (f32[2,20,16,511]{3,2,1,0:T(8,128)S(1)}, f32[2,20,16,511]{3,2,1,0:T(8,128)S(1)}) fusion(f32[2,20,16,512]{3,2,1,0:T(8,128)} %shard_map.121), kind=kLoop, calls=%fused_computation.129 | loop fusion | bytes 5232640 | tf_op jit(solution)/shard_map/slice | solution.py:23
  68.1 4.6 %collective-permute-start.7 = (f32[2,20,16,1]{3,2,1,0:T(8,128)}, f32[2,20,16,1]{3,2,1,0:T(8,128)S(1)}, u32[]{:S(2)}, u32[]{:S(2)}) collective-permute-start(f32[2,20,16,1]{3,2,1,0:T(8,128)} %get-tuple-element.12), channel_id=1, source_target_pairs={{0,1},{1,2},{2,3},{3,4},{4,5},{5,6},{6,7},{8,9},{9,10},{10,11},{11... | collective-permute-start | bytes 7688 | tf_op jit(solution)/shard_map/ppermute | solution.py:20
  72.7 5.2 %collective-permute-start.4 = (f32[2,20,1,512]{3,2,1,0:T(1,128)}, f32[2,20,1,512]{3,2,1,0:T(1,128)S(1)}, u32[]{:S(2)}, u32[]{:S(2)}) collective-permute-start(f32[2,20,1,512]{3,2,1,0:T(1,128)} %get-tuple-element.17), channel_id=1, source_target_pairs={{8,0},{16,8},{24,16},{32,24},{40,32},{48,40},{56,48},{64,56},{72,6... | collective-permute-start | bytes 245768 | tf_op jit(solution)/shard_map/ppermute | solution.py:21
  77.9 2.1 collective-permute-start.5
  82.5 3.4 %collective-permute-done.5 = f32[2,20,1,512]{3,2,1,0:T(1,128)S(1)} collective-permute-done((f32[2,20,1,512]{3,2,1,0:T(1,128)}, f32[2,20,1,512]{3,2,1,0:T(1,128)S(1)}, u32[]{:S(2)}, u32[]{:S(2)}) %collective-permute-start.5) | collective-permute-done | bytes 81952 | tf_op jit(solution)/shard_map/ppermute | solution.py:20
  85.9 3.6 %fusion.19.beside_ref = f32[2,20,16,512]{3,2,1,0:T(8,128)} fusion(f32[2,20,1,512]{3,2,1,0:T(1,128)S(1)} %collective-permute-done.4, f32[2,20,15,512]{3,2,1,0:T(8,128)} %get-tuple-element.19, f32[2,20,15,512]{3,2,1,0:T(8,128)} %get-tuple-element.18, f32[2,20,1,512]{3,2,1,0:T(1,128)S(1)} %collective-permute-done.5, ...), kind=kLoop, calls=%fused_computation.35 | loop fusion | flops 2293760 | bytes 6553600 | tf_op jit(solution)/shard_map/add | solution.py:26
  89.5 3.2 %shard_map.122 = f32[2,20,16,512]{3,2,1,0:T(8,128)} custom-call(f32[2,20,16,512]{3,2,1,0:T(8,128)} %fusion.19.beside_ref, f32[19,16,512]{2,1,0:T(8,128)} %coupling_ref.3, f32[16,512]{1,0:T(8,128)} %friction_ref.3, f32[16,512]{1,0:T(8,128)} %horiz_ref.3, f32[16,512]{1,0:T(8,128)} %convert_element_type.63.ice_ref, f32[2,16,512]{2,1,0:T(8,128)} %bitcast.87), custom_call_target="tpu_custom_call" | custom-call | flops 3932160 | bytes 3407872 | tf_op jit(solution)/shard_map/pallas_call | solution.py:108
  94.6 36.2 %all-to-all-start.1 = ((f32[64,1,136]{2,1,0:T(1,128)}), f32[64,1,136]{2,1,0:T(1,128)S(1)}, u32[]{:S(2)}, u32[]{:S(2)}) async-start(f32[64,1,136]{2,1,0:T(1,128)} %reshape.380), calls=%async_computation.1 | async-start | bytes 131072 | tf_op jit(solution)/shard_map/all_to_all | solution.py:251
  130.9 5.0 %bitcast_multiply_fusion = f32[1024,1024]{1,0:T(8,128)} fusion(f32[32,32,1024]{2,1,0:T(8,128)} %get-tuple-element.31, f32[1024]{0:T(1024)S(1)} %fusion.57), kind=kLoop, calls=%fused_computation.16 | loop fusion | flops 1048576 | bytes 8392704 | tf_op jit(solution)/shard_map/mul | solution.py:137
  135.9 10.8 %all-to-all-done.1 = f32[64,1,136]{2,1,0:T(1,128)S(1)} async-done(((f32[64,1,136]{2,1,0:T(1,128)}), f32[64,1,136]{2,1,0:T(1,128)S(1)}, u32[]{:S(2)}, u32[]{:S(2)}) %all-to-all-start.1) | async-done | bytes 34848 | tf_op jit(solution)/shard_map/all_to_all | solution.py:251
  148.4 4.4 %convolution_divide_fusion = f32[8,1024]{1,0:T(8,128)S(1)} fusion(f32[8,1024]{1,0:T(8,128)S(1)} %reshape.376, f32[1024,1024]{1,0:T(8,128)} %bitcast.83, f32[1024]{0:T(1024)S(1)} %multiply_add_fusion), kind=kOutput, calls=%fused_computation.36 | convolution fusion | flops 100671488 | bytes 4263936 | tf_op jit(solution)/shard_map/dot_general | solution.py:145
  152.8 4.2 %multiply_reduce_fusion = (f32[]{:T(128)}, f32[8,1024]{1,0:T(8,128)S(1)}) fusion(f32[8,1024]{1,0:T(8,128)S(1)} %convolution_divide_fusion, f32[1024,1024]{1,0:T(8,128)S(1)} %copy-done.2), kind=kOutput, calls=%fused_computation.108 | convolution fusion | flops 100679680 | bytes 4259844 | tf_op jit(solution)/shard_map/dot_general | solution.py:149
  158.8 6.8 %all-to-all-start.2 = ((f32[64,1,136]{2,1,0:T(1,128)}), f32[64,1,136]{2,1,0:T(1,128)S(1)}, u32[]{:S(2)}, u32[]{:S(2)}) async-start(f32[64,1,136]{2,1,0:T(1,128)} %reshape.382), calls=%async_computation.2 | async-start | bytes 131072 | tf_op jit(solution)/shard_map/all_to_all | solution.py:261
  166.4 15.1 %all-to-all-done.2 = f32[64,1,136]{2,1,0:T(1,128)S(1)} async-done(((f32[64,1,136]{2,1,0:T(1,128)}), f32[64,1,136]{2,1,0:T(1,128)S(1)}, u32[]{:S(2)}, u32[]{:S(2)}) %all-to-all-start.2) | async-done | bytes 34848 | tf_op jit(solution)/shard_map/all_to_all | solution.py:261
  184.5 27.6 %psum.7 = f32[2]{0:T(128)S(1)} all-reduce(f32[2]{0:T(128)S(1)} %pad_maximum_fusion.1), channel_id=1, replica_groups=mesh['wide'=64,'narrow'=8] {'narrow'}, use_global_device_ids=true, to_apply=%region_8.9 | all-reduce | flops 2 | bytes 16 | tf_op jit(solution)/shard_map/psum | solution.py:264
  (95 shorter events, 29.0 us)
Async XLA Ops:
  0.6 1.9 copy-start.5
  1.7 1.2 copy-start.7
  1.8 1.2 copy-start.8
  1.8 1.4 copy-start.9
  4.9 24.0 %copy-start.1 = (f32[2,20,16,512]{3,2,1,0:T(8,128)S(1)}, f32[2,20,16,512]{3,2,1,0:T(8,128)}, u32[]{:S(2)}) copy-start(f32[2,20,16,512]{3,2,1,0:T(8,128)} %param.10) | copy-start | bytes 3932164
  7.6 43.1 %all-to-all-start = ((f32[4,64,128]{2,0,1:T(4,128)}), f32[4,64,128]{2,0,1:T(4,128)S(1)}, u32[]{:S(2)}, u32[]{:S(2)}) async-start(f32[4,64,128]{2,0,1:T(4,128)} %copy.18), calls=%async_computation | async-start | bytes 262144 | tf_op jit(solution)/shard_map/all_to_all | solution.py:228
  29.1 19.7 %collective-permute-start.2 = (f32[2,20,16,1]{3,2,1,0:T(8,128)S(1)}, f32[2,20,16,1]{3,2,1,0:T(8,128)S(1)}, u32[]{:S(2)}, u32[]{:S(2)}) collective-permute-start(f32[2,20,16,1]{3,2,1,0:T(8,128)S(1)} %get-tuple-element.21), channel_id=1, source_target_pairs={{1,0},{2,1},{3,2},{4,3},{5,4},{6,5},{7,6},{9,8},{10,9},{11,10},{12... | collective-permute-start | bytes 7688 | tf_op jit(solution)/shard_map/ppermute | solution.py:21
  30.4 18.4 %collective-permute-start.3 = (f32[2,20,16,1]{3,2,1,0:T(8,128)S(1)}, f32[2,20,16,1]{3,2,1,0:T(8,128)S(1)}, u32[]{:S(2)}, u32[]{:S(2)}) collective-permute-start(f32[2,20,16,1]{3,2,1,0:T(8,128)S(1)} %get-tuple-element.20), channel_id=1, source_target_pairs={{0,1},{1,2},{2,3},{3,4},{4,5},{5,6},{6,7},{8,9},{9,10},{10,11},{11... | collective-permute-start | bytes 7688 | tf_op jit(solution)/shard_map/ppermute | solution.py:20
  35.1 13.6 %collective-permute-start = (f32[2,20,1,512]{3,2,1,0:T(1,128)S(1)}, f32[2,20,1,512]{3,2,1,0:T(1,128)S(1)}, u32[]{:S(2)}, u32[]{:S(2)}) collective-permute-start(f32[2,20,1,512]{3,2,1,0:T(1,128)S(1)} %get-tuple-element.25), channel_id=1, source_target_pairs={{8,0},{16,8},{24,16},{32,24},{40,32},{48,40},{56,48},{64,56},{72,6... | collective-permute-start | bytes 245768 | tf_op jit(solution)/shard_map/ppermute | solution.py:21
  39.2 9.6 %collective-permute-start.1 = (f32[2,20,1,512]{3,2,1,0:T(1,128)S(1)}, f32[2,20,1,512]{3,2,1,0:T(1,128)S(1)}, u32[]{:S(2)}, u32[]{:S(2)}) collective-permute-start(f32[2,20,1,512]{3,2,1,0:T(1,128)S(1)} %get-tuple-element.24), channel_id=1, source_target_pairs={{0,8},{8,16},{16,24},{24,32},{32,40},{40,48},{48,56},{56,64},{64,7... | collective-permute-start | bytes 245768 | tf_op jit(solution)/shard_map/ppermute | solution.py:20
  47.2 0.8 slice-start
  47.2 0.9 copy-start.6
  62.6 2.4 %copy-start = (f32[2,20,16,512]{3,2,1,0:T(8,128)S(1)}, f32[2,20,16,512]{3,2,1,0:T(8,128)}, u32[]{:S(2)}) copy-start(f32[2,20,16,512]{3,2,1,0:T(8,128)} %shard_map.121) | copy-start | bytes 3932164
  66.8 15.7 %collective-permute-start.6 = (f32[2,20,16,1]{3,2,1,0:T(8,128)}, f32[2,20,16,1]{3,2,1,0:T(8,128)S(1)}, u32[]{:S(2)}, u32[]{:S(2)}) collective-permute-start(f32[2,20,16,1]{3,2,1,0:T(8,128)} %get-tuple-element.13), channel_id=1, source_target_pairs={{1,0},{2,1},{3,2},{4,3},{5,4},{6,5},{7,6},{9,8},{10,9},{11,10},{12... | collective-permute-start | bytes 7688 | tf_op jit(solution)/shard_map/ppermute | solution.py:21
  68.1 14.4 %collective-permute-start.7 = (f32[2,20,16,1]{3,2,1,0:T(8,128)}, f32[2,20,16,1]{3,2,1,0:T(8,128)S(1)}, u32[]{:S(2)}, u32[]{:S(2)}) collective-permute-start(f32[2,20,16,1]{3,2,1,0:T(8,128)} %get-tuple-element.12), channel_id=1, source_target_pairs={{0,1},{1,2},{2,3},{3,4},{4,5},{5,6},{6,7},{8,9},{9,10},{10,11},{11... | collective-permute-start | bytes 7688 | tf_op jit(solution)/shard_map/ppermute | solution.py:20
  72.7 9.8 %collective-permute-start.4 = (f32[2,20,1,512]{3,2,1,0:T(1,128)}, f32[2,20,1,512]{3,2,1,0:T(1,128)S(1)}, u32[]{:S(2)}, u32[]{:S(2)}) collective-permute-start(f32[2,20,1,512]{3,2,1,0:T(1,128)} %get-tuple-element.17), channel_id=1, source_target_pairs={{8,0},{16,8},{24,16},{32,24},{40,32},{48,40},{56,48},{64,56},{72,6... | collective-permute-start | bytes 245768 | tf_op jit(solution)/shard_map/ppermute | solution.py:21
  77.9 8.1 %collective-permute-start.5 = (f32[2,20,1,512]{3,2,1,0:T(1,128)}, f32[2,20,1,512]{3,2,1,0:T(1,128)S(1)}, u32[]{:S(2)}, u32[]{:S(2)}) collective-permute-start(f32[2,20,1,512]{3,2,1,0:T(1,128)} %get-tuple-element.16), channel_id=1, source_target_pairs={{0,8},{8,16},{16,24},{24,32},{32,40},{40,48},{48,56},{56,64},{64,7... | collective-permute-start | bytes 245768 | tf_op jit(solution)/shard_map/ppermute | solution.py:20
  89.5 3.2 %copy-start.4 = (f32[2,20,16,512]{3,2,1,0:T(8,128)S(1)}, f32[2,20,16,512]{3,2,1,0:T(8,128)}, u32[]{:S(2)}) copy-start(f32[2,20,16,512]{3,2,1,0:T(8,128)} %param.11) | copy-start | bytes 3932164
  89.5 4.0 %copy-start.3 = (f32[16,512]{1,0:T(8,128)S(1)}, f32[16,512]{1,0:T(8,128)}, u32[]{:S(2)}) copy-start(f32[16,512]{1,0:T(8,128)} %friction_ref.3) | copy-start | bytes 98308
  94.6 52.1 %all-to-all-start.1 = ((f32[64,1,136]{2,1,0:T(1,128)}), f32[64,1,136]{2,1,0:T(1,128)S(1)}, u32[]{:S(2)}, u32[]{:S(2)}) async-start(f32[64,1,136]{2,1,0:T(1,128)} %reshape.380), calls=%async_computation.1 | async-start | bytes 131072 | tf_op jit(solution)/shard_map/all_to_all | solution.py:251
  148.4 4.4 %copy-start.2 = (f32[1024,1024]{1,0:T(8,128)S(1)}, f32[1024,1024]{1,0:T(8,128)}, u32[]{:S(2)}) copy-start(f32[1024,1024]{1,0:T(8,128)} %bitcast_multiply_fusion) | copy-start | bytes 12582916
  158.8 22.7 %all-to-all-start.2 = ((f32[64,1,136]{2,1,0:T(1,128)}), f32[64,1,136]{2,1,0:T(1,128)S(1)}, u32[]{:S(2)}, u32[]{:S(2)}) async-start(f32[64,1,136]{2,1,0:T(1,128)} %reshape.382), calls=%async_computation.2 | async-start | bytes 131072 | tf_op jit(solution)/shard_map/all_to_all | solution.py:261
where the time goes:
time: 215 us; the launch traced here: 214 us
  starting transfers between devices  89.5 us (42%)
  waiting for transfers between devices  29.4 us (14%)
  blocking collectives  27.6 us (13%)
  other arithmetic  26.6 us (12%)
  matrix products  18.2 us (8%)
  local copies, waits for them, and re-layouts  14.1 us (7%)
  Pallas kernels  6.32 us (3%)
  between operations  2.52 us (1%)
    all_to_all x1, starting transfers between devices, on_device(): lax.all_to_all(sent, 'wide', split_axis=0, concat_axis=1, tiled=True)  36.2 us
    psum x1, blocking collectives, on_device(): totals = lax.psum(jnp.stack([wide_square, wide_misfit]), 'narrow')  27.6 us
    all_to_all x1, starting transfers between devices, on_device(): lax.all_to_all(packed, 'wide', split_axis=1, concat_axis=1, tiled=True)  21.3 us
    all_to_all x1, waiting for transfers between devices, on_device(): lax.all_to_all(returned, 'wide', split_axis=1, concat_axis=0, tiled=True)  15.1 us
    ppermute x4, starting transfers between devices, neighbour_sum(): before = lax.ppermute(last, axis, up)  13.4 us
    ppermute x4, starting transfers between devices, neighbour_sum(): after = lax.ppermute(first, axis, down)  11.8 us
    all_to_all x1, waiting for transfers between devices, on_device(): lax.all_to_all(sent, 'wide', split_axis=0, concat_axis=1, tiled=True)  10.8 us
    dot_general x3, matrix products, exact_dot(): lax.dot_general(split_parts(value), selector, (((1,), (contract,)), ((),...  8.35 us
  transfers between devices with their start and end apart: 11, of which 3 were waited for; matrix products, arithmetic and copies ran while one was open for 8% of the time, Pallas kernels for 0%

commit v1 on v0

--- a/solution.py
+++ b/solution.py
@@ -120,9 +120,10 @@
     )(beside, coupling, friction, horiz, ice_float, force)
 
 
-def cosine_table(length):
+def cosine_table(length, after):
     block = 32
     freq = lax.broadcasted_iota(jnp.int32, (1, length), 1)
+    freq, _ = lax.optimization_barrier((freq, after))
     coarse = lax.broadcasted_iota(jnp.int32, (length // block, 1), 0)
     fine = lax.broadcasted_iota(jnp.int32, (block, 1), 0)
     period = 4 * length
@@ -137,9 +138,8 @@
     return table * norm_factor.astype(jnp.float32)
 
 
-def smooth_lines(lines, kappa_val):
+def smooth_lines(lines, kappa_val, table):
     length = lines.shape[1]
-    table = cosine_table(length)
     modes = lax.iota(jnp.int32, length).astype(jnp.float32)
     spectrum = 1.0 + kappa_val * (2.0 - 2.0 * jnp.cos(jnp.pi * modes / length))
     coefficients = jnp.dot(
@@ -248,12 +248,13 @@
     grad = -friction * ice_float * jnp.sum(adjoint[:, 0] * velocity[:, 0], axis=0)
     misfit_column = jnp.broadcast_to(local_misfit, (rows_y, 1))
     sent = jnp.concatenate([grad.T, misfit_column], axis=1)
+    table = cosine_table(wide_count * rows_x, sent)
     lines = lax.all_to_all(sent, "wide", split_axis=0, concat_axis=1, tiled=True)
     width = lines.shape[0]
     lines = lines.reshape(width, wide_count, rows_x + 1)
     wide_misfit = jnp.sum(lines[0, :, rows_x])
     lines = lines[:, :, :rows_x].reshape(width, wide_count * rows_x)
-    smooth = smooth_lines(lines, float(KAPPA))
+    smooth = smooth_lines(lines, float(KAPPA), table)
     local_square = jnp.sum(smooth * smooth)
     square_column = jnp.broadcast_to(local_square, (width, wide_count, 1))
     returned = jnp.concatenate([smooth.reshape(width, wide_count, rows_x), square_column], axis=2)

time: 215 us -> 213 us (level)
  starting transfers between devices: 89.5 us -> 70.5 us
  waiting for transfers between devices: 29.4 us -> 41.2 us
  blocking collectives: 27.6 us -> 33.7 us
  other arithmetic: 26.6 us -> 22.2 us
  local copies, waits for them, and re-layouts: 14.1 us -> 17.4 us
    all_to_all x1, starting transfers between devices: 36.2 us -> 18.1 us  [on_device(): lax.all_to_all(sent, 'wide', split_axis=0, concat_axis=1, tiled=True)]
    all_to_all x1, waiting for transfers between devices: 0.01 us -> 12.4 us  [on_device(): lax.all_to_all(packed, 'wide', split_axis=1, concat_axis=1, tiled=True)]
    psum x1, blocking collectives: 27.6 us -> 33.7 us  [on_device(): totals = lax.psum(jnp.stack([wide_square, wide_misfit]), 'narrow')]
    ppermute x4, waiting for transfers between devices: 0.01 us -> 3.93 us  [neighbour_sum(): after = lax.ppermute(first, axis, down)]
    slice x4, local copies, waits for them, and re-layouts: 2.07 us -> 5.75 us  [neighbour_sum(): last = lax.slice_in_dim(value, length - 1, length, axis=dim)]
    mul x1, other arithmetic: 5.01 us -> 2.48 us  [cosine_table(): return table * norm_factor.astype(jnp.float32)]
  transfers between devices with their start and end apart: 11 -> 11, of which waited for: 3 -> 5; matrix products, arithmetic and copies ran while one was open for 8% -> 9% of each run, Pallas kernels for 0% -> 0%
where the time goes in v1:
time: 213 us; the launch traced here: 211 us
  starting transfers between devices  70.5 us (33%)
  waiting for transfers between devices  41.2 us (19%)
  blocking collectives  33.7 us (16%)
  other arithmetic  22.2 us (10%)
  local copies, waits for them, and re-layouts  17.4 us (8%)
  matrix products  17.4 us (8%)
  Pallas kernels  6.27 us (3%)
  between operations  2.52 us (1%)
    psum x1, blocking collectives, on_device(): totals = lax.psum(jnp.stack([wide_square, wide_misfit]), 'narrow')  33.7 us
    all_to_all x1, starting transfers between devices, on_device(): lax.all_to_all(packed, 'wide', split_axis=1, concat_axis=1, tiled=True)  21.1 us
    all_to_all x1, starting transfers between devices, on_device(): lax.all_to_all(sent, 'wide', split_axis=0, concat_axis=1, tiled=True)  18.1 us
    all_to_all x1, waiting for transfers between devices, on_device(): lax.all_to_all(returned, 'wide', split_axis=1, concat_axis=0, tiled=True)  14.6 us
    ppermute x4, starting transfers between devices, neighbour_sum(): before = lax.ppermute(last, axis, up)  13 us
    all_to_all x1, waiting for transfers between devices, on_device(): lax.all_to_all(packed, 'wide', split_axis=1, concat_axis=1, tiled=True)  12.4 us
    ppermute x4, starting transfers between devices, neighbour_sum(): after = lax.ppermute(first, axis, down)  9.74 us
    all_to_all x1, waiting for transfers between devices, on_device(): lax.all_to_all(sent, 'wide', split_axis=0, concat_axis=1, tiled=True)  9.04 us
  transfers between devices with their start and end apart: 11, of which 5 were waited for; matrix products, arithmetic and copies ran while one was open for 9% of the time, Pallas kernels for 0%

profile of v1, /device:TPU:6, one launch (start us, length us, event | category | flops | bytes accessed | tf_op | source)
XLA Modules:
  0.0 211.2 jit_solution(3759522247540526188)
XLA Ops:
  2.1 4.6 %collective-permute-start = (f32[2,20,1,512]{3,2,1,0:T(1,128)S(1)}, f32[2,20,1,512]{3,2,1,0:T(1,128)S(1)}, u32[]{:S(2)}, u32[]{:S(2)}) collective-permute-start(f32[2,20,1,512]{3,2,1,0:T(1,128)S(1)} %get-tuple-element.27), channel_id=1, source_target_pairs={{8,0},{16,8},{24,16},{32,24},{40,32},{48,40},{56,48},{64,56},{72,6... | collective-permute-start | bytes 245768 | tf_op jit(solution)/shard_map/ppermute | solution.py:21
  11.2 4.6 %collective-permute-start.3 = (f32[2,20,16,1]{3,2,1,0:T(8,128)S(1)}, f32[2,20,16,1]{3,2,1,0:T(8,128)S(1)}, u32[]{:S(2)}, u32[]{:S(2)}) collective-permute-start(f32[2,20,16,1]{3,2,1,0:T(8,128)S(1)} %get-tuple-element.22), channel_id=1, source_target_pairs={{0,1},{1,2},{2,3},{3,4},{4,5},{5,6},{6,7},{8,9},{9,10},{10,11},{11... | collective-permute-start | bytes 7688 | tf_op jit(solution)/shard_map/ppermute | solution.py:20
  22.0 21.1 %all-to-all-start = ((f32[4,64,128]{2,0,1:T(4,128)}), f32[4,64,128]{2,0,1:T(4,128)S(1)}, u32[]{:S(2)}, u32[]{:S(2)}) async-start(f32[4,64,128]{2,0,1:T(4,128)} %copy.18), calls=%async_computation | async-start | bytes 262144 | tf_op jit(solution)/shard_map/all_to_all | solution.py:228
  46.8 12.4 %all-to-all-done = f32[4,64,128]{2,0,1:T(4,128)S(1)} async-done(((f32[4,64,128]{2,0,1:T(4,128)}), f32[4,64,128]{2,0,1:T(4,128)S(1)}, u32[]{:S(2)}, u32[]{:S(2)}) %all-to-all-start) | async-done | bytes 131104 | tf_op jit(solution)/shard_map/all_to_all | solution.py:228
  59.3 3.2 %fusion.1 = f32[96,8192]{1,0:T(8,128)S(1)} fusion(s32[8192]{0:T(1024)S(1)} %get-tuple-element.41, bf16[32,512]{1,0:T(8,128)(2,1)S(1)} %get-tuple-element.38, bf16[32,512]{1,0:T(8,128)(2,1)S(1)} %get-tuple-element.39, bf16[32,512]{1,0:T(8,128)(2,1)S(1)} %get-tuple-element.37), kind=kOutput, calls=%fused_computation.2 | convolution fusion | flops 809795584 | bytes 3276800 | tf_op jit(solution)/shard_map/dot_general | solution.py:168
  64.0 3.2 %fusion = f32[96,512]{1,0:T(8,128)S(1)} fusion(s32[8192]{0:T(1024)S(1)} %get-tuple-element.41, bf16[32,8192]{1,0:T(8,128)(2,1)S(1)} %get-tuple-element.31, bf16[32,8192]{1,0:T(8,128)(2,1)S(1)} %get-tuple-element.32, bf16[32,8192]{1,0:T(8,128)(2,1)S(1)} %get-tuple-element.30), kind=kOutput, calls=%fused_computation.1 | convolution fusion | flops 814219264 | bytes 1802240 | tf_op jit(solution)/shard_map/dot_general | solution.py:168
  67.9 3.1 %shard_map.121 = f32[2,20,16,512]{3,2,1,0:T(8,128)} custom-call(f32[2,20,16,512]{3,2,1,0:T(8,128)} %fusion.17.beside_ref, f32[19,16,512]{2,1,0:T(8,128)} %coupling_ref.3, f32[16,512]{1,0:T(8,128)} %friction_ref.3, f32[16,512]{1,0:T(8,128)} %horiz_ref.3, f32[16,512]{1,0:T(8,128)} %convert_element_type.59.ice_ref, f32[2,16,512]{2,1,0:T(8,128)} %bitcast.88), custom_call_target="tpu_custom_call" | custom-call | flops 3932160 | bytes 3407872 | tf_op jit(solution)/shard_map/pallas_call | solution.py:108
  71.0 2.1 fusion.56
  73.1 2.2 %fusion.57 = (f32[2,20,15,512]{3,2,1,0:T(8,128)S(1)}, f32[2,20,15,512]{3,2,1,0:T(8,128)S(1)}) fusion(f32[2,20,16,512]{3,2,1,0:T(8,128)} %shard_map.121), kind=kLoop, calls=%fused_computation.127 | loop fusion | bytes 4915200 | tf_op jit(solution)/shard_map/slice | solution.py:23
  76.2 2.5 %collective-permute-start.4 = (f32[2,20,1,512]{3,2,1,0:T(1,128)}, f32[2,20,1,512]{3,2,1,0:T(1,128)S(1)}, u32[]{:S(2)}, u32[]{:S(2)}) collective-permute-start(f32[2,20,1,512]{3,2,1,0:T(1,128)} %get-tuple-element.19), channel_id=1, source_target_pairs={{8,0},{16,8},{24,16},{32,24},{40,32},{48,40},{56,48},{64,56},{72,6... | collective-permute-start | bytes 245768 | tf_op jit(solution)/shard_map/ppermute | solution.py:21
  82.0 4.6 %collective-permute-start.7 = (f32[2,20,16,1]{3,2,1,0:T(8,128)}, f32[2,20,16,1]{3,2,1,0:T(8,128)S(1)}, u32[]{:S(2)}, u32[]{:S(2)}) collective-permute-start(f32[2,20,16,1]{3,2,1,0:T(8,128)} %get-tuple-element.14), channel_id=1, source_target_pairs={{0,1},{1,2},{2,3},{3,4},{4,5},{5,6},{6,7},{8,9},{9,10},{10,11},{11... | collective-permute-start | bytes 7688 | tf_op jit(solution)/shard_map/ppermute | solution.py:20
  86.6 2.0 fusion.55
  89.2 3.9 %collective-permute-done.6 = f32[2,20,16,1]{3,2,1,0:T(8,128)S(1)} collective-permute-done((f32[2,20,16,1]{3,2,1,0:T(8,128)}, f32[2,20,16,1]{3,2,1,0:T(8,128)S(1)}, u32[]{:S(2)}, u32[]{:S(2)}) %collective-permute-start.6) | collective-permute-done | bytes 2592 | tf_op jit(solution)/shard_map/ppermute | solution.py:21
  94.4 3.5 %fusion.19.beside_ref = f32[2,20,16,512]{3,2,1,0:T(8,128)} fusion(f32[2,20,1,512]{3,2,1,0:T(1,128)S(1)} %collective-permute-done.4, f32[2,20,15,512]{3,2,1,0:T(8,128)S(1)} %get-tuple-element.21, f32[2,20,15,512]{3,2,1,0:T(8,128)S(1)} %get-tuple-element.20, f32[2,20,1,512]{3,2,1,0:T(1,128)S(1)} %collective-permute-done.5, ...), kind=kLoop, calls=%fused_computation.35 | loop fusion | flops 2293760 | bytes 6553600 | tf_op jit(solution)/shard_map/add | solution.py:26
  98.0 3.2 %shard_map.122 = f32[2,20,16,512]{3,2,1,0:T(8,128)} custom-call(f32[2,20,16,512]{3,2,1,0:T(8,128)} %fusion.19.beside_ref, f32[19,16,512]{2,1,0:T(8,128)} %coupling_ref.3, f32[16,512]{1,0:T(8,128)} %friction_ref.3, f32[16,512]{1,0:T(8,128)} %horiz_ref.3, f32[16,512]{1,0:T(8,128)} %convert_element_type.59.ice_ref, f32[2,16,512]{2,1,0:T(8,128)} %bitcast.89), custom_call_target="tpu_custom_call" | custom-call | flops 3932160 | bytes 3407872 | tf_op jit(solution)/shard_map/pallas_call | solution.py:108
  103.0 18.1 %all-to-all-start.1 = ((f32[64,1,136]{2,1,0:T(1,128)}), f32[64,1,136]{2,1,0:T(1,128)S(1)}, u32[]{:S(2)}, u32[]{:S(2)}) async-start(f32[64,1,136]{2,1,0:T(1,128)} %reshape.412), calls=%async_computation.1 | async-start | bytes 131072 | tf_op jit(solution)/shard_map/all_to_all | solution.py:252
  122.2 2.7 %multiply_subtract_fusion = (f32[32,32,1024]{2,1,0:T(8,128)S(1)}, f32[32,32,1024]{2,1,0:T(8,128)}) fusion(f32[32,1024]{1,0:T(8,128)S(1)} %get-tuple-element.48, f32[32,1024]{1,0:T(8,128)S(1)} %get-tuple-element.45, f32[32,1024]{1,0:T(8,128)S(1)} %get-tuple-element.49, f32[32,1024]{1,0:T(8,128)S(1)} %get-tuple-element.44, f32[1024]{0:T(1024)S(1)} %bitcast.97), kind=kLoop, calls=%fused_computation.17 | loop fusion | flops 4194304 | bytes 8916992 | tf_op jit(solution)/shard_map/sub | solution.py:134
  124.9 2.5 %bitcast_multiply_fusion = f32[1024,1024]{1,0:T(8,128)} fusion(f32[32,32,1024]{2,1,0:T(8,128)S(1)} %get-tuple-element.33, f32[1024]{0:T(1024)S(1)} %bitcast.98), kind=kLoop, calls=%fused_computation.16 | loop fusion | flops 1048576 | bytes 8392704 | tf_op jit(solution)/shard_map/mul | solution.py:138
  127.4 9.0 %all-to-all-done.1 = f32[64,1,136]{2,1,0:T(1,128)S(1)} async-done(((f32[64,1,136]{2,1,0:T(1,128)}), f32[64,1,136]{2,1,0:T(1,128)S(1)}, u32[]{:S(2)}, u32[]{:S(2)}) %all-to-all-start.1) | async-done | bytes 34848 | tf_op jit(solution)/shard_map/all_to_all | solution.py:252
  138.1 4.4 %convolution_divide_fusion = f32[8,1024]{1,0:T(8,128)S(1)} fusion(f32[8,1024]{1,0:T(8,128)S(1)} %reshape.408, f32[1024,1024]{1,0:T(8,128)} %bitcast.84, f32[1024]{0:T(1024)S(1)} %multiply_add_fusion), kind=kOutput, calls=%fused_computation.36 | convolution fusion | flops 100671488 | bytes 4263936 | tf_op jit(solution)/shard_map/dot_general | solution.py:145
  142.5 4.2 %multiply_reduce_fusion = (f32[]{:T(128)}, f32[8,1024]{1,0:T(8,128)S(1)}) fusion(f32[8,1024]{1,0:T(8,128)S(1)} %convolution_divide_fusion, f32[1024,1024]{1,0:T(8,128)S(1)} %copy-done.2), kind=kOutput, calls=%fused_computation.105 | convolution fusion | flops 100679680 | bytes 4259844 | tf_op jit(solution)/shard_map/dot_general | solution.py:149
  148.5 8.6 %all-to-all-start.2 = ((f32[64,1,136]{2,1,0:T(1,128)}), f32[64,1,136]{2,1,0:T(1,128)S(1)}, u32[]{:S(2)}, u32[]{:S(2)}) async-start(f32[64,1,136]{2,1,0:T(1,128)} %reshape.414), calls=%async_computation.2 | async-start | bytes 131072 | tf_op jit(solution)/shard_map/all_to_all | solution.py:262
  157.8 14.6 %all-to-all-done.2 = f32[64,1,136]{2,1,0:T(1,128)S(1)} async-done(((f32[64,1,136]{2,1,0:T(1,128)}), f32[64,1,136]{2,1,0:T(1,128)S(1)}, u32[]{:S(2)}, u32[]{:S(2)}) %all-to-all-start.2) | async-done | bytes 34848 | tf_op jit(solution)/shard_map/all_to_all | solution.py:262
  175.5 33.7 %psum.7 = f32[2]{0:T(128)S(1)} all-reduce(f32[2]{0:T(128)S(1)} %pad_maximum_fusion.1), channel_id=1, replica_groups=mesh['wide'=64,'narrow'=8] {'narrow'}, use_global_device_ids=true, to_apply=%region_8.9 | all-reduce | flops 2 | bytes 16 | tf_op jit(solution)/shard_map/psum | solution.py:265
  (95 shorter events, 34.8 us)
Async XLA Ops:
  0.6 15.2 %copy-start.8 = (s32[1,4096]{1,0:T(1,128)S(1)}, s32[1,4096]{1,0:T(1,128)}, u32[]{:S(2)}) copy-start(s32[1,4096]{1,0:T(1,128)} %param.17) | copy-start | bytes 49156
  0.6 15.2 %copy-start.7 = (f32[2,1,4096]{2,1,0:T(1,128)S(1)}, f32[2,1,4096]{2,1,0:T(1,128)}, u32[]{:S(2)}) copy-start(f32[2,1,4096]{2,1,0:T(1,128)} %param.18) | copy-start | bytes 98308
  0.7 15.2 %copy-start.5 = (s32[1,4096,1]{1,2,0:T(1,128)S(1)}, s32[1,4096,1]{1,2,0:T(1,128)}, u32[]{:S(2)}) copy-start(s32[1,4096,1]{1,2,0:T(1,128)} %param.16) | copy-start | bytes 49156
  0.7 15.3 %copy-start.9 = (f32[1,4096]{1,0:T(1,128)S(1)}, f32[1,4096]{1,0:T(1,128)}, u32[]{:S(2)}) copy-start(f32[1,4096]{1,0:T(1,128)} %param.19) | copy-start | bytes 49156
  2.1 42.8 %collective-permute-start = (f32[2,20,1,512]{3,2,1,0:T(1,128)S(1)}, f32[2,20,1,512]{3,2,1,0:T(1,128)S(1)}, u32[]{:S(2)}, u32[]{:S(2)}) collective-permute-start(f32[2,20,1,512]{3,2,1,0:T(1,128)S(1)} %get-tuple-element.27), channel_id=1, source_target_pairs={{8,0},{16,8},{24,16},{32,24},{40,32},{48,40},{56,48},{64,56},{72,6... | collective-permute-start | bytes 245768 | tf_op jit(solution)/shard_map/ppermute | solution.py:21
  6.8 38.1 %collective-permute-start.1 = (f32[2,20,1,512]{3,2,1,0:T(1,128)S(1)}, f32[2,20,1,512]{3,2,1,0:T(1,128)S(1)}, u32[]{:S(2)}, u32[]{:S(2)}) collective-permute-start(f32[2,20,1,512]{3,2,1,0:T(1,128)S(1)} %get-tuple-element.26), channel_id=1, source_target_pairs={{0,8},{8,16},{16,24},{24,32},{32,40},{40,48},{48,56},{56,64},{64,7... | collective-permute-start | bytes 245768 | tf_op jit(solution)/shard_map/ppermute | solution.py:20
  9.9 35.0 %collective-permute-start.2 = (f32[2,20,16,1]{3,2,1,0:T(8,128)S(1)}, f32[2,20,16,1]{3,2,1,0:T(8,128)S(1)}, u32[]{:S(2)}, u32[]{:S(2)}) collective-permute-start(f32[2,20,16,1]{3,2,1,0:T(8,128)S(1)} %get-tuple-element.23), channel_id=1, source_target_pairs={{1,0},{2,1},{3,2},{4,3},{5,4},{6,5},{7,6},{9,8},{10,9},{11,10},{12... | collective-permute-start | bytes 7688 | tf_op jit(solution)/shard_map/ppermute | solution.py:21
  11.2 33.7 %collective-permute-start.3 = (f32[2,20,16,1]{3,2,1,0:T(8,128)S(1)}, f32[2,20,16,1]{3,2,1,0:T(8,128)S(1)}, u32[]{:S(2)}, u32[]{:S(2)}) collective-permute-start(f32[2,20,16,1]{3,2,1,0:T(8,128)S(1)} %get-tuple-element.22), channel_id=1, source_target_pairs={{0,1},{1,2},{2,3},{3,4},{4,5},{5,6},{6,7},{8,9},{9,10},{10,11},{11... | collective-permute-start | bytes 7688 | tf_op jit(solution)/shard_map/ppermute | solution.py:20
  19.3 23.8 %copy-start.1 = (f32[2,20,16,512]{3,2,1,0:T(8,128)S(1)}, f32[2,20,16,512]{3,2,1,0:T(8,128)}, u32[]{:S(2)}) copy-start(f32[2,20,16,512]{3,2,1,0:T(8,128)} %param.10) | copy-start | bytes 3932164
  22.0 37.2 %all-to-all-start = ((f32[4,64,128]{2,0,1:T(4,128)}), f32[4,64,128]{2,0,1:T(4,128)S(1)}, u32[]{:S(2)}, u32[]{:S(2)}) async-start(f32[4,64,128]{2,0,1:T(4,128)} %copy.18), calls=%async_computation | async-start | bytes 262144 | tf_op jit(solution)/shard_map/all_to_all | solution.py:228
  43.4 0.8 slice-start
  43.4 0.9 copy-start.6
  73.1 2.2 %copy-start = (f32[2,20,16,512]{3,2,1,0:T(8,128)S(1)}, f32[2,20,16,512]{3,2,1,0:T(8,128)}, u32[]{:S(2)}) copy-start(f32[2,20,16,512]{3,2,1,0:T(8,128)} %shard_map.121) | copy-start | bytes 3932164
  76.2 18.2 %collective-permute-start.4 = (f32[2,20,1,512]{3,2,1,0:T(1,128)}, f32[2,20,1,512]{3,2,1,0:T(1,128)S(1)}, u32[]{:S(2)}, u32[]{:S(2)}) collective-permute-start(f32[2,20,1,512]{3,2,1,0:T(1,128)} %get-tuple-element.19), channel_id=1, source_target_pairs={{8,0},{16,8},{24,16},{32,24},{40,32},{48,40},{56,48},{64,56},{72,6... | collective-permute-start | bytes 245768 | tf_op jit(solution)/shard_map/ppermute | solution.py:21
  78.8 15.7 %collective-permute-start.5 = (f32[2,20,1,512]{3,2,1,0:T(1,128)}, f32[2,20,1,512]{3,2,1,0:T(1,128)S(1)}, u32[]{:S(2)}, u32[]{:S(2)}) collective-permute-start(f32[2,20,1,512]{3,2,1,0:T(1,128)} %get-tuple-element.18), channel_id=1, source_target_pairs={{0,8},{8,16},{16,24},{24,32},{32,40},{40,48},{48,56},{56,64},{64,7... | collective-permute-start | bytes 245768 | tf_op jit(solution)/shard_map/ppermute | solution.py:20
  80.7 12.4 %collective-permute-start.6 = (f32[2,20,16,1]{3,2,1,0:T(8,128)}, f32[2,20,16,1]{3,2,1,0:T(8,128)S(1)}, u32[]{:S(2)}, u32[]{:S(2)}) collective-permute-start(f32[2,20,16,1]{3,2,1,0:T(8,128)} %get-tuple-element.15), channel_id=1, source_target_pairs={{1,0},{2,1},{3,2},{4,3},{5,4},{6,5},{7,6},{9,8},{10,9},{11,10},{12... | collective-permute-start | bytes 7688 | tf_op jit(solution)/shard_map/ppermute | solution.py:21
  82.0 12.4 %collective-permute-start.7 = (f32[2,20,16,1]{3,2,1,0:T(8,128)}, f32[2,20,16,1]{3,2,1,0:T(8,128)S(1)}, u32[]{:S(2)}, u32[]{:S(2)}) collective-permute-start(f32[2,20,16,1]{3,2,1,0:T(8,128)} %get-tuple-element.14), channel_id=1, source_target_pairs={{0,1},{1,2},{2,3},{3,4},{4,5},{5,6},{6,7},{8,9},{9,10},{10,11},{11... | collective-permute-start | bytes 7688 | tf_op jit(solution)/shard_map/ppermute | solution.py:20
  97.9 3.2 %copy-start.4 = (f32[2,20,16,512]{3,2,1,0:T(8,128)S(1)}, f32[2,20,16,512]{3,2,1,0:T(8,128)}, u32[]{:S(2)}) copy-start(f32[2,20,16,512]{3,2,1,0:T(8,128)} %param.11) | copy-start | bytes 3932164
  98.0 4.0 %copy-start.3 = (f32[16,512]{1,0:T(8,128)S(1)}, f32[16,512]{1,0:T(8,128)}, u32[]{:S(2)}) copy-start(f32[16,512]{1,0:T(8,128)} %friction_ref.3) | copy-start | bytes 98308
  103.0 33.4 %all-to-all-start.1 = ((f32[64,1,136]{2,1,0:T(1,128)}), f32[64,1,136]{2,1,0:T(1,128)S(1)}, u32[]{:S(2)}, u32[]{:S(2)}) async-start(f32[64,1,136]{2,1,0:T(1,128)} %reshape.412), calls=%async_computation.1 | async-start | bytes 131072 | tf_op jit(solution)/shard_map/all_to_all | solution.py:252
  138.1 4.4 %copy-start.2 = (f32[1024,1024]{1,0:T(8,128)S(1)}, f32[1024,1024]{1,0:T(8,128)}, u32[]{:S(2)}) copy-start(f32[1024,1024]{1,0:T(8,128)} %bitcast_multiply_fusion) | copy-start | bytes 12582916
  148.5 23.9 %all-to-all-start.2 = ((f32[64,1,136]{2,1,0:T(1,128)}), f32[64,1,136]{2,1,0:T(1,128)S(1)}, u32[]{:S(2)}, u32[]{:S(2)}) async-start(f32[64,1,136]{2,1,0:T(1,128)} %reshape.414), calls=%async_computation.2 | async-start | bytes 131072 | tf_op jit(solution)/shard_map/all_to_all | solution.py:262

commit v2 on v1

--- a/solution.py
+++ b/solution.py
@@ -59,8 +59,24 @@
     return ice_float * thomas(coupling, diagonal, right_side)
 
 
-def column_kernel(beside_ref, coupling_ref, friction_ref, horiz_ref, ice_ref, force_ref, out_ref, ratio_ref, partial_ref):
-    comps, layers = beside_ref.shape[0], beside_ref.shape[1]
+def column_kernel(
+    adjoint_ref,
+    x_prev_ref,
+    x_next_ref,
+    y_prev_ref,
+    y_next_ref,
+    coupling_ref,
+    friction_ref,
+    horiz_ref,
+    ice_ref,
+    force_ref,
+    out_ref,
+    ratio_ref,
+    partial_ref,
+):
+    comps, layers, rows_x, rows_y = adjoint_ref.shape
+    rows = lax.broadcasted_iota(jnp.int32, (rows_x, rows_y), 0)
+    cols = lax.broadcasted_iota(jnp.int32, (rows_x, rows_y), 1)
     horiz = horiz_ref[...]
     base = 0.5 + 4.0 * horiz
 
@@ -74,8 +90,16 @@
             value = value + friction_ref[...]
         return value
 
+    def beside(comp, level):
+        center = adjoint_ref[comp, level]
+        x_next = jnp.where(rows == rows_x - 1, x_next_ref[comp, level], pltpu.roll(center, rows_x - 1, 0))
+        x_prev = jnp.where(rows == 0, x_prev_ref[comp, level], pltpu.roll(center, 1, 0))
+        y_next = jnp.where(cols == rows_y - 1, y_next_ref[comp, level], pltpu.roll(center, rows_y - 1, 1))
+        y_prev = jnp.where(cols == 0, y_prev_ref[comp, level], pltpu.roll(center, 1, 1))
+        return x_next + x_prev + y_next + y_prev
+
     def right_side(comp, level):
-        value = horiz * beside_ref[comp, level]
+        value = horiz * beside(comp, level)
         if level == layers - 1:
             value = value + force_ref[comp]
         return value
@@ -102,22 +126,35 @@
             out_ref[comp, level] = ice * result
 
 
-def column_solve(beside, coupling, friction, horiz, ice_float, force):
-    comps, layers, rows_x, rows_y = beside.shape
+def halo_edges(value):
+    edges = []
+    for axis, dim in (("wide", 2), ("narrow", 3)):
+        peers, length = (lax.axis_size(axis), value.shape[dim])
+        up = [(i, i + 1) for i in range(peers - 1)]
+        down = [(j, i) for i, j in up]
+        last = lax.slice_in_dim(value, length - 1, length, axis=dim)
+        first = lax.slice_in_dim(value, 0, 1, axis=dim)
+        edges.append(lax.ppermute(last, axis, up))
+        edges.append(lax.ppermute(first, axis, down))
+    return edges
+
+
+def column_solve(adjoint, edges, coupling, friction, horiz, ice_float, force):
+    comps, layers, rows_x, rows_y = adjoint.shape
     cells = rows_x * rows_y
     return pl.pallas_call(
         column_kernel,
-        out_shape=jax.ShapeDtypeStruct(beside.shape, jnp.float32),
+        out_shape=jax.ShapeDtypeStruct(adjoint.shape, jnp.float32),
         scratch_shapes=[
             pltpu.VMEM((layers - 1, rows_x, rows_y), jnp.float32),
-            pltpu.VMEM(beside.shape, jnp.float32),
+            pltpu.VMEM(adjoint.shape, jnp.float32),
         ],
         cost_estimate=pl.CostEstimate(
-            flops=12 * comps * layers * cells,
+            flops=20 * comps * layers * cells,
             transcendentals=0,
             bytes_accessed=4 * cells * (2 * comps * layers + layers + 4),
         ),
-    )(beside, coupling, friction, horiz, ice_float, force)
+    )(adjoint, *edges, coupling, friction, horiz, ice_float, force)
 
 
 def cosine_table(length, after):
@@ -244,7 +281,7 @@
     ice_float = ice_mask.astype(jnp.float32)
     adjoint = adjoint_start
     for sweep_no in range(ITERS):
-        adjoint = column_solve(neighbour_sum(adjoint), coupling, friction, horiz, ice_float, force)
+        adjoint = column_solve(adjoint, halo_edges(adjoint), coupling, friction, horiz, ice_float, force)
     grad = -friction * ice_float * jnp.sum(adjoint[:, 0] * velocity[:, 0], axis=0)
     misfit_column = jnp.broadcast_to(local_misfit, (rows_y, 1))
     sent = jnp.concatenate([grad.T, misfit_column], axis=1)

time: 213 us -> 208 us (0.977)
  starting transfers between devices: 70.5 us -> 78.4 us
  blocking collectives: 33.7 us -> 25.9 us
  local copies, waits for them, and re-layouts: 17.4 us -> 13.7 us
  other arithmetic: 22.2 us -> 19 us
    psum x1, blocking collectives: 33.7 us -> 25.9 us  [on_device(): totals = lax.psum(jnp.stack([wide_square, wide_misfit]), 'narrow')]
    slice x8 -> x4, local copies, waits for them, and re-layouts: 10.6 us -> 4.26 us  [halo_edges(): first = lax.slice_in_dim(value, 0, 1, axis=dim)]
    all_to_all x1, starting transfers between devices: 21.1 us -> 27 us  [on_device(): lax.all_to_all(packed, 'wide', split_axis=1, concat_axis=1, tiled=True)]
    ppermute x8, starting transfers between devices: 22.7 us -> 28.3 us  [the longest x4 14.3 us: halo_edges(): edges.append(lax.ppermute(first, axis, down))]
    add x2 -> x0, other arithmetic: 5.39 us -> none  [neighbour_sum(): return edges[0] + edges[1] + edges[2] + edges[3]]
    all_to_all x1, starting transfers between devices: 18.1 us -> 14.5 us  [on_device(): lax.all_to_all(sent, 'wide', split_axis=0, concat_axis=1, tiled=True)]
    unnamed x27 -> x35, local copies, waits for them, and re-layouts: 3.54 us -> 5.7 us
  transfers between devices with their start and end apart: 11 -> 11, of which waited for: 5 -> 5; matrix products, arithmetic and copies ran while one was open for 9% -> 12% of each run, Pallas kernels for 0% -> 0%
where the time goes in v2:
time: 208 us; the launch traced here: 207 us
  starting transfers between devices  78.4 us (38%)
  waiting for transfers between devices  41.5 us (20%)
  blocking collectives  25.9 us (12%)
  other arithmetic  19 us (9%)
  matrix products  17.4 us (8%)
  local copies, waits for them, and re-layouts  13.7 us (7%)
  Pallas kernels  8.31 us (4%)
  between operations  2.48 us (1%)
    all_to_all x1, starting transfers between devices, on_device(): lax.all_to_all(packed, 'wide', split_axis=1, concat_axis=1, tiled=True)  27 us
    psum x1, blocking collectives, on_device(): totals = lax.psum(jnp.stack([wide_square, wide_misfit]), 'narrow')  25.9 us
    all_to_all x1, waiting for transfers between devices, on_device(): lax.all_to_all(returned, 'wide', split_axis=1, concat_axis=0, tiled=True)  14.6 us
    all_to_all x1, starting transfers between devices, on_device(): lax.all_to_all(sent, 'wide', split_axis=0, concat_axis=1, tiled=True)  14.5 us
    ppermute x4, starting transfers between devices, halo_edges(): edges.append(lax.ppermute(first, axis, down))  14.3 us
    ppermute x4, starting transfers between devices, halo_edges(): edges.append(lax.ppermute(last, axis, up))  14 us
    all_to_all x1, waiting for transfers between devices, on_device(): lax.all_to_all(packed, 'wide', split_axis=1, concat_axis=1, tiled=True)  10.8 us
    all_to_all x1, waiting for transfers between devices, on_device(): lax.all_to_all(sent, 'wide', split_axis=0, concat_axis=1, tiled=True)  9.04 us
  transfers between devices with their start and end apart: 11, of which 5 were waited for; matrix products, arithmetic and copies ran while one was open for 12% of the time, Pallas kernels for 0%

profile of v2, /device:TPU:6, one launch (start us, length us, event | category | flops | bytes accessed | tf_op | source)
XLA Modules:
  0.0 206.5 jit_solution(7212074082515697300)
XLA Ops:
  2.1 1.9 collective-permute-start
  4.0 5.8 %collective-permute-start.1 = (f32[2,20,1,512]{3,2,1,0:T(1,128)S(1)}, f32[2,20,1,512]{3,2,1,0:T(1,128)S(1)}, u32[]{:S(2)}, u32[]{:S(2)}) collective-permute-start(f32[2,20,1,512]{3,2,1,0:T(1,128)S(1)} %get-tuple-element.20), channel_id=1, source_target_pairs={{8,0},{16,8},{24,16},{32,24},{40,32},{48,40},{56,48},{64,56},{72,6... | collective-permute-start | bytes 245768 | tf_op jit(solution)/shard_map/ppermute | solution.py:138
  16.1 1.9 fusion.4
  18.8 27.0 %all-to-all-start = ((f32[4,64,128]{2,0,1:T(4,128)}), f32[4,64,128]{2,0,1:T(4,128)S(1)}, u32[]{:S(2)}, u32[]{:S(2)}) async-start(f32[4,64,128]{2,0,1:T(4,128)} %copy.18), calls=%async_computation | async-start | bytes 262144 | tf_op jit(solution)/shard_map/all_to_all | solution.py:265
  46.0 2.9 %collective-permute-start.2 = (f32[2,20,16,1]{3,2,1,0:T(8,128)S(1)}, f32[2,20,16,1]{3,2,1,0:T(8,128)S(1)}, u32[]{:S(2)}, u32[]{:S(2)}) collective-permute-start(f32[2,20,16,1]{3,2,1,0:T(8,128)S(1)} %get-tuple-element.19), channel_id=1, source_target_pairs={{0,1},{1,2},{2,3},{3,4},{4,5},{5,6},{6,7},{8,9},{9,10},{10,11},{11... | collective-permute-start | bytes 7688 | tf_op jit(solution)/shard_map/ppermute | solution.py:137
  51.1 10.8 %all-to-all-done = f32[4,64,128]{2,0,1:T(4,128)S(1)} async-done(((f32[4,64,128]{2,0,1:T(4,128)}), f32[4,64,128]{2,0,1:T(4,128)S(1)}, u32[]{:S(2)}, u32[]{:S(2)}) %all-to-all-start) | async-done | bytes 131104 | tf_op jit(solution)/shard_map/all_to_all | solution.py:265
  62.1 3.2 %fusion.1 = f32[96,8192]{1,0:T(8,128)S(1)} fusion(s32[8192]{0:T(1024)S(1)} %get-tuple-element.33, bf16[32,512]{1,0:T(8,128)(2,1)S(1)} %get-tuple-element.30, bf16[32,512]{1,0:T(8,128)(2,1)S(1)} %get-tuple-element.31, bf16[32,512]{1,0:T(8,128)(2,1)S(1)} %get-tuple-element.29), kind=kOutput, calls=%fused_computation.2 | convolution fusion | flops 809795584 | bytes 3276800 | tf_op jit(solution)/shard_map/dot_general | solution.py:205
  66.8 3.2 %fusion = f32[96,512]{1,0:T(8,128)S(1)} fusion(s32[8192]{0:T(1024)S(1)} %get-tuple-element.33, bf16[32,8192]{1,0:T(8,128)(2,1)S(1)} %get-tuple-element.23, bf16[32,8192]{1,0:T(8,128)(2,1)S(1)} %get-tuple-element.24, bf16[32,8192]{1,0:T(8,128)(2,1)S(1)} %get-tuple-element.22), kind=kOutput, calls=%fused_computation.1 | convolution fusion | flops 814219264 | bytes 1802240 | tf_op jit(solution)/shard_map/dot_general | solution.py:205
  71.5 4.2 %shard_map.121.adjoint_ref = f32[2,20,16,512]{3,2,1,0:T(8,128)} custom-call(f32[2,20,16,512]{3,2,1,0:T(8,128)} %adjoint_ref.1, f32[2,20,1,512]{3,2,1,0:T(1,128)} %copy-done.10, f32[2,20,1,512]{3,2,1,0:T(1,128)} %copy-done.11, f32[2,20,16,1]{3,2,1,0:T(8,128)} %copy-done.2, f32[2,20,16,1]{3,2,1,0:T(8,128)} %copy-done.3, f32[19,16,512]{2,1,0:T(8,128)} %coupling_ref.3, ...), custom_call_target="tpu_custom_call" | custom-call | flops 6553600 | bytes 3407872 | tf_op jit(solution)/shard_map/pallas_call | solution.py:145
  78.4 1.9 collective-permute-start.4
  80.4 5.8 %collective-permute-start.5 = (f32[2,20,1,512]{3,2,1,0:T(1,128)S(1)}, f32[2,20,1,512]{3,2,1,0:T(1,128)S(1)}, u32[]{:S(2)}, u32[]{:S(2)}) collective-permute-start(f32[2,20,1,512]{3,2,1,0:T(1,128)S(1)} %get-tuple-element.16), channel_id=1, source_target_pairs={{8,0},{16,8},{24,16},{32,24},{40,32},{48,40},{56,48},{64,56},{72,6... | collective-permute-start | bytes 245768 | tf_op jit(solution)/shard_map/ppermute | solution.py:138
  86.1 7.2 %collective-permute-start.6 = (f32[2,20,16,1]{3,2,1,0:T(8,128)S(1)}, f32[2,20,16,1]{3,2,1,0:T(8,128)S(1)}, u32[]{:S(2)}, u32[]{:S(2)}) collective-permute-start(f32[2,20,16,1]{3,2,1,0:T(8,128)S(1)} %get-tuple-element.15), channel_id=1, source_target_pairs={{0,1},{1,2},{2,3},{3,4},{4,5},{5,6},{6,7},{8,9},{9,10},{10,11},{11... | collective-permute-start | bytes 7688 | tf_op jit(solution)/shard_map/ppermute | solution.py:137
  95.3 2.6 %collective-permute-done.6.y_prev_ref = f32[2,20,16,1]{3,2,1,0:T(8,128)S(1)} collective-permute-done((f32[2,20,16,1]{3,2,1,0:T(8,128)S(1)}, f32[2,20,16,1]{3,2,1,0:T(8,128)S(1)}, u32[]{:S(2)}, u32[]{:S(2)}) %collective-permute-start.6) | collective-permute-done | bytes 2592 | tf_op jit(solution)/shard_map/ppermute | solution.py:137
  97.9 4.4 %collective-permute-done.7.y_next_ref = f32[2,20,16,1]{3,2,1,0:T(8,128)S(1)} collective-permute-done((f32[2,20,16,1]{3,2,1,0:T(8,128)S(1)}, f32[2,20,16,1]{3,2,1,0:T(8,128)S(1)}, u32[]{:S(2)}, u32[]{:S(2)}) %collective-permute-start.7) | collective-permute-done | bytes 2592 | tf_op jit(solution)/shard_map/ppermute | solution.py:138
  103.7 4.1 %shard_map.122 = f32[2,20,16,512]{3,2,1,0:T(8,128)} custom-call(f32[2,20,16,512]{3,2,1,0:T(8,128)} %shard_map.121.adjoint_ref, f32[2,20,1,512]{3,2,1,0:T(1,128)} %copy-done.12, f32[2,20,1,512]{3,2,1,0:T(1,128)} %copy-done.13, f32[2,20,16,1]{3,2,1,0:T(8,128)} %copy-done.4, f32[2,20,16,1]{3,2,1,0:T(8,128)} %copy-done.5, f32[19,16,512]{2,1,0:T(8,128)} %coupling_ref.3, ...), custom_call_target="tpu_custom_call" | custom-call | flops 6553600 | bytes 3407872 | tf_op jit(solution)/shard_map/pallas_call | solution.py:145
  109.7 14.5 %all-to-all-start.1 = ((f32[64,1,136]{2,1,0:T(1,128)}), f32[64,1,136]{2,1,0:T(1,128)S(1)}, u32[]{:S(2)}, u32[]{:S(2)}) async-start(f32[64,1,136]{2,1,0:T(1,128)} %reshape.412), calls=%async_computation.1 | async-start | bytes 131072 | tf_op jit(solution)/shard_map/all_to_all | solution.py:289
  125.4 2.7 %multiply_subtract_fusion = (f32[32,32,1024]{2,1,0:T(8,128)S(1)}, f32[32,32,1024]{2,1,0:T(8,128)}) fusion(f32[32,1024]{1,0:T(8,128)S(1)} %get-tuple-element.40, f32[32,1024]{1,0:T(8,128)S(1)} %get-tuple-element.37, f32[32,1024]{1,0:T(8,128)S(1)} %get-tuple-element.41, f32[32,1024]{1,0:T(8,128)S(1)} %get-tuple-element.36, f32[1024]{0:T(1024)S(1)} %bitcast.97), kind=kLoop, calls=%fused_computation.17 | loop fusion | flops 4194304 | bytes 8916992 | tf_op jit(solution)/shard_map/sub | solution.py:171
  128.0 2.5 %bitcast_multiply_fusion = f32[1024,1024]{1,0:T(8,128)} fusion(f32[32,32,1024]{2,1,0:T(8,128)S(1)} %get-tuple-element.25, f32[1024]{0:T(1024)S(1)} %bitcast.98), kind=kLoop, calls=%fused_computation.16 | loop fusion | flops 1048576 | bytes 8392704 | tf_op jit(solution)/shard_map/mul | solution.py:175
  130.5 9.0 %all-to-all-done.1 = f32[64,1,136]{2,1,0:T(1,128)S(1)} async-done(((f32[64,1,136]{2,1,0:T(1,128)}), f32[64,1,136]{2,1,0:T(1,128)S(1)}, u32[]{:S(2)}, u32[]{:S(2)}) %all-to-all-start.1) | async-done | bytes 34848 | tf_op jit(solution)/shard_map/all_to_all | solution.py:289
  141.2 4.4 %convolution_divide_fusion = f32[8,1024]{1,0:T(8,128)S(1)} fusion(f32[8,1024]{1,0:T(8,128)S(1)} %reshape.408, f32[1024,1024]{1,0:T(8,128)} %bitcast.84, f32[1024]{0:T(1024)S(1)} %multiply_add_fusion), kind=kOutput, calls=%fused_computation.30 | convolution fusion | flops 100671488 | bytes 4263936 | tf_op jit(solution)/shard_map/dot_general | solution.py:182
  145.7 4.2 %multiply_reduce_fusion = (f32[]{:T(128)}, f32[8,1024]{1,0:T(8,128)S(1)}) fusion(f32[8,1024]{1,0:T(8,128)S(1)} %convolution_divide_fusion, f32[1024,1024]{1,0:T(8,128)S(1)} %copy-done), kind=kOutput, calls=%fused_computation.99 | convolution fusion | flops 100679680 | bytes 4259844 | tf_op jit(solution)/shard_map/dot_general | solution.py:186
  151.6 8.6 %all-to-all-start.2 = ((f32[64,1,136]{2,1,0:T(1,128)}), f32[64,1,136]{2,1,0:T(1,128)S(1)}, u32[]{:S(2)}, u32[]{:S(2)}) async-start(f32[64,1,136]{2,1,0:T(1,128)} %reshape.414), calls=%async_computation.2 | async-start | bytes 131072 | tf_op jit(solution)/shard_map/all_to_all | solution.py:299
  161.0 14.6 %all-to-all-done.2 = f32[64,1,136]{2,1,0:T(1,128)S(1)} async-done(((f32[64,1,136]{2,1,0:T(1,128)}), f32[64,1,136]{2,1,0:T(1,128)S(1)}, u32[]{:S(2)}, u32[]{:S(2)}) %all-to-all-start.2) | async-done | bytes 34848 | tf_op jit(solution)/shard_map/all_to_all | solution.py:299
  178.6 25.9 %psum.7 = f32[2]{0:T(128)S(1)} all-reduce(f32[2]{0:T(128)S(1)} %pad_maximum_fusion.1), channel_id=1, replica_groups=mesh['wide'=64,'narrow'=8] {'narrow'}, use_global_device_ids=true, to_apply=%region_8.9 | all-reduce | flops 2 | bytes 16 | tf_op jit(solution)/shard_map/psum | solution.py:302
  (97 shorter events, 30.7 us)
Async XLA Ops:
  2.1 68.6 %collective-permute-start = (f32[2,20,1,512]{3,2,1,0:T(1,128)S(1)}, f32[2,20,1,512]{3,2,1,0:T(1,128)S(1)}, u32[]{:S(2)}, u32[]{:S(2)}) collective-permute-start(f32[2,20,1,512]{3,2,1,0:T(1,128)S(1)} %get-tuple-element.21), channel_id=1, source_target_pairs={{0,8},{8,16},{16,24},{24,32},{32,40},{40,48},{48,56},{56,64},{64,7... | collective-permute-start | bytes 245768 | tf_op jit(solution)/shard_map/ppermute | solution.py:137
  4.0 66.7 %collective-permute-start.1 = (f32[2,20,1,512]{3,2,1,0:T(1,128)S(1)}, f32[2,20,1,512]{3,2,1,0:T(1,128)S(1)}, u32[]{:S(2)}, u32[]{:S(2)}) collective-permute-start(f32[2,20,1,512]{3,2,1,0:T(1,128)S(1)} %get-tuple-element.20), channel_id=1, source_target_pairs={{8,0},{16,8},{24,16},{32,24},{40,32},{48,40},{56,48},{64,56},{72,6... | collective-permute-start | bytes 245768 | tf_op jit(solution)/shard_map/ppermute | solution.py:138
  13.4 1.2 copy-start.8
  16.1 29.7 %copy-start.1 = (f32[2,20,16,512]{3,2,1,0:T(8,128)S(1)}, f32[2,20,16,512]{3,2,1,0:T(8,128)}, u32[]{:S(2)}) copy-start(f32[2,20,16,512]{3,2,1,0:T(8,128)} %adjoint_ref.1) | copy-start | bytes 3932164
  16.1 34.3 %copy-start.9 = (s32[16,512]{1,0:T(8,128)S(1)}, s32[16,512]{1,0:T(8,128)}, u32[]{:S(2)}) copy-start(s32[16,512]{1,0:T(8,128)} %param.15) | copy-start | bytes 98308
  16.1 35.0 %slice-start = ((f32[2,20,16,512]{3,2,1,0:T(8,128)}), f32[2,1,16,512]{3,2,1,0:T(8,128)S(1)}, s32[]{:S(2)}) async-start(f32[2,20,16,512]{3,2,1,0:T(8,128)} %param.11), calls=%async_computation.3 | async-start | bytes 131072 | tf_op jit(solution)/shard_map/slice | solution.py:272
  18.8 43.1 %all-to-all-start = ((f32[4,64,128]{2,0,1:T(4,128)}), f32[4,64,128]{2,0,1:T(4,128)S(1)}, u32[]{:S(2)}, u32[]{:S(2)}) async-start(f32[4,64,128]{2,0,1:T(4,128)} %copy.18), calls=%async_computation | async-start | bytes 262144 | tf_op jit(solution)/shard_map/all_to_all | solution.py:265
  46.0 24.7 %collective-permute-start.2 = (f32[2,20,16,1]{3,2,1,0:T(8,128)S(1)}, f32[2,20,16,1]{3,2,1,0:T(8,128)S(1)}, u32[]{:S(2)}, u32[]{:S(2)}) collective-permute-start(f32[2,20,16,1]{3,2,1,0:T(8,128)S(1)} %get-tuple-element.19), channel_id=1, source_target_pairs={{0,1},{1,2},{2,3},{3,4},{4,5},{5,6},{6,7},{8,9},{9,10},{10,11},{11... | collective-permute-start | bytes 7688 | tf_op jit(solution)/shard_map/ppermute | solution.py:137
  48.9 21.7 %collective-permute-start.3 = (f32[2,20,16,1]{3,2,1,0:T(8,128)S(1)}, f32[2,20,16,1]{3,2,1,0:T(8,128)S(1)}, u32[]{:S(2)}, u32[]{:S(2)}) collective-permute-start(f32[2,20,16,1]{3,2,1,0:T(8,128)S(1)} %get-tuple-element.18), channel_id=1, source_target_pairs={{1,0},{2,1},{3,2},{4,3},{5,4},{6,5},{7,6},{9,8},{10,9},{11,10},{12... | collective-permute-start | bytes 7688 | tf_op jit(solution)/shard_map/ppermute | solution.py:138
  70.7 0.7 copy-start.2
  70.7 0.8 copy-start.3
  70.7 0.8 copy-start.10
  70.7 0.8 copy-start.11
  71.5 36.2 %copy-start.7 = (f32[2,20,16,512]{3,2,1,0:T(8,128)S(1)}, f32[2,20,16,512]{3,2,1,0:T(8,128)}, u32[]{:S(2)}) copy-start(f32[2,20,16,512]{3,2,1,0:T(8,128)} %param.11) | copy-start | bytes 3932164
  71.5 37.1 %copy-start.6 = (f32[16,512]{1,0:T(8,128)S(1)}, f32[16,512]{1,0:T(8,128)}, u32[]{:S(2)}) copy-start(f32[16,512]{1,0:T(8,128)} %friction_ref.3) | copy-start | bytes 98308
  78.4 23.9 %collective-permute-start.4 = (f32[2,20,1,512]{3,2,1,0:T(1,128)S(1)}, f32[2,20,1,512]{3,2,1,0:T(1,128)S(1)}, u32[]{:S(2)}, u32[]{:S(2)}) collective-permute-start(f32[2,20,1,512]{3,2,1,0:T(1,128)S(1)} %get-tuple-element.17), channel_id=1, source_target_pairs={{0,8},{8,16},{16,24},{24,32},{32,40},{40,48},{48,56},{56,64},{64,7... | collective-permute-start | bytes 245768 | tf_op jit(solution)/shard_map/ppermute | solution.py:137
  80.4 22.0 %collective-permute-start.5 = (f32[2,20,1,512]{3,2,1,0:T(1,128)S(1)}, f32[2,20,1,512]{3,2,1,0:T(1,128)S(1)}, u32[]{:S(2)}, u32[]{:S(2)}) collective-permute-start(f32[2,20,1,512]{3,2,1,0:T(1,128)S(1)} %get-tuple-element.16), channel_id=1, source_target_pairs={{8,0},{16,8},{24,16},{32,24},{40,32},{48,40},{56,48},{64,56},{72,6... | collective-permute-start | bytes 245768 | tf_op jit(solution)/shard_map/ppermute | solution.py:138
  86.1 11.8 %collective-permute-start.6 = (f32[2,20,16,1]{3,2,1,0:T(8,128)S(1)}, f32[2,20,16,1]{3,2,1,0:T(8,128)S(1)}, u32[]{:S(2)}, u32[]{:S(2)}) collective-permute-start(f32[2,20,16,1]{3,2,1,0:T(8,128)S(1)} %get-tuple-element.15), channel_id=1, source_target_pairs={{0,1},{1,2},{2,3},{3,4},{4,5},{5,6},{6,7},{8,9},{9,10},{10,11},{11... | collective-permute-start | bytes 7688 | tf_op jit(solution)/shard_map/ppermute | solution.py:137
  93.3 9.0 %collective-permute-start.7 = (f32[2,20,16,1]{3,2,1,0:T(8,128)S(1)}, f32[2,20,16,1]{3,2,1,0:T(8,128)S(1)}, u32[]{:S(2)}, u32[]{:S(2)}) collective-permute-start(f32[2,20,16,1]{3,2,1,0:T(8,128)S(1)} %get-tuple-element.14), channel_id=1, source_target_pairs={{1,0},{2,1},{3,2},{4,3},{5,4},{6,5},{7,6},{9,8},{10,9},{11,10},{12... | collective-permute-start | bytes 7688 | tf_op jit(solution)/shard_map/ppermute | solution.py:138
  97.9 4.4 %copy-start.4 = (f32[2,20,16,1]{3,2,1,0:T(8,128)}, f32[2,20,16,1]{3,2,1,0:T(8,128)S(1)}, u32[]{:S(2)}) copy-start(f32[2,20,16,1]{3,2,1,0:T(8,128)S(1)} %collective-permute-done.6.y_prev_ref) | copy-start | bytes 7684
  102.3 0.7 copy-start.12
  109.7 29.9 %all-to-all-start.1 = ((f32[64,1,136]{2,1,0:T(1,128)}), f32[64,1,136]{2,1,0:T(1,128)S(1)}, u32[]{:S(2)}, u32[]{:S(2)}) async-start(f32[64,1,136]{2,1,0:T(1,128)} %reshape.412), calls=%async_computation.1 | async-start | bytes 131072 | tf_op jit(solution)/shard_map/all_to_all | solution.py:289
  141.2 4.4 %copy-start = (f32[1024,1024]{1,0:T(8,128)S(1)}, f32[1024,1024]{1,0:T(8,128)}, u32[]{:S(2)}) copy-start(f32[1024,1024]{1,0:T(8,128)} %bitcast_multiply_fusion) | copy-start | bytes 12582916
  151.6 23.9 %all-to-all-start.2 = ((f32[64,1,136]{2,1,0:T(1,128)}), f32[64,1,136]{2,1,0:T(1,128)S(1)}, u32[]{:S(2)}, u32[]{:S(2)}) async-start(f32[64,1,136]{2,1,0:T(1,128)} %reshape.414), calls=%async_computation.2 | async-start | bytes 131072 | tf_op jit(solution)/shard_map/all_to_all | solution.py:299
  (2 other events, 1.3 us)

commit v3 on v2

--- a/solution.py
+++ b/solution.py
@@ -263,6 +263,7 @@
     packed = exact_dot(spread.reshape(4 * wide_count, how_many), rank_hot, 0)
     packed = packed.reshape(4, wide_count, capacity)
     arrived = lax.all_to_all(packed, "wide", split_axis=1, concat_axis=1, tiled=True).reshape(4, -1)
+    adjoint, arrived = lax.optimization_barrier((adjoint_start, arrived))
     target = arrived[3].astype(jnp.int32)
     slots = target.shape[0]
     column_hot = (
@@ -279,7 +280,6 @@
     force = exact_dot(placed, column_hot, 1).reshape(2, rows_x, rows_y)
     local_misfit = 0.5 * jnp.sum(weights * jnp.sum(residual * residual, axis=0))
     ice_float = ice_mask.astype(jnp.float32)
-    adjoint = adjoint_start
     for sweep_no in range(ITERS):
         adjoint = column_solve(adjoint, halo_edges(adjoint), coupling, friction, horiz, ice_float, force)
     grad = -friction * ice_float * jnp.sum(adjoint[:, 0] * velocity[:, 0], axis=0)

time: 208 us -> 218 us (1.048)
  starting transfers between devices: 78.4 us -> 85.3 us
  waiting for transfers between devices: 41.5 us -> 45.3 us
    all_to_all x1, starting transfers between devices: 14.5 us -> 25.7 us  [on_device(): lax.all_to_all(sent, 'wide', split_axis=0, concat_axis=1, tiled=True)]
    all_to_all x1, starting transfers between devices: 27 us -> 21.3 us  [on_device(): lax.all_to_all(packed, 'wide', split_axis=1, concat_axis=1, tiled=True)]
    all_to_all x1, waiting for transfers between devices: 10.8 us -> 15.2 us  [on_device(): lax.all_to_all(packed, 'wide', split_axis=1, concat_axis=1, tiled=True)]
  transfers between devices with their start and end apart: 11 -> 11, of which waited for: 5 -> 5; matrix products, arithmetic and copies ran while one was open for 12% -> 8% of each run, Pallas kernels for 0% -> 0%
where the time goes in v3:
time: 218 us; the launch traced here: 217 us
  starting transfers between devices  85.3 us (39%)
  waiting for transfers between devices  45.3 us (21%)
  blocking collectives  26.5 us (12%)
  other arithmetic  19 us (9%)
  matrix products  17.4 us (8%)
  local copies, waits for them, and re-layouts  12.4 us (6%)
  Pallas kernels  8.31 us (4%)
  between operations  2.48 us (1%)
    psum x1, blocking collectives, on_device(): totals = lax.psum(jnp.stack([wide_square, wide_misfit]), 'narrow')  26.5 us
    all_to_all x1, starting transfers between devices, on_device(): lax.all_to_all(sent, 'wide', split_axis=0, concat_axis=1, tiled=True)  25.7 us
    all_to_all x1, starting transfers between devices, on_device(): lax.all_to_all(packed, 'wide', split_axis=1, concat_axis=1, tiled=True)  21.3 us
    ppermute x4, starting transfers between devices, halo_edges(): edges.append(lax.ppermute(last, axis, up))  15.5 us
    all_to_all x1, waiting for transfers between devices, on_device(): lax.all_to_all(packed, 'wide', split_axis=1, concat_axis=1, tiled=True)  15.2 us
    all_to_all x1, waiting for transfers between devices, on_device(): lax.all_to_all(returned, 'wide', split_axis=1, concat_axis=0, tiled=True)  14.6 us
    ppermute x4, starting transfers between devices, halo_edges(): edges.append(lax.ppermute(first, axis, down))  14.3 us
    all_to_all x1, waiting for transfers between devices, on_device(): lax.all_to_all(sent, 'wide', split_axis=0, concat_axis=1, tiled=True)  9.04 us
  transfers between devices with their start and end apart: 11, of which 5 were waited for; matrix products, arithmetic and copies ran while one was open for 8% of the time, Pallas kernels for 0%

profile of v3, /device:TPU:6, one launch (start us, length us, event | category | flops | bytes accessed | tf_op | source)
XLA Modules:
  0.0 216.7 jit_solution(11700945977463426309)
XLA Ops:
  7.0 1.9 fusion.4
  9.7 21.3 %all-to-all-start = ((f32[4,64,128]{2,0,1:T(4,128)}), f32[4,64,128]{2,0,1:T(4,128)S(1)}, u32[]{:S(2)}, u32[]{:S(2)}) async-start(f32[4,64,128]{2,0,1:T(4,128)} %copy.18), calls=%async_computation | async-start | bytes 262144 | tf_op jit(solution)/shard_map/all_to_all | solution.py:265
  31.7 15.2 %all-to-all-done = f32[4,64,128]{2,0,1:T(4,128)S(1)} async-done(((f32[4,64,128]{2,0,1:T(4,128)}), f32[4,64,128]{2,0,1:T(4,128)S(1)}, u32[]{:S(2)}, u32[]{:S(2)}) %all-to-all-start) | async-done | bytes 131104 | tf_op jit(solution)/shard_map/all_to_all | solution.py:265
  47.5 1.9 collective-permute-start
  49.4 5.8 %collective-permute-start.1 = (f32[2,20,1,512]{3,2,1,0:T(1,128)S(1)}, f32[2,20,1,512]{3,2,1,0:T(1,128)S(1)}, u32[]{:S(2)}, u32[]{:S(2)}) collective-permute-start(f32[2,20,1,512]{3,2,1,0:T(1,128)S(1)} %get-tuple-element.26), channel_id=1, source_target_pairs={{8,0},{16,8},{24,16},{32,24},{40,32},{48,40},{56,48},{64,56},{72,6... | collective-permute-start | bytes 245768 | tf_op jit(solution)/shard_map/ppermute | solution.py:138
  55.1 7.1 %collective-permute-start.2 = (f32[2,20,16,1]{3,2,1,0:T(8,128)S(1)}, f32[2,20,16,1]{3,2,1,0:T(8,128)S(1)}, u32[]{:S(2)}, u32[]{:S(2)}) collective-permute-start(f32[2,20,16,1]{3,2,1,0:T(8,128)S(1)} %get-tuple-element.25), channel_id=1, source_target_pairs={{0,1},{1,2},{2,3},{3,4},{4,5},{5,6},{6,7},{8,9},{9,10},{10,11},{11... | collective-permute-start | bytes 7688 | tf_op jit(solution)/shard_map/ppermute | solution.py:137
  63.8 3.2 %fusion.1 = f32[96,8192]{1,0:T(8,128)S(1)} fusion(s32[8192]{0:T(1024)S(1)} %bitcast.94, bf16[32,512]{1,0:T(8,128)(2,1)S(1)} %get-tuple-element.36, bf16[32,512]{1,0:T(8,128)(2,1)S(1)} %get-tuple-element.37, bf16[32,512]{1,0:T(8,128)(2,1)S(1)} %get-tuple-element.35), kind=kOutput, calls=%fused_computation.2 | convolution fusion | flops 809795584 | bytes 3276800 | tf_op jit(solution)/shard_map/dot_general | solution.py:205
  67.8 3.2 %fusion = f32[96,512]{1,0:T(8,128)S(1)} fusion(s32[8192]{0:T(1024)S(1)} %bitcast.95, bf16[32,8192]{1,0:T(8,128)(2,1)S(1)} %get-tuple-element.29, bf16[32,8192]{1,0:T(8,128)(2,1)S(1)} %get-tuple-element.30, bf16[32,8192]{1,0:T(8,128)(2,1)S(1)} %get-tuple-element.28), kind=kOutput, calls=%fused_computation.1 | convolution fusion | flops 814219264 | bytes 1802240 | tf_op jit(solution)/shard_map/dot_general | solution.py:205
  72.6 4.2 %shard_map.121.adjoint_ref = f32[2,20,16,512]{3,2,1,0:T(8,128)} custom-call(f32[2,20,16,512]{3,2,1,0:T(8,128)} %adjoint_ref, f32[2,20,1,512]{3,2,1,0:T(1,128)} %copy-done.10, f32[2,20,1,512]{3,2,1,0:T(1,128)} %copy-done.11, f32[2,20,16,1]{3,2,1,0:T(8,128)} %copy-done.2, f32[2,20,16,1]{3,2,1,0:T(8,128)} %copy-done.3, f32[19,16,512]{2,1,0:T(8,128)} %coupling_ref.3, ...), custom_call_target="tpu_custom_call" | custom-call | flops 6553600 | bytes 3407872 | tf_op jit(solution)/shard_map/pallas_call | solution.py:145
  79.5 1.9 collective-permute-start.4
  81.4 5.8 %collective-permute-start.5 = (f32[2,20,1,512]{3,2,1,0:T(1,128)S(1)}, f32[2,20,1,512]{3,2,1,0:T(1,128)S(1)}, u32[]{:S(2)}, u32[]{:S(2)}) collective-permute-start(f32[2,20,1,512]{3,2,1,0:T(1,128)S(1)} %get-tuple-element.22), channel_id=1, source_target_pairs={{8,0},{16,8},{24,16},{32,24},{40,32},{48,40},{56,48},{64,56},{72,6... | collective-permute-start | bytes 245768 | tf_op jit(solution)/shard_map/ppermute | solution.py:138
  87.1 4.6 %collective-permute-start.6 = (f32[2,20,16,1]{3,2,1,0:T(8,128)S(1)}, f32[2,20,16,1]{3,2,1,0:T(8,128)S(1)}, u32[]{:S(2)}, u32[]{:S(2)}) collective-permute-start(f32[2,20,16,1]{3,2,1,0:T(8,128)S(1)} %get-tuple-element.21), channel_id=1, source_target_pairs={{0,1},{1,2},{2,3},{3,4},{4,5},{5,6},{6,7},{8,9},{9,10},{10,11},{11... | collective-permute-start | bytes 7688 | tf_op jit(solution)/shard_map/ppermute | solution.py:137
  94.3 2.0 collective-permute-done.6.y_prev_ref
  96.3 4.4 %collective-permute-done.7.y_next_ref = f32[2,20,16,1]{3,2,1,0:T(8,128)S(1)} collective-permute-done((f32[2,20,16,1]{3,2,1,0:T(8,128)S(1)}, f32[2,20,16,1]{3,2,1,0:T(8,128)S(1)}, u32[]{:S(2)}, u32[]{:S(2)}) %collective-permute-start.7) | collective-permute-done | bytes 2592 | tf_op jit(solution)/shard_map/ppermute | solution.py:138
  102.1 4.1 %shard_map.122 = f32[2,20,16,512]{3,2,1,0:T(8,128)} custom-call(f32[2,20,16,512]{3,2,1,0:T(8,128)} %shard_map.121.adjoint_ref, f32[2,20,1,512]{3,2,1,0:T(1,128)} %copy-done.12, f32[2,20,1,512]{3,2,1,0:T(1,128)} %copy-done.13, f32[2,20,16,1]{3,2,1,0:T(8,128)} %copy-done.4, f32[2,20,16,1]{3,2,1,0:T(8,128)} %copy-done.5, f32[19,16,512]{2,1,0:T(8,128)} %coupling_ref.3, ...), custom_call_target="tpu_custom_call" | custom-call | flops 6553600 | bytes 3407872 | tf_op jit(solution)/shard_map/pallas_call | solution.py:145
  108.1 25.7 %all-to-all-start.1 = ((f32[64,1,136]{2,1,0:T(1,128)}), f32[64,1,136]{2,1,0:T(1,128)S(1)}, u32[]{:S(2)}, u32[]{:S(2)}) async-start(f32[64,1,136]{2,1,0:T(1,128)} %reshape.353), calls=%async_computation.1 | async-start | bytes 131072 | tf_op jit(solution)/shard_map/all_to_all | solution.py:289
  134.9 2.7 %multiply_subtract_fusion = (f32[32,32,1024]{2,1,0:T(8,128)S(1)}, f32[32,32,1024]{2,1,0:T(8,128)}) fusion(f32[32,1024]{1,0:T(8,128)S(1)} %get-tuple-element.44, f32[32,1024]{1,0:T(8,128)S(1)} %get-tuple-element.41, f32[32,1024]{1,0:T(8,128)S(1)} %get-tuple-element.45, f32[32,1024]{1,0:T(8,128)S(1)} %get-tuple-element.40, f32[1024]{0:T(1024)S(1)} %bitcast.91), kind=kLoop, calls=%fused_computation.17 | loop fusion | flops 4194304 | bytes 8916992 | tf_op jit(solution)/shard_map/sub | solution.py:171
  137.6 2.5 %bitcast_multiply_fusion = f32[1024,1024]{1,0:T(8,128)} fusion(f32[32,32,1024]{2,1,0:T(8,128)S(1)} %get-tuple-element.31, f32[1024]{0:T(1024)S(1)} %bitcast.92), kind=kLoop, calls=%fused_computation.16 | loop fusion | flops 1048576 | bytes 8392704 | tf_op jit(solution)/shard_map/mul | solution.py:175
  140.1 9.0 %all-to-all-done.1 = f32[64,1,136]{2,1,0:T(1,128)S(1)} async-done(((f32[64,1,136]{2,1,0:T(1,128)}), f32[64,1,136]{2,1,0:T(1,128)S(1)}, u32[]{:S(2)}, u32[]{:S(2)}) %all-to-all-start.1) | async-done | bytes 34848 | tf_op jit(solution)/shard_map/all_to_all | solution.py:289
  150.8 4.4 %convolution_divide_fusion = f32[8,1024]{1,0:T(8,128)S(1)} fusion(f32[8,1024]{1,0:T(8,128)S(1)} %reshape.349, f32[1024,1024]{1,0:T(8,128)} %bitcast.75, f32[1024]{0:T(1024)S(1)} %multiply_add_fusion), kind=kOutput, calls=%fused_computation.30 | convolution fusion | flops 100671488 | bytes 4263936 | tf_op jit(solution)/shard_map/dot_general | solution.py:182
  155.2 4.2 %multiply_reduce_fusion.1 = (f32[]{:T(128)}, f32[8,1024]{1,0:T(8,128)S(1)}) fusion(f32[8,1024]{1,0:T(8,128)S(1)} %convolution_divide_fusion, f32[1024,1024]{1,0:T(8,128)S(1)} %copy-done), kind=kOutput, calls=%fused_computation.95 | convolution fusion | flops 100679680 | bytes 4259844 | tf_op jit(solution)/shard_map/dot_general | solution.py:186
  161.2 8.6 %all-to-all-start.2 = ((f32[64,1,136]{2,1,0:T(1,128)}), f32[64,1,136]{2,1,0:T(1,128)S(1)}, u32[]{:S(2)}, u32[]{:S(2)}) async-start(f32[64,1,136]{2,1,0:T(1,128)} %reshape.355), calls=%async_computation.2 | async-start | bytes 131072 | tf_op jit(solution)/shard_map/all_to_all | solution.py:299
  170.5 14.6 %all-to-all-done.2 = f32[64,1,136]{2,1,0:T(1,128)S(1)} async-done(((f32[64,1,136]{2,1,0:T(1,128)}), f32[64,1,136]{2,1,0:T(1,128)S(1)}, u32[]{:S(2)}, u32[]{:S(2)}) %all-to-all-start.2) | async-done | bytes 34848 | tf_op jit(solution)/shard_map/all_to_all | solution.py:299
  188.2 26.5 %psum.7 = f32[2]{0:T(128)S(1)} all-reduce(f32[2]{0:T(128)S(1)} %pad_maximum_fusion.1), channel_id=1, replica_groups=mesh['wide'=64,'narrow'=8] {'narrow'}, use_global_device_ids=true, to_apply=%region_8.9 | all-reduce | flops 2 | bytes 16 | tf_op jit(solution)/shard_map/psum | solution.py:302
  (97 shorter events, 29.5 us)
Async XLA Ops:
  4.2 1.2 copy-start.8
  7.0 24.0 %copy-start.9 = (s32[16,512]{1,0:T(8,128)S(1)}, s32[16,512]{1,0:T(8,128)}, u32[]{:S(2)}) copy-start(s32[16,512]{1,0:T(8,128)} %param.15) | copy-start | bytes 98308
  7.0 24.7 %slice-start = ((f32[2,20,16,512]{3,2,1,0:T(8,128)}), f32[2,1,16,512]{3,2,1,0:T(8,128)S(1)}, s32[]{:S(2)}) async-start(f32[2,20,16,512]{3,2,1,0:T(8,128)} %param.11), calls=%async_computation.3 | async-start | bytes 131072 | tf_op jit(solution)/shard_map/slice | solution.py:273
  7.0 39.9 %copy-start.1 = (f32[2,20,16,512]{3,2,1,0:T(8,128)S(1)}, f32[2,20,16,512]{3,2,1,0:T(8,128)}, u32[]{:S(2)}) copy-start(f32[2,20,16,512]{3,2,1,0:T(8,128)} %adjoint_ref) | copy-start | bytes 3932164
  9.7 37.2 %all-to-all-start = ((f32[4,64,128]{2,0,1:T(4,128)}), f32[4,64,128]{2,0,1:T(4,128)S(1)}, u32[]{:S(2)}, u32[]{:S(2)}) async-start(f32[4,64,128]{2,0,1:T(4,128)} %copy.18), calls=%async_computation | async-start | bytes 262144 | tf_op jit(solution)/shard_map/all_to_all | solution.py:265
  47.5 24.3 %collective-permute-start = (f32[2,20,1,512]{3,2,1,0:T(1,128)S(1)}, f32[2,20,1,512]{3,2,1,0:T(1,128)S(1)}, u32[]{:S(2)}, u32[]{:S(2)}) collective-permute-start(f32[2,20,1,512]{3,2,1,0:T(1,128)S(1)} %get-tuple-element.27), channel_id=1, source_target_pairs={{0,8},{8,16},{16,24},{24,32},{32,40},{40,48},{48,56},{56,64},{64,7... | collective-permute-start | bytes 245768 | tf_op jit(solution)/shard_map/ppermute | solution.py:137
  49.4 22.4 %collective-permute-start.1 = (f32[2,20,1,512]{3,2,1,0:T(1,128)S(1)}, f32[2,20,1,512]{3,2,1,0:T(1,128)S(1)}, u32[]{:S(2)}, u32[]{:S(2)}) collective-permute-start(f32[2,20,1,512]{3,2,1,0:T(1,128)S(1)} %get-tuple-element.26), channel_id=1, source_target_pairs={{8,0},{16,8},{24,16},{32,24},{40,32},{48,40},{56,48},{64,56},{72,6... | collective-permute-start | bytes 245768 | tf_op jit(solution)/shard_map/ppermute | solution.py:138
  55.1 16.6 %collective-permute-start.2 = (f32[2,20,16,1]{3,2,1,0:T(8,128)S(1)}, f32[2,20,16,1]{3,2,1,0:T(8,128)S(1)}, u32[]{:S(2)}, u32[]{:S(2)}) collective-permute-start(f32[2,20,16,1]{3,2,1,0:T(8,128)S(1)} %get-tuple-element.25), channel_id=1, source_target_pairs={{0,1},{1,2},{2,3},{3,4},{4,5},{5,6},{6,7},{8,9},{9,10},{10,11},{11... | collective-permute-start | bytes 7688 | tf_op jit(solution)/shard_map/ppermute | solution.py:137
  62.2 9.5 %collective-permute-start.3 = (f32[2,20,16,1]{3,2,1,0:T(8,128)S(1)}, f32[2,20,16,1]{3,2,1,0:T(8,128)S(1)}, u32[]{:S(2)}, u32[]{:S(2)}) collective-permute-start(f32[2,20,16,1]{3,2,1,0:T(8,128)S(1)} %get-tuple-element.24), channel_id=1, source_target_pairs={{1,0},{2,1},{3,2},{4,3},{5,4},{6,5},{7,6},{9,8},{10,9},{11,10},{12... | collective-permute-start | bytes 7688 | tf_op jit(solution)/shard_map/ppermute | solution.py:138
  71.7 0.7 copy-start.2
  71.7 0.8 copy-start.3
  71.7 0.8 copy-start.10
  71.8 0.8 copy-start.11
  72.6 33.6 %copy-start.7 = (f32[2,20,16,512]{3,2,1,0:T(8,128)S(1)}, f32[2,20,16,512]{3,2,1,0:T(8,128)}, u32[]{:S(2)}) copy-start(f32[2,20,16,512]{3,2,1,0:T(8,128)} %param.11) | copy-start | bytes 3932164
  72.6 34.4 %copy-start.6 = (f32[16,512]{1,0:T(8,128)S(1)}, f32[16,512]{1,0:T(8,128)}, u32[]{:S(2)}) copy-start(f32[16,512]{1,0:T(8,128)} %friction_ref.3) | copy-start | bytes 98308
  79.5 21.2 %collective-permute-start.4 = (f32[2,20,1,512]{3,2,1,0:T(1,128)S(1)}, f32[2,20,1,512]{3,2,1,0:T(1,128)S(1)}, u32[]{:S(2)}, u32[]{:S(2)}) collective-permute-start(f32[2,20,1,512]{3,2,1,0:T(1,128)S(1)} %get-tuple-element.23), channel_id=1, source_target_pairs={{0,8},{8,16},{16,24},{24,32},{32,40},{40,48},{48,56},{56,64},{64,7... | collective-permute-start | bytes 245768 | tf_op jit(solution)/shard_map/ppermute | solution.py:137
  81.4 19.3 %collective-permute-start.5 = (f32[2,20,1,512]{3,2,1,0:T(1,128)S(1)}, f32[2,20,1,512]{3,2,1,0:T(1,128)S(1)}, u32[]{:S(2)}, u32[]{:S(2)}) collective-permute-start(f32[2,20,1,512]{3,2,1,0:T(1,128)S(1)} %get-tuple-element.22), channel_id=1, source_target_pairs={{8,0},{16,8},{24,16},{32,24},{40,32},{48,40},{56,48},{64,56},{72,6... | collective-permute-start | bytes 245768 | tf_op jit(solution)/shard_map/ppermute | solution.py:138
  87.1 9.1 %collective-permute-start.6 = (f32[2,20,16,1]{3,2,1,0:T(8,128)S(1)}, f32[2,20,16,1]{3,2,1,0:T(8,128)S(1)}, u32[]{:S(2)}, u32[]{:S(2)}) collective-permute-start(f32[2,20,16,1]{3,2,1,0:T(8,128)S(1)} %get-tuple-element.21), channel_id=1, source_target_pairs={{0,1},{1,2},{2,3},{3,4},{4,5},{5,6},{6,7},{8,9},{9,10},{10,11},{11... | collective-permute-start | bytes 7688 | tf_op jit(solution)/shard_map/ppermute | solution.py:137
  91.7 9.0 %collective-permute-start.7 = (f32[2,20,16,1]{3,2,1,0:T(8,128)S(1)}, f32[2,20,16,1]{3,2,1,0:T(8,128)S(1)}, u32[]{:S(2)}, u32[]{:S(2)}) collective-permute-start(f32[2,20,16,1]{3,2,1,0:T(8,128)S(1)} %get-tuple-element.20), channel_id=1, source_target_pairs={{1,0},{2,1},{3,2},{4,3},{5,4},{6,5},{7,6},{9,8},{10,9},{11,10},{12... | collective-permute-start | bytes 7688 | tf_op jit(solution)/shard_map/ppermute | solution.py:138
  96.3 4.4 %copy-start.4 = (f32[2,20,16,1]{3,2,1,0:T(8,128)}, f32[2,20,16,1]{3,2,1,0:T(8,128)S(1)}, u32[]{:S(2)}) copy-start(f32[2,20,16,1]{3,2,1,0:T(8,128)S(1)} %collective-permute-done.6.y_prev_ref) | copy-start | bytes 7684
  100.7 0.7 copy-start.12
  108.1 41.1 %all-to-all-start.1 = ((f32[64,1,136]{2,1,0:T(1,128)}), f32[64,1,136]{2,1,0:T(1,128)S(1)}, u32[]{:S(2)}, u32[]{:S(2)}) async-start(f32[64,1,136]{2,1,0:T(1,128)} %reshape.353), calls=%async_computation.1 | async-start | bytes 131072 | tf_op jit(solution)/shard_map/all_to_all | solution.py:289
  150.8 4.4 %copy-start = (f32[1024,1024]{1,0:T(8,128)S(1)}, f32[1024,1024]{1,0:T(8,128)}, u32[]{:S(2)}) copy-start(f32[1024,1024]{1,0:T(8,128)} %bitcast_multiply_fusion) | copy-start | bytes 12582916
  161.2 23.9 %all-to-all-start.2 = ((f32[64,1,136]{2,1,0:T(1,128)}), f32[64,1,136]{2,1,0:T(1,128)S(1)}, u32[]{:S(2)}, u32[]{:S(2)}) async-start(f32[64,1,136]{2,1,0:T(1,128)} %reshape.355), calls=%async_computation.2 | async-start | bytes 131072 | tf_op jit(solution)/shard_map/all_to_all | solution.py:299
  (2 other events, 1.3 us)

commit v4 on v2

--- a/solution.py
+++ b/solution.py
@@ -157,10 +157,9 @@
     )(adjoint, *edges, coupling, friction, horiz, ice_float, force)
 
 
-def cosine_table(length, after):
+def cosine_table(length):
     block = 32
     freq = lax.broadcasted_iota(jnp.int32, (1, length), 1)
-    freq, _ = lax.optimization_barrier((freq, after))
     coarse = lax.broadcasted_iota(jnp.int32, (length // block, 1), 0)
     fine = lax.broadcasted_iota(jnp.int32, (block, 1), 0)
     period = 4 * length
@@ -285,7 +284,7 @@
     grad = -friction * ice_float * jnp.sum(adjoint[:, 0] * velocity[:, 0], axis=0)
     misfit_column = jnp.broadcast_to(local_misfit, (rows_y, 1))
     sent = jnp.concatenate([grad.T, misfit_column], axis=1)
-    table = cosine_table(wide_count * rows_x, sent)
+    table = cosine_table(wide_count * rows_x)
     lines = lax.all_to_all(sent, "wide", split_axis=0, concat_axis=1, tiled=True)
     width = lines.shape[0]
     lines = lines.reshape(width, wide_count, rows_x + 1)

time: 208 us -> 209 us (level)
  waiting for transfers between devices: 41.5 us -> 27.6 us
  starting transfers between devices: 78.4 us -> 86.9 us
  blocking collectives: 25.9 us -> 30.6 us
  other arithmetic: 19 us -> 21.8 us
    all_to_all x1, starting transfers between devices: 14.5 us -> 30.2 us  [on_device(): lax.all_to_all(sent, 'wide', split_axis=0, concat_axis=1, tiled=True)]
    all_to_all x1, waiting for transfers between devices: 10.8 us -> 1.9 us  [on_device(): lax.all_to_all(packed, 'wide', split_axis=1, concat_axis=1, tiled=True)]
    all_to_all x1, starting transfers between devices: 27 us -> 21.3 us  [on_device(): lax.all_to_all(packed, 'wide', split_axis=1, concat_axis=1, tiled=True)]
    psum x1, blocking collectives: 25.9 us -> 30.6 us  [on_device(): totals = lax.psum(jnp.stack([wide_square, wide_misfit]), 'narrow')]
    ppermute x4, waiting for transfers between devices: 4.42 us -> 0.01 us  [halo_edges(): edges.append(lax.ppermute(first, axis, down))]
    ppermute x4, waiting for transfers between devices: 2.6 us -> 0.01 us  [halo_edges(): edges.append(lax.ppermute(last, axis, up))]
    mul x1, other arithmetic: 2.48 us -> 5.01 us  [cosine_table(): return table * norm_factor.astype(jnp.float32)]
    unnamed x35 -> x42, local copies, waits for them, and re-layouts: 5.7 us -> 5.91 us
  transfers between devices with their start and end apart: 11 -> 11, of which waited for: 5 -> 3; matrix products, arithmetic and copies ran while one was open for 12% -> 10% of each run, Pallas kernels for 0% -> 0%
where the time goes in v4:
time: 209 us; the launch traced here: 208 us
  starting transfers between devices  86.9 us (42%)
  blocking collectives  30.6 us (15%)
  waiting for transfers between devices  27.6 us (13%)
  other arithmetic  21.8 us (10%)
  matrix products  18.1 us (9%)
  local copies, waits for them, and re-layouts  11.7 us (6%)
  Pallas kernels  8.28 us (4%)
  between operations  2.69 us (1%)
    psum x1, blocking collectives, on_device(): totals = lax.psum(jnp.stack([wide_square, wide_misfit]), 'narrow')  30.6 us
    all_to_all x1, starting transfers between devices, on_device(): lax.all_to_all(sent, 'wide', split_axis=0, concat_axis=1, tiled=True)  30.2 us
    all_to_all x1, starting transfers between devices, on_device(): lax.all_to_all(packed, 'wide', split_axis=1, concat_axis=1, tiled=True)  21.3 us
    all_to_all x1, waiting for transfers between devices, on_device(): lax.all_to_all(returned, 'wide', split_axis=1, concat_axis=0, tiled=True)  15 us
    ppermute x4, starting transfers between devices, halo_edges(): edges.append(lax.ppermute(first, axis, down))  14.5 us
    ppermute x4, starting transfers between devices, halo_edges(): edges.append(lax.ppermute(last, axis, up))  14 us
    all_to_all x1, waiting for transfers between devices, on_device(): lax.all_to_all(sent, 'wide', split_axis=0, concat_axis=1, tiled=True)  10.7 us
    dot_general x3, matrix products, exact_dot(): lax.dot_general(split_parts(value), selector, (((1,), (contract,)), ((),...  8.34 us
  transfers between devices with their start and end apart: 11, of which 3 were waited for; matrix products, arithmetic and copies ran while one was open for 10% of the time, Pallas kernels for 0%

profile of v4, /device:TPU:6, one launch (start us, length us, event | category | flops | bytes accessed | tf_op | source)
XLA Modules:
  0.0 207.6 jit_solution(14200830877975749822)
XLA Ops:
  5.7 1.9 fusion.4
  8.3 21.3 %all-to-all-start = ((f32[4,64,128]{2,0,1:T(4,128)}), f32[4,64,128]{2,0,1:T(4,128)S(1)}, u32[]{:S(2)}, u32[]{:S(2)}) async-start(f32[4,64,128]{2,0,1:T(4,128)} %copy.18), calls=%async_computation | async-start | bytes 262144 | tf_op jit(solution)/shard_map/all_to_all | solution.py:264
  29.8 2.9 %collective-permute-start.2 = (f32[2,20,16,1]{3,2,1,0:T(8,128)S(1)}, f32[2,20,16,1]{3,2,1,0:T(8,128)S(1)}, u32[]{:S(2)}, u32[]{:S(2)}) collective-permute-start(f32[2,20,16,1]{3,2,1,0:T(8,128)S(1)} %get-tuple-element.17), channel_id=1, source_target_pairs={{0,1},{1,2},{2,3},{3,4},{4,5},{5,6},{6,7},{8,9},{9,10},{10,11},{11... | collective-permute-start | bytes 7688 | tf_op jit(solution)/shard_map/ppermute | solution.py:137
  34.2 1.9 collective-permute-start
  36.1 5.9 %collective-permute-start.1 = (f32[2,20,1,512]{3,2,1,0:T(1,128)S(1)}, f32[2,20,1,512]{3,2,1,0:T(1,128)S(1)}, u32[]{:S(2)}, u32[]{:S(2)}) collective-permute-start(f32[2,20,1,512]{3,2,1,0:T(1,128)S(1)} %get-tuple-element.18), channel_id=1, source_target_pairs={{8,0},{16,8},{24,16},{32,24},{40,32},{48,40},{56,48},{64,56},{72,6... | collective-permute-start | bytes 245768 | tf_op jit(solution)/shard_map/ppermute | solution.py:138
  43.8 1.9 all-to-all-done
  45.9 3.2 %fusion.1 = f32[96,8192]{1,0:T(8,128)S(1)} fusion(s32[8192]{0:T(1024)S(1)} %get-tuple-element.31, bf16[32,512]{1,0:T(8,128)(2,1)S(1)} %get-tuple-element.28, bf16[32,512]{1,0:T(8,128)(2,1)S(1)} %get-tuple-element.29, bf16[32,512]{1,0:T(8,128)(2,1)S(1)} %get-tuple-element.27), kind=kOutput, calls=%fused_computation.2 | convolution fusion | flops 809795584 | bytes 3276800 | tf_op jit(solution)/shard_map/dot_general | solution.py:204
  50.6 3.2 %fusion = f32[96,512]{1,0:T(8,128)S(1)} fusion(s32[8192]{0:T(1024)S(1)} %get-tuple-element.31, bf16[32,8192]{1,0:T(8,128)(2,1)S(1)} %get-tuple-element.21, bf16[32,8192]{1,0:T(8,128)(2,1)S(1)} %get-tuple-element.22, bf16[32,8192]{1,0:T(8,128)(2,1)S(1)} %get-tuple-element.20), kind=kOutput, calls=%fused_computation.1 | convolution fusion | flops 814219264 | bytes 1802240 | tf_op jit(solution)/shard_map/dot_general | solution.py:204
  55.4 4.2 %shard_map.121.adjoint_ref = f32[2,20,16,512]{3,2,1,0:T(8,128)} custom-call(f32[2,20,16,512]{3,2,1,0:T(8,128)} %adjoint_ref.1, f32[2,20,1,512]{3,2,1,0:T(1,128)} %copy-done.10, f32[2,20,1,512]{3,2,1,0:T(1,128)} %copy-done.11, f32[2,20,16,1]{3,2,1,0:T(8,128)} %copy-done.2, f32[2,20,16,1]{3,2,1,0:T(8,128)} %copy-done.3, f32[19,16,512]{2,1,0:T(8,128)} %coupling_ref.3, ...), custom_call_target="tpu_custom_call" | custom-call | flops 6553600 | bytes 3407872 | tf_op jit(solution)/shard_map/pallas_call | solution.py:145
  60.8 1.4 fusion.58
  62.2 7.2 %collective-permute-start.6 = (f32[2,20,16,1]{3,2,1,0:T(8,128)S(1)}, f32[2,20,16,1]{3,2,1,0:T(8,128)S(1)}, u32[]{:S(2)}, u32[]{:S(2)}) collective-permute-start(f32[2,20,16,1]{3,2,1,0:T(8,128)S(1)} %get-tuple-element.13), channel_id=1, source_target_pairs={{0,1},{1,2},{2,3},{3,4},{4,5},{5,6},{6,7},{8,9},{9,10},{10,11},{11... | collective-permute-start | bytes 7688 | tf_op jit(solution)/shard_map/ppermute | solution.py:137
  70.7 1.9 collective-permute-start.4
  72.6 6.0 %collective-permute-start.5 = (f32[2,20,1,512]{3,2,1,0:T(1,128)S(1)}, f32[2,20,1,512]{3,2,1,0:T(1,128)S(1)}, u32[]{:S(2)}, u32[]{:S(2)}) collective-permute-start(f32[2,20,1,512]{3,2,1,0:T(1,128)S(1)} %get-tuple-element.14), channel_id=1, source_target_pairs={{8,0},{16,8},{24,16},{32,24},{40,32},{48,40},{56,48},{64,56},{72,6... | collective-permute-start | bytes 245768 | tf_op jit(solution)/shard_map/ppermute | solution.py:138
  78.6 4.4 %multiply_subtract_fusion = (f32[32,32,1024]{2,1,0:T(8,128)}, f32[32,32,1024]{2,1,0:T(8,128)}) fusion(f32[32,1024]{1,0:T(8,128)S(1)} %get-tuple-element.39, f32[32,1024]{1,0:T(8,128)S(1)} %get-tuple-element.42, f32[32,1024]{1,0:T(8,128)S(1)} %get-tuple-element.38, f32[32,1024]{1,0:T(8,128)S(1)} %get-tuple-element.43, f32[1024]{0:T(1024)S(1)} %fusion.53), kind=kLoop, calls=%fused_computation.17 | loop fusion | flops 4194304 | bytes 8916992 | tf_op jit(solution)/shard_map/sub | solution.py:170
  85.3 4.1 %shard_map.122 = f32[2,20,16,512]{3,2,1,0:T(8,128)} custom-call(f32[2,20,16,512]{3,2,1,0:T(8,128)} %shard_map.121.adjoint_ref, f32[2,20,1,512]{3,2,1,0:T(1,128)} %copy-done.12, f32[2,20,1,512]{3,2,1,0:T(1,128)} %copy-done.13, f32[2,20,16,1]{3,2,1,0:T(8,128)} %copy-done.4, f32[2,20,16,1]{3,2,1,0:T(8,128)} %copy-done.5, f32[19,16,512]{2,1,0:T(8,128)} %coupling_ref.3, ...), custom_call_target="tpu_custom_call" | custom-call | flops 6553600 | bytes 3407872 | tf_op jit(solution)/shard_map/pallas_call | solution.py:145
  91.3 30.2 %all-to-all-start.1 = ((f32[64,1,136]{2,1,0:T(1,128)}), f32[64,1,136]{2,1,0:T(1,128)S(1)}, u32[]{:S(2)}, u32[]{:S(2)}) async-start(f32[64,1,136]{2,1,0:T(1,128)} %reshape.380), calls=%async_computation.1 | async-start | bytes 131072 | tf_op jit(solution)/shard_map/all_to_all | solution.py:288
  121.5 5.0 %bitcast_multiply_fusion = f32[1024,1024]{1,0:T(8,128)} fusion(f32[32,32,1024]{2,1,0:T(8,128)} %get-tuple-element.23, f32[1024]{0:T(1024)S(1)} %fusion.53), kind=kLoop, calls=%fused_computation.16 | loop fusion | flops 1048576 | bytes 8392704 | tf_op jit(solution)/shard_map/mul | solution.py:174
  126.5 10.7 %all-to-all-done.1 = f32[64,1,136]{2,1,0:T(1,128)S(1)} async-done(((f32[64,1,136]{2,1,0:T(1,128)}), f32[64,1,136]{2,1,0:T(1,128)S(1)}, u32[]{:S(2)}, u32[]{:S(2)}) %all-to-all-start.1) | async-done | bytes 34848 | tf_op jit(solution)/shard_map/all_to_all | solution.py:288
  138.9 4.4 %convolution_divide_fusion = f32[8,1024]{1,0:T(8,128)S(1)} fusion(f32[8,1024]{1,0:T(8,128)S(1)} %reshape.376, f32[1024,1024]{1,0:T(8,128)} %bitcast.83, f32[1024]{0:T(1024)S(1)} %multiply_add_fusion), kind=kOutput, calls=%fused_computation.30 | convolution fusion | flops 100671488 | bytes 4263936 | tf_op jit(solution)/shard_map/dot_general | solution.py:181
  143.3 4.2 %multiply_reduce_fusion = (f32[]{:T(128)}, f32[8,1024]{1,0:T(8,128)S(1)}) fusion(f32[8,1024]{1,0:T(8,128)S(1)} %convolution_divide_fusion, f32[1024,1024]{1,0:T(8,128)S(1)} %copy-done), kind=kOutput, calls=%fused_computation.102 | convolution fusion | flops 100679680 | bytes 4259844 | tf_op jit(solution)/shard_map/dot_general | solution.py:185
  149.3 7.0 %all-to-all-start.2 = ((f32[64,1,136]{2,1,0:T(1,128)}), f32[64,1,136]{2,1,0:T(1,128)S(1)}, u32[]{:S(2)}, u32[]{:S(2)}) async-start(f32[64,1,136]{2,1,0:T(1,128)} %reshape.382), calls=%async_computation.2 | async-start | bytes 131072 | tf_op jit(solution)/shard_map/all_to_all | solution.py:298
  157.0 15.0 %all-to-all-done.2 = f32[64,1,136]{2,1,0:T(1,128)S(1)} async-done(((f32[64,1,136]{2,1,0:T(1,128)}), f32[64,1,136]{2,1,0:T(1,128)S(1)}, u32[]{:S(2)}, u32[]{:S(2)}) %all-to-all-start.2) | async-done | bytes 34848 | tf_op jit(solution)/shard_map/all_to_all | solution.py:298
  173.6 1.4 pad_maximum_fusion.1
  175.0 30.6 %psum.7 = f32[2]{0:T(128)S(1)} all-reduce(f32[2]{0:T(128)S(1)} %pad_maximum_fusion.1), channel_id=1, replica_groups=mesh['wide'=64,'narrow'=8] {'narrow'}, use_global_device_ids=true, to_apply=%region_8.9 | all-reduce | flops 2 | bytes 16 | tf_op jit(solution)/shard_map/psum | solution.py:301
  (103 shorter events, 25.1 us)
Async XLA Ops:
  0.6 3.1 %copy-start.8 = (s32[1,4096,1]{1,2,0:T(1,128)S(1)}, s32[1,4096,1]{1,2,0:T(1,128)}, u32[]{:S(2)}) copy-start(s32[1,4096,1]{1,2,0:T(1,128)} %param.16) | copy-start | bytes 49156
  0.6 3.0 %copy-start.14 = (f32[2,1,4096]{2,1,0:T(1,128)S(1)}, f32[2,1,4096]{2,1,0:T(1,128)}, u32[]{:S(2)}) copy-start(f32[2,1,4096]{2,1,0:T(1,128)} %param.18) | copy-start | bytes 98308
  0.7 3.0 %copy-start.15 = (s32[1,4096]{1,0:T(1,128)S(1)}, s32[1,4096]{1,0:T(1,128)}, u32[]{:S(2)}) copy-start(s32[1,4096]{1,0:T(1,128)} %param.17) | copy-start | bytes 49156
  0.7 3.2 %copy-start.16 = (f32[1,4096]{1,0:T(1,128)S(1)}, f32[1,4096]{1,0:T(1,128)}, u32[]{:S(2)}) copy-start(f32[1,4096]{1,0:T(1,128)} %param.19) | copy-start | bytes 49156
  5.6 24.0 %copy-start.1 = (f32[2,20,16,512]{3,2,1,0:T(8,128)S(1)}, f32[2,20,16,512]{3,2,1,0:T(8,128)}, u32[]{:S(2)}) copy-start(f32[2,20,16,512]{3,2,1,0:T(8,128)} %adjoint_ref.1) | copy-start | bytes 3932164
  5.6 36.5 %copy-start.9 = (s32[16,512]{1,0:T(8,128)S(1)}, s32[16,512]{1,0:T(8,128)}, u32[]{:S(2)}) copy-start(s32[16,512]{1,0:T(8,128)} %param.15) | copy-start | bytes 98308
  5.6 37.1 %slice-start = ((f32[2,20,16,512]{3,2,1,0:T(8,128)}), f32[2,1,16,512]{3,2,1,0:T(8,128)S(1)}, s32[]{:S(2)}) async-start(f32[2,20,16,512]{3,2,1,0:T(8,128)} %param.11), calls=%async_computation.3 | async-start | bytes 131072 | tf_op jit(solution)/shard_map/slice | solution.py:271
  8.3 37.4 %all-to-all-start = ((f32[4,64,128]{2,0,1:T(4,128)}), f32[4,64,128]{2,0,1:T(4,128)S(1)}, u32[]{:S(2)}, u32[]{:S(2)}) async-start(f32[4,64,128]{2,0,1:T(4,128)} %copy.18), calls=%async_computation | async-start | bytes 262144 | tf_op jit(solution)/shard_map/all_to_all | solution.py:264
  29.8 24.7 %collective-permute-start.2 = (f32[2,20,16,1]{3,2,1,0:T(8,128)S(1)}, f32[2,20,16,1]{3,2,1,0:T(8,128)S(1)}, u32[]{:S(2)}, u32[]{:S(2)}) collective-permute-start(f32[2,20,16,1]{3,2,1,0:T(8,128)S(1)} %get-tuple-element.17), channel_id=1, source_target_pairs={{0,1},{1,2},{2,3},{3,4},{4,5},{5,6},{6,7},{8,9},{9,10},{10,11},{11... | collective-permute-start | bytes 7688 | tf_op jit(solution)/shard_map/ppermute | solution.py:137
  32.7 21.8 %collective-permute-start.3 = (f32[2,20,16,1]{3,2,1,0:T(8,128)S(1)}, f32[2,20,16,1]{3,2,1,0:T(8,128)S(1)}, u32[]{:S(2)}, u32[]{:S(2)}) collective-permute-start(f32[2,20,16,1]{3,2,1,0:T(8,128)S(1)} %get-tuple-element.16), channel_id=1, source_target_pairs={{1,0},{2,1},{3,2},{4,3},{5,4},{6,5},{7,6},{9,8},{10,9},{11,10},{12... | collective-permute-start | bytes 7688 | tf_op jit(solution)/shard_map/ppermute | solution.py:138
  34.2 20.3 %collective-permute-start = (f32[2,20,1,512]{3,2,1,0:T(1,128)S(1)}, f32[2,20,1,512]{3,2,1,0:T(1,128)S(1)}, u32[]{:S(2)}, u32[]{:S(2)}) collective-permute-start(f32[2,20,1,512]{3,2,1,0:T(1,128)S(1)} %get-tuple-element.19), channel_id=1, source_target_pairs={{0,8},{8,16},{16,24},{24,32},{32,40},{40,48},{48,56},{56,64},{64,7... | collective-permute-start | bytes 245768 | tf_op jit(solution)/shard_map/ppermute | solution.py:137
  36.1 18.4 %collective-permute-start.1 = (f32[2,20,1,512]{3,2,1,0:T(1,128)S(1)}, f32[2,20,1,512]{3,2,1,0:T(1,128)S(1)}, u32[]{:S(2)}, u32[]{:S(2)}) collective-permute-start(f32[2,20,1,512]{3,2,1,0:T(1,128)S(1)} %get-tuple-element.18), channel_id=1, source_target_pairs={{8,0},{16,8},{24,16},{32,24},{40,32},{48,40},{56,48},{64,56},{72,6... | collective-permute-start | bytes 245768 | tf_op jit(solution)/shard_map/ppermute | solution.py:138
  54.5 0.8 copy-start.3
  54.5 0.8 copy-start.10
  54.5 0.8 copy-start.11
  62.2 21.5 %collective-permute-start.6 = (f32[2,20,16,1]{3,2,1,0:T(8,128)S(1)}, f32[2,20,16,1]{3,2,1,0:T(8,128)S(1)}, u32[]{:S(2)}, u32[]{:S(2)}) collective-permute-start(f32[2,20,16,1]{3,2,1,0:T(8,128)S(1)} %get-tuple-element.13), channel_id=1, source_target_pairs={{0,1},{1,2},{2,3},{3,4},{4,5},{5,6},{6,7},{8,9},{9,10},{10,11},{11... | collective-permute-start | bytes 7688 | tf_op jit(solution)/shard_map/ppermute | solution.py:137
  69.4 14.4 %collective-permute-start.7 = (f32[2,20,16,1]{3,2,1,0:T(8,128)S(1)}, f32[2,20,16,1]{3,2,1,0:T(8,128)S(1)}, u32[]{:S(2)}, u32[]{:S(2)}) collective-permute-start(f32[2,20,16,1]{3,2,1,0:T(8,128)S(1)} %get-tuple-element.12), channel_id=1, source_target_pairs={{1,0},{2,1},{3,2},{4,3},{5,4},{6,5},{7,6},{9,8},{10,9},{11,10},{12... | collective-permute-start | bytes 7688 | tf_op jit(solution)/shard_map/ppermute | solution.py:138
  70.7 13.1 %collective-permute-start.4 = (f32[2,20,1,512]{3,2,1,0:T(1,128)S(1)}, f32[2,20,1,512]{3,2,1,0:T(1,128)S(1)}, u32[]{:S(2)}, u32[]{:S(2)}) collective-permute-start(f32[2,20,1,512]{3,2,1,0:T(1,128)S(1)} %get-tuple-element.15), channel_id=1, source_target_pairs={{0,8},{8,16},{16,24},{24,32},{32,40},{40,48},{48,56},{56,64},{64,7... | collective-permute-start | bytes 245768 | tf_op jit(solution)/shard_map/ppermute | solution.py:137
  72.6 11.2 %collective-permute-start.5 = (f32[2,20,1,512]{3,2,1,0:T(1,128)S(1)}, f32[2,20,1,512]{3,2,1,0:T(1,128)S(1)}, u32[]{:S(2)}, u32[]{:S(2)}) collective-permute-start(f32[2,20,1,512]{3,2,1,0:T(1,128)S(1)} %get-tuple-element.14), channel_id=1, source_target_pairs={{8,0},{16,8},{24,16},{32,24},{40,32},{48,40},{56,48},{64,56},{72,6... | collective-permute-start | bytes 245768 | tf_op jit(solution)/shard_map/ppermute | solution.py:138
  83.0 6.4 %copy-start.7 = (f32[2,20,16,512]{3,2,1,0:T(8,128)S(1)}, f32[2,20,16,512]{3,2,1,0:T(8,128)}, u32[]{:S(2)}) copy-start(f32[2,20,16,512]{3,2,1,0:T(8,128)} %param.11) | copy-start | bytes 3932164
  83.0 7.2 %copy-start.6 = (f32[16,512]{1,0:T(8,128)S(1)}, f32[16,512]{1,0:T(8,128)}, u32[]{:S(2)}) copy-start(f32[16,512]{1,0:T(8,128)} %friction_ref.3) | copy-start | bytes 98308
  91.3 45.9 %all-to-all-start.1 = ((f32[64,1,136]{2,1,0:T(1,128)}), f32[64,1,136]{2,1,0:T(1,128)S(1)}, u32[]{:S(2)}, u32[]{:S(2)}) async-start(f32[64,1,136]{2,1,0:T(1,128)} %reshape.380), calls=%async_computation.1 | async-start | bytes 131072 | tf_op jit(solution)/shard_map/all_to_all | solution.py:288
  138.9 4.4 %copy-start = (f32[1024,1024]{1,0:T(8,128)S(1)}, f32[1024,1024]{1,0:T(8,128)}, u32[]{:S(2)}) copy-start(f32[1024,1024]{1,0:T(8,128)} %bitcast_multiply_fusion) | copy-start | bytes 12582916
  149.3 22.7 %all-to-all-start.2 = ((f32[64,1,136]{2,1,0:T(1,128)}), f32[64,1,136]{2,1,0:T(1,128)S(1)}, u32[]{:S(2)}, u32[]{:S(2)}) async-start(f32[64,1,136]{2,1,0:T(1,128)} %reshape.382), calls=%async_computation.2 | async-start | bytes 131072 | tf_op jit(solution)/shard_map/all_to_all | solution.py:298
  (5 other events, 3.7 us)

commit v5 on v2

--- a/solution.py
+++ b/solution.py
@@ -71,9 +71,9 @@
     ice_ref,
     force_ref,
     out_ref,
-    ratio_ref,
-    partial_ref,
+    *rest,
 ):
+    edge_refs, (ratio_ref, partial_ref) = rest[:-2], rest[-2:]
     comps, layers, rows_x, rows_y = adjoint_ref.shape
     rows = lax.broadcasted_iota(jnp.int32, (rows_x, rows_y), 0)
     cols = lax.broadcasted_iota(jnp.int32, (rows_x, rows_y), 1)
@@ -124,27 +124,47 @@
         for level in range(layers - 2, -1, -1):
             result = partial_ref[comp, level] + ratio_ref[level] * result
             out_ref[comp, level] = ice * result
-
-
-def halo_edges(value):
+    if edge_refs:
+        last_row, first_row, last_col, first_col = edge_refs
+        last_row[...] = out_ref[:, :, rows_x - 1 : rows_x, :]
+        first_row[...] = out_ref[:, :, 0:1, :]
+        for comp in range(comps):
+            for level in range(layers):
+                last_col[comp, level] = out_ref[comp, level, :, rows_y - 128 : rows_y][:, 127:128]
+                first_col[comp, level] = out_ref[comp, level, :, 0:128][:, 0:1]
+
+
+def block_edges(value):
     edges = []
-    for axis, dim in (("wide", 2), ("narrow", 3)):
-        peers, length = (lax.axis_size(axis), value.shape[dim])
+    for dim in (2, 3):
+        length = value.shape[dim]
+        edges.append(lax.slice_in_dim(value, length - 1, length, axis=dim))
+        edges.append(lax.slice_in_dim(value, 0, 1, axis=dim))
+    return edges
+
+
+def halo_edges(block):
+    edges = []
+    for index, axis in enumerate(("wide", "narrow")):
+        peers = lax.axis_size(axis)
         up = [(i, i + 1) for i in range(peers - 1)]
         down = [(j, i) for i, j in up]
-        last = lax.slice_in_dim(value, length - 1, length, axis=dim)
-        first = lax.slice_in_dim(value, 0, 1, axis=dim)
-        edges.append(lax.ppermute(last, axis, up))
-        edges.append(lax.ppermute(first, axis, down))
+        edges.append(lax.ppermute(block[2 * index], axis, up))
+        edges.append(lax.ppermute(block[2 * index + 1], axis, down))
     return edges
 
 
-def column_solve(adjoint, edges, coupling, friction, horiz, ice_float, force):
+def column_solve(adjoint, edges, coupling, friction, horiz, ice_float, force, with_edges):
     comps, layers, rows_x, rows_y = adjoint.shape
     cells = rows_x * rows_y
+    out_shape = jax.ShapeDtypeStruct(adjoint.shape, jnp.float32)
+    if with_edges:
+        row = jax.ShapeDtypeStruct((comps, layers, 1, rows_y), jnp.float32)
+        col = jax.ShapeDtypeStruct((comps, layers, rows_x, 1), jnp.float32)
+        out_shape = (out_shape, row, row, col, col)
     return pl.pallas_call(
         column_kernel,
-        out_shape=jax.ShapeDtypeStruct(adjoint.shape, jnp.float32),
+        out_shape=out_shape,
         scratch_shapes=[
             pltpu.VMEM((layers - 1, rows_x, rows_y), jnp.float32),
             pltpu.VMEM(adjoint.shape, jnp.float32),
@@ -280,8 +300,16 @@
     local_misfit = 0.5 * jnp.sum(weights * jnp.sum(residual * residual, axis=0))
     ice_float = ice_mask.astype(jnp.float32)
     adjoint = adjoint_start
+    block = block_edges(adjoint)
     for sweep_no in range(ITERS):
-        adjoint = column_solve(adjoint, halo_edges(adjoint), coupling, friction, horiz, ice_float, force)
+        solved = column_solve(
+            adjoint, halo_edges(block), coupling, friction, horiz, ice_float, force,
+            sweep_no < ITERS - 1,
+        )
+        if sweep_no < ITERS - 1:
+            adjoint, block = solved[0], list(solved[1:])
+        else:
+            adjoint = solved
     grad = -friction * ice_float * jnp.sum(adjoint[:, 0] * velocity[:, 0], axis=0)
     misfit_column = jnp.broadcast_to(local_misfit, (rows_y, 1))
     sent = jnp.concatenate([grad.T, misfit_column], axis=1)

time: 208 us -> 206 us (level)
  local copies, waits for them, and re-layouts: 13.7 us -> 11.1 us
    slice x4 -> x2, local copies, waits for them, and re-layouts: 4.26 us -> 2.26 us  [block_edges(): edges.append(lax.slice_in_dim(value, 0, 1, axis=dim))]
    unnamed x35 -> x33, local copies, waits for them, and re-layouts: 5.7 us -> 5.08 us
where the time goes in v5:
time: 206 us; the launch traced here: 204 us
  starting transfers between devices  78.4 us (38%)
  waiting for transfers between devices  41.7 us (20%)
  blocking collectives  25.9 us (13%)
  other arithmetic  19 us (9%)
  matrix products  17.4 us (8%)
  local copies, waits for them, and re-layouts  11.1 us (5%)
  Pallas kernels  8.52 us (4%)
  between operations  2.49 us (1%)
    all_to_all x1, starting transfers between devices, on_device(): lax.all_to_all(packed, 'wide', split_axis=1, concat_axis=1, tiled=True)  27 us
    psum x1, blocking collectives, on_device(): totals = lax.psum(jnp.stack([wide_square, wide_misfit]), 'narrow')  25.9 us
    all_to_all x1, waiting for transfers between devices, on_device(): lax.all_to_all(returned, 'wide', split_axis=1, concat_axis=0, tiled=True)  14.6 us
    all_to_all x1, starting transfers between devices, on_device(): lax.all_to_all(sent, 'wide', split_axis=0, concat_axis=1, tiled=True)  14.6 us
    ppermute x4, starting transfers between devices, halo_edges(): edges.append(lax.ppermute(block[2 * index + 1], axis, down))  14.3 us
    ppermute x4, starting transfers between devices, halo_edges(): edges.append(lax.ppermute(block[2 * index], axis, up))  14 us
    all_to_all x1, waiting for transfers between devices, on_device(): lax.all_to_all(packed, 'wide', split_axis=1, concat_axis=1, tiled=True)  10.8 us
    all_to_all x1, waiting for transfers between devices, on_device(): lax.all_to_all(sent, 'wide', split_axis=0, concat_axis=1, tiled=True)  9.03 us
  transfers between devices with their start and end apart: 11, of which 5 were waited for; matrix products, arithmetic and copies ran while one was open for 12% of the time, Pallas kernels for 0%

profile of v5, /device:TPU:6, one launch (start us, length us, event | category | flops | bytes accessed | tf_op | source)
XLA Modules:
  0.0 204.3 jit_solution(6857179480907188802)
XLA Ops:
  0.6 2.1 %fusion.51 = (f32[2,20,1,512]{3,2,1,0:T(1,128)}, f32[2,20,1,512]{3,2,1,0:T(1,128)}) fusion(f32[2,20,16,512]{3,2,1,0:T(8,128)} %adjoint_ref.1), kind=kLoop, calls=%fused_computation.119 | loop fusion | bytes 327680 | tf_op jit(solution)/shard_map/slice | solution.py:142
  2.7 1.9 collective-permute-start
  4.6 5.8 %collective-permute-start.1 = (f32[2,20,1,512]{3,2,1,0:T(1,128)}, f32[2,20,1,512]{3,2,1,0:T(1,128)}, u32[]{:S(2)}, u32[]{:S(2)}) collective-permute-start(f32[2,20,1,512]{3,2,1,0:T(1,128)} %get-tuple-element.26), channel_id=1, source_target_pairs={{8,0},{16,8},{24,16},{32,24},{40,32},{48,40},{56,48},{64,56},{72,6... | collective-permute-start | bytes 245768 | tf_op jit(solution)/shard_map/ppermute | solution.py:153
  19.5 27.0 %all-to-all-start = ((f32[4,64,128]{2,0,1:T(4,128)}), f32[4,64,128]{2,0,1:T(4,128)S(1)}, u32[]{:S(2)}, u32[]{:S(2)}) async-start(f32[4,64,128]{2,0,1:T(4,128)} %copy.18), calls=%async_computation | async-start | bytes 262144 | tf_op jit(solution)/shard_map/all_to_all | solution.py:285
  46.7 2.9 %collective-permute-start.2 = (f32[2,20,16,1]{3,2,1,0:T(8,128)S(1)}, f32[2,20,16,1]{3,2,1,0:T(8,128)S(1)}, u32[]{:S(2)}, u32[]{:S(2)}) collective-permute-start(f32[2,20,16,1]{3,2,1,0:T(8,128)S(1)} %get-tuple-element.25), channel_id=1, source_target_pairs={{0,1},{1,2},{2,3},{3,4},{4,5},{5,6},{6,7},{8,9},{9,10},{10,11},{11... | collective-permute-start | bytes 7688 | tf_op jit(solution)/shard_map/ppermute | solution.py:152
  51.8 10.8 %all-to-all-done = f32[4,64,128]{2,0,1:T(4,128)S(1)} async-done(((f32[4,64,128]{2,0,1:T(4,128)}), f32[4,64,128]{2,0,1:T(4,128)S(1)}, u32[]{:S(2)}, u32[]{:S(2)}) %all-to-all-start) | async-done | bytes 131104 | tf_op jit(solution)/shard_map/all_to_all | solution.py:285
  62.8 3.2 %fusion.1 = f32[96,8192]{1,0:T(8,128)S(1)} fusion(s32[8192]{0:T(1024)S(1)} %get-tuple-element.39, bf16[32,512]{1,0:T(8,128)(2,1)S(1)} %get-tuple-element.36, bf16[32,512]{1,0:T(8,128)(2,1)S(1)} %get-tuple-element.37, bf16[32,512]{1,0:T(8,128)(2,1)S(1)} %get-tuple-element.35), kind=kOutput, calls=%fused_computation.2 | convolution fusion | flops 809795584 | bytes 3276800 | tf_op jit(solution)/shard_map/dot_general | solution.py:225
  67.5 3.2 %fusion = f32[96,512]{1,0:T(8,128)S(1)} fusion(s32[8192]{0:T(1024)S(1)} %get-tuple-element.39, bf16[32,8192]{1,0:T(8,128)(2,1)S(1)} %get-tuple-element.29, bf16[32,8192]{1,0:T(8,128)(2,1)S(1)} %get-tuple-element.30, bf16[32,8192]{1,0:T(8,128)(2,1)S(1)} %get-tuple-element.28), kind=kOutput, calls=%fused_computation.1 | convolution fusion | flops 814219264 | bytes 1802240 | tf_op jit(solution)/shard_map/dot_general | solution.py:225
  72.2 4.4 %shard_map.121 = (f32[2,20,16,512]{3,2,1,0:T(8,128)}, f32[2,20,1,512]{3,2,1,0:T(1,128)}, f32[2,20,1,512]{3,2,1,0:T(1,128)}, f32[2,20,16,1]{3,2,1,0:T(8,128)}, f32[2,20,16,1]{3,2,1,0:T(8,128)}) custom-call(f32[2,20,16,512]{3,2,1,0:T(8,128)} %adjoint_ref.1, f32[2,20,1,512]{3,2,1,0:T(1,128)} %copy-done.10, f32[2,20,1,512]{3,2,1,0:T(1,128)} %collective-permute-done.1.x_next_ref, ...), custom_call_target="tpu_custom_call" | custom-call | flops 6553600 | bytes 3407872 | tf_op jit(solution)/shard_map/pallas_call | solution.py:165
  76.6 1.9 collective-permute-start.4
  78.5 5.8 %collective-permute-start.5 = (f32[2,20,1,512]{3,2,1,0:T(1,128)}, f32[2,20,1,512]{3,2,1,0:T(1,128)S(1)}, u32[]{:S(2)}, u32[]{:S(2)}) collective-permute-start(f32[2,20,1,512]{3,2,1,0:T(1,128)} %get-tuple-element.11), channel_id=1, source_target_pairs={{8,0},{16,8},{24,16},{32,24},{40,32},{48,40},{56,48},{64,56},{72,6... | collective-permute-start | bytes 245768 | tf_op jit(solution)/shard_map/ppermute | solution.py:153
  84.3 7.2 %collective-permute-start.6 = (f32[2,20,16,1]{3,2,1,0:T(8,128)}, f32[2,20,16,1]{3,2,1,0:T(8,128)S(1)}, u32[]{:S(2)}, u32[]{:S(2)}) collective-permute-start(f32[2,20,16,1]{3,2,1,0:T(8,128)} %get-tuple-element.12), channel_id=1, source_target_pairs={{0,1},{1,2},{2,3},{3,4},{4,5},{5,6},{6,7},{8,9},{9,10},{10,11},{11... | collective-permute-start | bytes 7688 | tf_op jit(solution)/shard_map/ppermute | solution.py:152
  93.5 2.9 %collective-permute-done.6.y_prev_ref = f32[2,20,16,1]{3,2,1,0:T(8,128)S(1)} collective-permute-done((f32[2,20,16,1]{3,2,1,0:T(8,128)}, f32[2,20,16,1]{3,2,1,0:T(8,128)S(1)}, u32[]{:S(2)}, u32[]{:S(2)}) %collective-permute-start.6) | collective-permute-done | bytes 2592 | tf_op jit(solution)/shard_map/ppermute | solution.py:152
  96.4 4.3 %collective-permute-done.7.y_next_ref = f32[2,20,16,1]{3,2,1,0:T(8,128)S(1)} collective-permute-done((f32[2,20,16,1]{3,2,1,0:T(8,128)}, f32[2,20,16,1]{3,2,1,0:T(8,128)S(1)}, u32[]{:S(2)}, u32[]{:S(2)}) %collective-permute-start.7) | collective-permute-done | bytes 2592 | tf_op jit(solution)/shard_map/ppermute | solution.py:153
  101.5 4.1 %shard_map.122 = f32[2,20,16,512]{3,2,1,0:T(8,128)} custom-call(f32[2,20,16,512]{3,2,1,0:T(8,128)} %get-tuple-element.9.adjoint_ref, f32[2,20,1,512]{3,2,1,0:T(1,128)} %copy-done.11, f32[2,20,1,512]{3,2,1,0:T(1,128)} %copy-done.12, f32[2,20,16,1]{3,2,1,0:T(8,128)} %copy-done.2, f32[2,20,16,1]{3,2,1,0:T(8,128)} %copy-done.3, f32[19,16,512]{2,1,0:T(8,128)} %coupling_ref.3, ...), custom_call_target="tpu_custom_call" | custom-call | flops 6553600 | bytes 3407872 | tf_op jit(solution)/shard_map/pallas_call | solution.py:165
  107.5 14.6 %all-to-all-start.1 = ((f32[64,1,136]{2,1,0:T(1,128)}), f32[64,1,136]{2,1,0:T(1,128)S(1)}, u32[]{:S(2)}, u32[]{:S(2)}) async-start(f32[64,1,136]{2,1,0:T(1,128)} %reshape.412), calls=%async_computation.1 | async-start | bytes 131072 | tf_op jit(solution)/shard_map/all_to_all | solution.py:317
  123.2 2.7 %multiply_subtract_fusion = (f32[32,32,1024]{2,1,0:T(8,128)S(1)}, f32[32,32,1024]{2,1,0:T(8,128)}) fusion(f32[32,1024]{1,0:T(8,128)S(1)} %get-tuple-element.46, f32[32,1024]{1,0:T(8,128)S(1)} %get-tuple-element.43, f32[32,1024]{1,0:T(8,128)S(1)} %get-tuple-element.47, f32[32,1024]{1,0:T(8,128)S(1)} %get-tuple-element.42, f32[1024]{0:T(1024)S(1)} %bitcast.97), kind=kLoop, calls=%fused_computation.17 | loop fusion | flops 4194304 | bytes 8916992 | tf_op jit(solution)/shard_map/sub | solution.py:191
  125.8 2.5 %bitcast_multiply_fusion = f32[1024,1024]{1,0:T(8,128)} fusion(f32[32,32,1024]{2,1,0:T(8,128)S(1)} %get-tuple-element.31, f32[1024]{0:T(1024)S(1)} %bitcast.98), kind=kLoop, calls=%fused_computation.16 | loop fusion | flops 1048576 | bytes 8392704 | tf_op jit(solution)/shard_map/mul | solution.py:195
  128.3 9.0 %all-to-all-done.1 = f32[64,1,136]{2,1,0:T(1,128)S(1)} async-done(((f32[64,1,136]{2,1,0:T(1,128)}), f32[64,1,136]{2,1,0:T(1,128)S(1)}, u32[]{:S(2)}, u32[]{:S(2)}) %all-to-all-start.1) | async-done | bytes 34848 | tf_op jit(solution)/shard_map/all_to_all | solution.py:317
  139.0 4.4 %convolution_divide_fusion = f32[8,1024]{1,0:T(8,128)S(1)} fusion(f32[8,1024]{1,0:T(8,128)S(1)} %reshape.408, f32[1024,1024]{1,0:T(8,128)} %bitcast.84, f32[1024]{0:T(1024)S(1)} %multiply_add_fusion), kind=kOutput, calls=%fused_computation.30 | convolution fusion | flops 100671488 | bytes 4263936 | tf_op jit(solution)/shard_map/dot_general | solution.py:202
  143.5 4.2 %multiply_reduce_fusion = (f32[]{:T(128)}, f32[8,1024]{1,0:T(8,128)S(1)}) fusion(f32[8,1024]{1,0:T(8,128)S(1)} %convolution_divide_fusion, f32[1024,1024]{1,0:T(8,128)S(1)} %copy-done), kind=kOutput, calls=%fused_computation.99 | convolution fusion | flops 100679680 | bytes 4259844 | tf_op jit(solution)/shard_map/dot_general | solution.py:206
  149.4 8.6 %all-to-all-start.2 = ((f32[64,1,136]{2,1,0:T(1,128)}), f32[64,1,136]{2,1,0:T(1,128)S(1)}, u32[]{:S(2)}, u32[]{:S(2)}) async-start(f32[64,1,136]{2,1,0:T(1,128)} %reshape.414), calls=%async_computation.2 | async-start | bytes 131072 | tf_op jit(solution)/shard_map/all_to_all | solution.py:327
  158.8 14.6 %all-to-all-done.2 = f32[64,1,136]{2,1,0:T(1,128)S(1)} async-done(((f32[64,1,136]{2,1,0:T(1,128)}), f32[64,1,136]{2,1,0:T(1,128)S(1)}, u32[]{:S(2)}, u32[]{:S(2)}) %all-to-all-start.2) | async-done | bytes 34848 | tf_op jit(solution)/shard_map/all_to_all | solution.py:327
  176.4 25.9 %psum.7 = f32[2]{0:T(128)S(1)} all-reduce(f32[2]{0:T(128)S(1)} %pad_maximum_fusion.1), channel_id=1, replica_groups=mesh['wide'=64,'narrow'=8] {'narrow'}, use_global_device_ids=true, to_apply=%region_8.9 | all-reduce | flops 2 | bytes 16 | tf_op jit(solution)/shard_map/psum | solution.py:330
  (93 shorter events, 27.9 us)
Async XLA Ops:
  2.7 68.7 %collective-permute-start = (f32[2,20,1,512]{3,2,1,0:T(1,128)}, f32[2,20,1,512]{3,2,1,0:T(1,128)S(1)}, u32[]{:S(2)}, u32[]{:S(2)}) collective-permute-start(f32[2,20,1,512]{3,2,1,0:T(1,128)} %get-tuple-element.27), channel_id=1, source_target_pairs={{0,8},{8,16},{16,24},{24,32},{32,40},{40,48},{48,56},{56,64},{64,7... | collective-permute-start | bytes 245768 | tf_op jit(solution)/shard_map/ppermute | solution.py:152
  4.6 66.8 %collective-permute-start.1 = (f32[2,20,1,512]{3,2,1,0:T(1,128)}, f32[2,20,1,512]{3,2,1,0:T(1,128)}, u32[]{:S(2)}, u32[]{:S(2)}) collective-permute-start(f32[2,20,1,512]{3,2,1,0:T(1,128)} %get-tuple-element.26), channel_id=1, source_target_pairs={{8,0},{16,8},{24,16},{32,24},{40,32},{48,40},{56,48},{64,56},{72,6... | collective-permute-start | bytes 245768 | tf_op jit(solution)/shard_map/ppermute | solution.py:153
  14.0 1.2 copy-start.8
  16.8 29.7 %copy-start.1 = (f32[2,20,16,512]{3,2,1,0:T(8,128)S(1)}, f32[2,20,16,512]{3,2,1,0:T(8,128)}, u32[]{:S(2)}) copy-start(f32[2,20,16,512]{3,2,1,0:T(8,128)} %adjoint_ref.1) | copy-start | bytes 3932164
  16.8 34.3 %copy-start.9 = (s32[16,512]{1,0:T(8,128)S(1)}, s32[16,512]{1,0:T(8,128)}, u32[]{:S(2)}) copy-start(s32[16,512]{1,0:T(8,128)} %param.15) | copy-start | bytes 98308
  16.8 35.0 %slice-start = ((f32[2,20,16,512]{3,2,1,0:T(8,128)}), f32[2,1,16,512]{3,2,1,0:T(8,128)S(1)}, s32[]{:S(2)}) async-start(f32[2,20,16,512]{3,2,1,0:T(8,128)} %param.11), calls=%async_computation.3 | async-start | bytes 131072 | tf_op jit(solution)/shard_map/slice | solution.py:292
  19.5 43.1 %all-to-all-start = ((f32[4,64,128]{2,0,1:T(4,128)}), f32[4,64,128]{2,0,1:T(4,128)S(1)}, u32[]{:S(2)}, u32[]{:S(2)}) async-start(f32[4,64,128]{2,0,1:T(4,128)} %copy.18), calls=%async_computation | async-start | bytes 262144 | tf_op jit(solution)/shard_map/all_to_all | solution.py:285
  46.7 24.7 %collective-permute-start.2 = (f32[2,20,16,1]{3,2,1,0:T(8,128)S(1)}, f32[2,20,16,1]{3,2,1,0:T(8,128)S(1)}, u32[]{:S(2)}, u32[]{:S(2)}) collective-permute-start(f32[2,20,16,1]{3,2,1,0:T(8,128)S(1)} %get-tuple-element.25), channel_id=1, source_target_pairs={{0,1},{1,2},{2,3},{3,4},{4,5},{5,6},{6,7},{8,9},{9,10},{10,11},{11... | collective-permute-start | bytes 7688 | tf_op jit(solution)/shard_map/ppermute | solution.py:152
  49.6 21.8 %collective-permute-start.3 = (f32[2,20,16,1]{3,2,1,0:T(8,128)S(1)}, f32[2,20,16,1]{3,2,1,0:T(8,128)S(1)}, u32[]{:S(2)}, u32[]{:S(2)}) collective-permute-start(f32[2,20,16,1]{3,2,1,0:T(8,128)S(1)} %get-tuple-element.24), channel_id=1, source_target_pairs={{1,0},{2,1},{3,2},{4,3},{5,4},{6,5},{7,6},{9,8},{10,9},{11,10},{12... | collective-permute-start | bytes 7688 | tf_op jit(solution)/shard_map/ppermute | solution.py:153
  70.7 34.9 %copy-start.7 = (f32[2,20,16,512]{3,2,1,0:T(8,128)S(1)}, f32[2,20,16,512]{3,2,1,0:T(8,128)}, u32[]{:S(2)}) copy-start(f32[2,20,16,512]{3,2,1,0:T(8,128)} %param.11) | copy-start | bytes 3932164
  70.7 35.7 %copy-start.6 = (f32[16,512]{1,0:T(8,128)S(1)}, f32[16,512]{1,0:T(8,128)}, u32[]{:S(2)}) copy-start(f32[16,512]{1,0:T(8,128)} %friction_ref.3) | copy-start | bytes 98308
  71.4 0.8 copy-start.5
  71.4 0.8 copy-start.10
  76.6 24.1 %collective-permute-start.4 = (f32[2,20,1,512]{3,2,1,0:T(1,128)}, f32[2,20,1,512]{3,2,1,0:T(1,128)S(1)}, u32[]{:S(2)}, u32[]{:S(2)}) collective-permute-start(f32[2,20,1,512]{3,2,1,0:T(1,128)} %get-tuple-element.10), channel_id=1, source_target_pairs={{0,8},{8,16},{16,24},{24,32},{32,40},{40,48},{48,56},{56,64},{64,7... | collective-permute-start | bytes 245768 | tf_op jit(solution)/shard_map/ppermute | solution.py:152
  78.5 22.2 %collective-permute-start.5 = (f32[2,20,1,512]{3,2,1,0:T(1,128)}, f32[2,20,1,512]{3,2,1,0:T(1,128)S(1)}, u32[]{:S(2)}, u32[]{:S(2)}) collective-permute-start(f32[2,20,1,512]{3,2,1,0:T(1,128)} %get-tuple-element.11), channel_id=1, source_target_pairs={{8,0},{16,8},{24,16},{32,24},{40,32},{48,40},{56,48},{64,56},{72,6... | collective-permute-start | bytes 245768 | tf_op jit(solution)/shard_map/ppermute | solution.py:153
  84.3 12.1 %collective-permute-start.6 = (f32[2,20,16,1]{3,2,1,0:T(8,128)}, f32[2,20,16,1]{3,2,1,0:T(8,128)S(1)}, u32[]{:S(2)}, u32[]{:S(2)}) collective-permute-start(f32[2,20,16,1]{3,2,1,0:T(8,128)} %get-tuple-element.12), channel_id=1, source_target_pairs={{0,1},{1,2},{2,3},{3,4},{4,5},{5,6},{6,7},{8,9},{9,10},{10,11},{11... | collective-permute-start | bytes 7688 | tf_op jit(solution)/shard_map/ppermute | solution.py:152
  91.5 9.2 %collective-permute-start.7 = (f32[2,20,16,1]{3,2,1,0:T(8,128)}, f32[2,20,16,1]{3,2,1,0:T(8,128)S(1)}, u32[]{:S(2)}, u32[]{:S(2)}) collective-permute-start(f32[2,20,16,1]{3,2,1,0:T(8,128)} %get-tuple-element.13), channel_id=1, source_target_pairs={{1,0},{2,1},{3,2},{4,3},{5,4},{6,5},{7,6},{9,8},{10,9},{11,10},{12... | collective-permute-start | bytes 7688 | tf_op jit(solution)/shard_map/ppermute | solution.py:153
  96.4 4.3 %copy-start.2 = (f32[2,20,16,1]{3,2,1,0:T(8,128)}, f32[2,20,16,1]{3,2,1,0:T(8,128)S(1)}, u32[]{:S(2)}) copy-start(f32[2,20,16,1]{3,2,1,0:T(8,128)S(1)} %collective-permute-done.6.y_prev_ref) | copy-start | bytes 7684
  100.7 0.7 copy-start.3
  100.7 0.7 copy-start.11
  100.7 0.8 copy-start.12
  107.5 29.9 %all-to-all-start.1 = ((f32[64,1,136]{2,1,0:T(1,128)}), f32[64,1,136]{2,1,0:T(1,128)S(1)}, u32[]{:S(2)}, u32[]{:S(2)}) async-start(f32[64,1,136]{2,1,0:T(1,128)} %reshape.412), calls=%async_computation.1 | async-start | bytes 131072 | tf_op jit(solution)/shard_map/all_to_all | solution.py:317
  139.0 4.4 %copy-start = (f32[1024,1024]{1,0:T(8,128)S(1)}, f32[1024,1024]{1,0:T(8,128)}, u32[]{:S(2)}) copy-start(f32[1024,1024]{1,0:T(8,128)} %bitcast_multiply_fusion) | copy-start | bytes 12582916
  149.4 23.9 %all-to-all-start.2 = ((f32[64,1,136]{2,1,0:T(1,128)}), f32[64,1,136]{2,1,0:T(1,128)S(1)}, u32[]{:S(2)}, u32[]{:S(2)}) async-start(f32[64,1,136]{2,1,0:T(1,128)} %reshape.414), calls=%async_computation.2 | async-start | bytes 131072 | tf_op jit(solution)/shard_map/all_to_all | solution.py:327
  (1 other events, 0.7 us)

commit v6 on v5

--- a/solution.py
+++ b/solution.py
@@ -149,8 +149,12 @@
         peers = lax.axis_size(axis)
         up = [(i, i + 1) for i in range(peers - 1)]
         down = [(j, i) for i, j in up]
-        edges.append(lax.ppermute(block[2 * index], axis, up))
-        edges.append(lax.ppermute(block[2 * index + 1], axis, down))
+        for part, pairs in ((block[2 * index], up), (block[2 * index + 1], down)):
+            if index:
+                sent = lax.ppermute(part.reshape(part.shape[0], -1), axis, pairs)
+                edges.append(sent.reshape(part.shape))
+            else:
+                edges.append(lax.ppermute(part, axis, pairs))
     return edges
 
 

time: 206 us -> 209 us (1.015)
  waiting for transfers between devices: 41.7 us -> 29.6 us
  starting transfers between devices: 78.4 us -> 87.5 us
  blocking collectives: 25.9 us -> 28.1 us
  local copies, waits for them, and re-layouts: 11.1 us -> 13.3 us
  other arithmetic: 19 us -> 21.2 us
    all_to_all x1, starting transfers between devices: 14.6 us -> 32 us  [on_device(): lax.all_to_all(sent, 'wide', split_axis=0, concat_axis=1, tiled=True)]
    all_to_all x1, waiting for transfers between devices: 10.8 us -> 0.01 us  [on_device(): lax.all_to_all(packed, 'wide', split_axis=1, concat_axis=1, tiled=True)]
    all_to_all x1, starting transfers between devices: 27 us -> 21.3 us  [on_device(): lax.all_to_all(packed, 'wide', split_axis=1, concat_axis=1, tiled=True)]
    reshape x0 -> x8, local copies, waits for them, and re-layouts: none -> 4.24 us  [the longest x4 3.9 us: halo_edges(): edges.append(sent.reshape(part.shape))]
    ppermute x8, waiting for transfers between devices: 7.23 us -> 4.87 us  [the longest x4 4.86 us: halo_edges(): sent = lax.ppermute(part.reshape(part.shape[0], -1), axis, pairs)]
    pallas_call x0 -> x2, other arithmetic: none -> 2.27 us  [column_solve(): pl.pallas_call(column_kernel, out_shape=out_shape, scratch_shapes=[pltpu....]
    psum x1, blocking collectives: 25.9 us -> 28.1 us  [on_device(): totals = lax.psum(jnp.stack([wide_square, wide_misfit]), 'narrow')]
    unnamed x33 -> x27, local copies, waits for them, and re-layouts: 5.08 us -> 4.83 us
  transfers between devices with their start and end apart: 11 -> 11, of which waited for: 5 -> 4; matrix products, arithmetic and copies ran while one was open for 12% -> 11% of each run, Pallas kernels for 0% -> 0%
where the time goes in v6:
time: 209 us; the launch traced here: 208 us
  starting transfers between devices  87.5 us (42%)
  waiting for transfers between devices  29.6 us (14%)
  blocking collectives  28.1 us (13%)
  other arithmetic  21.2 us (10%)
  matrix products  17.4 us (8%)
  local copies, waits for them, and re-layouts  13.3 us (6%)
  Pallas kernels  8.59 us (4%)
  between operations  2.47 us (1%)
    all_to_all x1, starting transfers between devices, on_device(): lax.all_to_all(sent, 'wide', split_axis=0, concat_axis=1, tiled=True)  32 us
    psum x1, blocking collectives, on_device(): totals = lax.psum(jnp.stack([wide_square, wide_misfit]), 'narrow')  28.1 us
    all_to_all x1, starting transfers between devices, on_device(): lax.all_to_all(packed, 'wide', split_axis=1, concat_axis=1, tiled=True)  21.3 us
    ppermute x4, starting transfers between devices, halo_edges(): edges.append(lax.ppermute(part, axis, pairs))  15.3 us
    all_to_all x1, waiting for transfers between devices, on_device(): lax.all_to_all(returned, 'wide', split_axis=1, concat_axis=0, tiled=True)  15.1 us
    ppermute x4, starting transfers between devices, halo_edges(): sent = lax.ppermute(part.reshape(part.shape[0], -1), axis, pairs)  10.9 us
    all_to_all x1, waiting for transfers between devices, on_device(): lax.all_to_all(sent, 'wide', split_axis=0, concat_axis=1, tiled=True)  9.6 us
    pallas_call x2, Pallas kernels, column_solve(): pl.pallas_call(column_kernel, out_shape=out_shape, scratch_shapes=[pltpu....  8.59 us
  transfers between devices with their start and end apart: 11, of which 4 were waited for; matrix products, arithmetic and copies ran while one was open for 11% of the time, Pallas kernels for 0%

profile of v6, /device:TPU:6, one launch (start us, length us, event | category | flops | bytes accessed | tf_op | source)
XLA Modules:
  0.0 208.1 jit_solution(8353273235145121990)
XLA Ops:
  7.0 1.9 fusion.4
  9.7 21.3 %all-to-all-start = ((f32[4,64,128]{2,0,1:T(4,128)}), f32[4,64,128]{2,0,1:T(4,128)S(1)}, u32[]{:S(2)}, u32[]{:S(2)}) async-start(f32[4,64,128]{2,0,1:T(4,128)} %copy.22), calls=%async_computation | async-start | bytes 262144 | tf_op jit(solution)/shard_map/all_to_all | solution.py:289
  31.1 2.1 collective-permute-start
  33.2 5.6 %collective-permute-start.1 = (f32[2,20,1,512]{3,2,1,0:T(1,128)S(1)}, f32[2,20,1,512]{3,2,1,0:T(1,128)S(1)}, u32[]{:S(2)}, u32[]{:S(2)}) collective-permute-start(f32[2,20,1,512]{3,2,1,0:T(1,128)S(1)} %get-tuple-element.26), channel_id=1, source_target_pairs={{8,0},{16,8},{24,16},{32,24},{40,32},{48,40},{56,48},{64,56},{72,6... | collective-permute-start | bytes 245768 | tf_op jit(solution)/shard_map/ppermute | solution.py:157
  39.2 2.9 %collective-permute-start.2 = (f32[2,320]{1,0:T(2,128)S(1)}, f32[2,320]{1,0:T(2,128)S(1)}, u32[]{:S(2)}, u32[]{:S(2)}) collective-permute-start(f32[2,320]{1,0:T(2,128)S(1)} %reshape.432), channel_id=1, source_target_pairs={{0,1},{1,2},{2,3},{3,4},{4,5},{5,6},{6,7},{8,9},{9,10},{10,11},{11... | collective-permute-start | bytes 7688 | tf_op jit(solution)/shard_map/ppermute | solution.py:154
  42.2 1.5 collective-permute-start.3
  45.4 2.3 %collective-permute-done.3 = f32[2,320]{1,0:T(2,128)S(1)} collective-permute-done((f32[2,320]{1,0:T(2,128)S(1)}, f32[2,320]{1,0:T(2,128)S(1)}, u32[]{:S(2)}, u32[]{:S(2)}) %collective-permute-start.3) | collective-permute-done | bytes 2592 | tf_op jit(solution)/shard_map/ppermute | solution.py:154
  48.9 3.2 %fusion.1 = f32[96,8192]{1,0:T(8,128)S(1)} fusion(s32[8192]{0:T(1024)S(1)} %get-tuple-element.39, bf16[32,512]{1,0:T(8,128)(2,1)S(1)} %get-tuple-element.36, bf16[32,512]{1,0:T(8,128)(2,1)S(1)} %get-tuple-element.37, bf16[32,512]{1,0:T(8,128)(2,1)S(1)} %get-tuple-element.35), kind=kOutput, calls=%fused_computation.2 | convolution fusion | flops 809795584 | bytes 3276800 | tf_op jit(solution)/shard_map/dot_general | solution.py:229
  53.6 3.2 %fusion = f32[96,512]{1,0:T(8,128)S(1)} fusion(s32[8192]{0:T(1024)S(1)} %get-tuple-element.39, bf16[32,8192]{1,0:T(8,128)(2,1)S(1)} %get-tuple-element.29, bf16[32,8192]{1,0:T(8,128)(2,1)S(1)} %get-tuple-element.30, bf16[32,8192]{1,0:T(8,128)(2,1)S(1)} %get-tuple-element.28), kind=kOutput, calls=%fused_computation.1 | convolution fusion | flops 814219264 | bytes 1802240 | tf_op jit(solution)/shard_map/dot_general | solution.py:229
  58.1 4.5 %shard_map.121 = (f32[2,20,16,512]{3,2,1,0:T(8,128)}, f32[2,20,1,512]{3,2,1,0:T(1,128)}, f32[2,20,1,512]{3,2,1,0:T(1,128)}, f32[2,20,16,1]{3,2,1,0:T(8,128)}, f32[2,20,16,1]{3,2,1,0:T(8,128)}) custom-call(f32[2,20,16,512]{3,2,1,0:T(8,128)} %adjoint_ref.1, f32[2,20,1,512]{3,2,1,0:T(1,128)} %copy-done.6, f32[2,20,1,512]{3,2,1,0:T(1,128)} %copy-done.7, ...), custom_call_target="tpu_custom_call" | custom-call | flops 6553600 | bytes 3407872 | tf_op jit(solution)/shard_map/pallas_call | solution.py:169
  62.6 1.9 collective-permute-start.4
  64.5 5.8 %collective-permute-start.5 = (f32[2,20,1,512]{3,2,1,0:T(1,128)}, f32[2,20,1,512]{3,2,1,0:T(1,128)S(1)}, u32[]{:S(2)}, u32[]{:S(2)}) collective-permute-start(f32[2,20,1,512]{3,2,1,0:T(1,128)} %get-tuple-element.11), channel_id=1, source_target_pairs={{8,0},{16,8},{24,16},{32,24},{40,32},{48,40},{56,48},{64,56},{72,6... | collective-permute-start | bytes 245768 | tf_op jit(solution)/shard_map/ppermute | solution.py:157
  71.5 5.2 %collective-permute-start.6 = (f32[2,320]{1,0:T(2,128)S(1)}, f32[2,320]{1,0:T(2,128)S(1)}, u32[]{:S(2)}, u32[]{:S(2)}) collective-permute-start(f32[2,320]{1,0:T(2,128)S(1)} %reshape.436), channel_id=1, source_target_pairs={{0,1},{1,2},{2,3},{3,4},{4,5},{5,6},{6,7},{8,9},{9,10},{10,11},{11... | collective-permute-start | bytes 7688 | tf_op jit(solution)/shard_map/ppermute | solution.py:154
  80.9 2.5 %collective-permute-done.7 = f32[2,320]{1,0:T(2,128)S(1)} collective-permute-done((f32[2,320]{1,0:T(2,128)S(1)}, f32[2,320]{1,0:T(2,128)S(1)}, u32[]{:S(2)}, u32[]{:S(2)}) %collective-permute-start.7) | collective-permute-done | bytes 2592 | tf_op jit(solution)/shard_map/ppermute | solution.py:154
  85.1 4.1 %shard_map.122 = f32[2,20,16,512]{3,2,1,0:T(8,128)} custom-call(f32[2,20,16,512]{3,2,1,0:T(8,128)} %get-tuple-element.9.adjoint_ref, f32[2,20,1,512]{3,2,1,0:T(1,128)} %copy-done.8, f32[2,20,1,512]{3,2,1,0:T(1,128)} %copy-done.9, f32[2,20,16,1]{3,2,1,0:T(8,128)} %reshape.445.y_prev_ref, f32[2,20,16,1]{3,2,1,0:T(8,128)} %reshape.446.y_next_ref, ...), custom_call_target="tpu_custom_call" | custom-call | flops 6553600 | bytes 3407872 | tf_op jit(solution)/shard_map/pallas_call | solution.py:169
  91.1 32.0 %all-to-all-start.1 = ((f32[64,1,136]{2,1,0:T(1,128)}), f32[64,1,136]{2,1,0:T(1,128)S(1)}, u32[]{:S(2)}, u32[]{:S(2)}) async-start(f32[64,1,136]{2,1,0:T(1,128)} %reshape.452), calls=%async_computation.1 | async-start | bytes 131072 | tf_op jit(solution)/shard_map/all_to_all | solution.py:321
  124.2 2.7 %multiply_subtract_fusion = (f32[32,32,1024]{2,1,0:T(8,128)S(1)}, f32[32,32,1024]{2,1,0:T(8,128)}) fusion(f32[32,1024]{1,0:T(8,128)S(1)} %get-tuple-element.46, f32[32,1024]{1,0:T(8,128)S(1)} %get-tuple-element.43, f32[32,1024]{1,0:T(8,128)S(1)} %get-tuple-element.47, f32[32,1024]{1,0:T(8,128)S(1)} %get-tuple-element.42, f32[1024]{0:T(1024)S(1)} %bitcast.97), kind=kLoop, calls=%fused_computation.17 | loop fusion | flops 4194304 | bytes 8916992 | tf_op jit(solution)/shard_map/sub | solution.py:195
  126.9 2.5 %bitcast_multiply_fusion = f32[1024,1024]{1,0:T(8,128)} fusion(f32[32,32,1024]{2,1,0:T(8,128)S(1)} %get-tuple-element.31, f32[1024]{0:T(1024)S(1)} %bitcast.98), kind=kLoop, calls=%fused_computation.16 | loop fusion | flops 1048576 | bytes 8392704 | tf_op jit(solution)/shard_map/mul | solution.py:199
  129.4 9.6 %all-to-all-done.1 = f32[64,1,136]{2,1,0:T(1,128)S(1)} async-done(((f32[64,1,136]{2,1,0:T(1,128)}), f32[64,1,136]{2,1,0:T(1,128)S(1)}, u32[]{:S(2)}, u32[]{:S(2)}) %all-to-all-start.1) | async-done | bytes 34848 | tf_op jit(solution)/shard_map/all_to_all | solution.py:321
  140.6 4.4 %convolution_divide_fusion = f32[8,1024]{1,0:T(8,128)S(1)} fusion(f32[8,1024]{1,0:T(8,128)S(1)} %reshape.440, f32[1024,1024]{1,0:T(8,128)} %bitcast.84, f32[1024]{0:T(1024)S(1)} %multiply_add_fusion), kind=kOutput, calls=%fused_computation.30 | convolution fusion | flops 100671488 | bytes 4263936 | tf_op jit(solution)/shard_map/dot_general | solution.py:206
  145.1 4.2 %multiply_reduce_fusion = (f32[]{:T(128)}, f32[8,1024]{1,0:T(8,128)S(1)}) fusion(f32[8,1024]{1,0:T(8,128)S(1)} %convolution_divide_fusion, f32[1024,1024]{1,0:T(8,128)S(1)} %copy-done), kind=kOutput, calls=%fused_computation.101 | convolution fusion | flops 100679680 | bytes 4259844 | tf_op jit(solution)/shard_map/dot_general | solution.py:210
  151.0 8.0 %all-to-all-start.2 = ((f32[64,1,136]{2,1,0:T(1,128)}), f32[64,1,136]{2,1,0:T(1,128)S(1)}, u32[]{:S(2)}, u32[]{:S(2)}) async-start(f32[64,1,136]{2,1,0:T(1,128)} %reshape.454), calls=%async_computation.2 | async-start | bytes 131072 | tf_op jit(solution)/shard_map/all_to_all | solution.py:331
  159.8 15.1 %all-to-all-done.2 = f32[64,1,136]{2,1,0:T(1,128)S(1)} async-done(((f32[64,1,136]{2,1,0:T(1,128)}), f32[64,1,136]{2,1,0:T(1,128)S(1)}, u32[]{:S(2)}, u32[]{:S(2)}) %all-to-all-start.2) | async-done | bytes 34848 | tf_op jit(solution)/shard_map/all_to_all | solution.py:331
  178.0 28.1 %psum.7 = f32[2]{0:T(128)S(1)} all-reduce(f32[2]{0:T(128)S(1)} %pad_maximum_fusion.1), channel_id=1, replica_groups=mesh['wide'=64,'narrow'=8] {'narrow'}, use_global_device_ids=true, to_apply=%region_8.9 | all-reduce | flops 2 | bytes 16 | tf_op jit(solution)/shard_map/psum | solution.py:334
  (97 shorter events, 31.1 us)
Async XLA Ops:
  4.2 1.2 copy-start.4
  7.0 24.0 %copy-start.1 = (f32[2,20,16,512]{3,2,1,0:T(8,128)S(1)}, f32[2,20,16,512]{3,2,1,0:T(8,128)}, u32[]{:S(2)}) copy-start(f32[2,20,16,512]{3,2,1,0:T(8,128)} %adjoint_ref.1) | copy-start | bytes 3932164
  7.0 36.7 %slice-start = ((f32[2,20,16,512]{3,2,1,0:T(8,128)}), f32[2,1,16,512]{3,2,1,0:T(8,128)S(1)}, s32[]{:S(2)}) async-start(f32[2,20,16,512]{3,2,1,0:T(8,128)} %param.11), calls=%async_computation.3 | async-start | bytes 131072 | tf_op jit(solution)/shard_map/slice | solution.py:296
  7.0 36.8 %copy-start.5 = (s32[16,512]{1,0:T(8,128)S(1)}, s32[16,512]{1,0:T(8,128)}, u32[]{:S(2)}) copy-start(s32[16,512]{1,0:T(8,128)} %param.15) | copy-start | bytes 98308
  9.7 39.0 %all-to-all-start = ((f32[4,64,128]{2,0,1:T(4,128)}), f32[4,64,128]{2,0,1:T(4,128)S(1)}, u32[]{:S(2)}, u32[]{:S(2)}) async-start(f32[4,64,128]{2,0,1:T(4,128)} %copy.22), calls=%async_computation | async-start | bytes 262144 | tf_op jit(solution)/shard_map/all_to_all | solution.py:289
  31.1 26.3 %collective-permute-start = (f32[2,20,1,512]{3,2,1,0:T(1,128)S(1)}, f32[2,20,1,512]{3,2,1,0:T(1,128)S(1)}, u32[]{:S(2)}, u32[]{:S(2)}) collective-permute-start(f32[2,20,1,512]{3,2,1,0:T(1,128)S(1)} %get-tuple-element.27), channel_id=1, source_target_pairs={{0,8},{8,16},{16,24},{24,32},{32,40},{40,48},{48,56},{56,64},{64,7... | collective-permute-start | bytes 245768 | tf_op jit(solution)/shard_map/ppermute | solution.py:157
  33.2 24.3 %collective-permute-start.1 = (f32[2,20,1,512]{3,2,1,0:T(1,128)S(1)}, f32[2,20,1,512]{3,2,1,0:T(1,128)S(1)}, u32[]{:S(2)}, u32[]{:S(2)}) collective-permute-start(f32[2,20,1,512]{3,2,1,0:T(1,128)S(1)} %get-tuple-element.26), channel_id=1, source_target_pairs={{8,0},{16,8},{24,16},{32,24},{40,32},{48,40},{56,48},{64,56},{72,6... | collective-permute-start | bytes 245768 | tf_op jit(solution)/shard_map/ppermute | solution.py:157
  39.2 5.2 %collective-permute-start.2 = (f32[2,320]{1,0:T(2,128)S(1)}, f32[2,320]{1,0:T(2,128)S(1)}, u32[]{:S(2)}, u32[]{:S(2)}) collective-permute-start(f32[2,320]{1,0:T(2,128)S(1)} %reshape.432), channel_id=1, source_target_pairs={{0,1},{1,2},{2,3},{3,4},{4,5},{5,6},{6,7},{8,9},{9,10},{10,11},{11... | collective-permute-start | bytes 7688 | tf_op jit(solution)/shard_map/ppermute | solution.py:154
  42.2 5.5 %collective-permute-start.3 = (f32[2,320]{1,0:T(2,128)S(1)}, f32[2,320]{1,0:T(2,128)S(1)}, u32[]{:S(2)}, u32[]{:S(2)}) collective-permute-start(f32[2,320]{1,0:T(2,128)S(1)} %reshape.434), channel_id=1, source_target_pairs={{1,0},{2,1},{3,2},{4,3},{5,4},{6,5},{7,6},{9,8},{10,9},{11,10},{12... | collective-permute-start | bytes 7688 | tf_op jit(solution)/shard_map/ppermute | solution.py:154
  57.5 0.6 copy-start.6
  57.5 0.7 copy-start.7
  58.1 31.1 %copy-start.3 = (f32[2,20,16,512]{3,2,1,0:T(8,128)S(1)}, f32[2,20,16,512]{3,2,1,0:T(8,128)}, u32[]{:S(2)}) copy-start(f32[2,20,16,512]{3,2,1,0:T(8,128)} %param.11) | copy-start | bytes 3932164
  58.1 31.9 %copy-start.2 = (f32[16,512]{1,0:T(8,128)S(1)}, f32[16,512]{1,0:T(8,128)}, u32[]{:S(2)}) copy-start(f32[16,512]{1,0:T(8,128)} %friction_ref.3) | copy-start | bytes 98308
  62.6 21.8 %collective-permute-start.4 = (f32[2,20,1,512]{3,2,1,0:T(1,128)}, f32[2,20,1,512]{3,2,1,0:T(1,128)S(1)}, u32[]{:S(2)}, u32[]{:S(2)}) collective-permute-start(f32[2,20,1,512]{3,2,1,0:T(1,128)} %get-tuple-element.10), channel_id=1, source_target_pairs={{0,8},{8,16},{16,24},{24,32},{32,40},{40,48},{48,56},{56,64},{64,7... | collective-permute-start | bytes 245768 | tf_op jit(solution)/shard_map/ppermute | solution.py:157
  64.5 19.9 %collective-permute-start.5 = (f32[2,20,1,512]{3,2,1,0:T(1,128)}, f32[2,20,1,512]{3,2,1,0:T(1,128)S(1)}, u32[]{:S(2)}, u32[]{:S(2)}) collective-permute-start(f32[2,20,1,512]{3,2,1,0:T(1,128)} %get-tuple-element.11), channel_id=1, source_target_pairs={{8,0},{16,8},{24,16},{32,24},{40,32},{48,40},{56,48},{64,56},{72,6... | collective-permute-start | bytes 245768 | tf_op jit(solution)/shard_map/ppermute | solution.py:157
  71.5 8.4 %collective-permute-start.6 = (f32[2,320]{1,0:T(2,128)S(1)}, f32[2,320]{1,0:T(2,128)S(1)}, u32[]{:S(2)}, u32[]{:S(2)}) collective-permute-start(f32[2,320]{1,0:T(2,128)S(1)} %reshape.436), channel_id=1, source_target_pairs={{0,1},{1,2},{2,3},{3,4},{4,5},{5,6},{6,7},{8,9},{9,10},{10,11},{11... | collective-permute-start | bytes 7688 | tf_op jit(solution)/shard_map/ppermute | solution.py:154
  78.0 5.5 %collective-permute-start.7 = (f32[2,320]{1,0:T(2,128)S(1)}, f32[2,320]{1,0:T(2,128)S(1)}, u32[]{:S(2)}, u32[]{:S(2)}) collective-permute-start(f32[2,320]{1,0:T(2,128)S(1)} %reshape.438), channel_id=1, source_target_pairs={{1,0},{2,1},{3,2},{4,3},{5,4},{6,5},{7,6},{9,8},{10,9},{11,10},{12... | collective-permute-start | bytes 7688 | tf_op jit(solution)/shard_map/ppermute | solution.py:154
  84.4 0.6 copy-start.8
  84.4 0.6 copy-start.9
  91.1 47.9 %all-to-all-start.1 = ((f32[64,1,136]{2,1,0:T(1,128)}), f32[64,1,136]{2,1,0:T(1,128)S(1)}, u32[]{:S(2)}, u32[]{:S(2)}) async-start(f32[64,1,136]{2,1,0:T(1,128)} %reshape.452), calls=%async_computation.1 | async-start | bytes 131072 | tf_op jit(solution)/shard_map/all_to_all | solution.py:321
  140.6 4.4 %copy-start = (f32[1024,1024]{1,0:T(8,128)S(1)}, f32[1024,1024]{1,0:T(8,128)}, u32[]{:S(2)}) copy-start(f32[1024,1024]{1,0:T(8,128)} %bitcast_multiply_fusion) | copy-start | bytes 12582916
  151.0 23.9 %all-to-all-start.2 = ((f32[64,1,136]{2,1,0:T(1,128)}), f32[64,1,136]{2,1,0:T(1,128)S(1)}, u32[]{:S(2)}, u32[]{:S(2)}) async-start(f32[64,1,136]{2,1,0:T(1,128)} %reshape.454), calls=%async_computation.2 | async-start | bytes 131072 | tf_op jit(solution)/shard_map/all_to_all | solution.py:331

commit v7 on v5

--- a/solution.py
+++ b/solution.py
@@ -327,10 +327,11 @@
     back = lax.all_to_all(returned, "wide", split_axis=1, concat_axis=0, tiled=True)
     wide_square = jnp.sum(back[::width, rows_x])
     back = back[:, :rows_x].T
-    totals = lax.psum(jnp.stack([wide_square, wide_misfit]), "narrow")
+    back, wide_square = lax.optimization_barrier((back, wide_square))
+    square_total, misfit_total = lax.psum((wide_square, wide_misfit), "narrow")
     cell_total = wide_count * rows_x * rows_y * lax.axis_size("narrow")
-    direction = back * lax.rsqrt(totals[0] / cell_total + 1e-06)
-    return (adjoint, direction, totals[1])
+    direction = back * lax.rsqrt(square_total / cell_total + 1e-06)
+    return (adjoint, direction, misfit_total)
 
 
 def solution(mesh):

time: 206 us -> 205 us (level)
  transfers between devices with their start and end apart: 11 -> 11, of which waited for: 5 -> 5; matrix products, arithmetic and copies ran while one was open for 12% -> 13% of each run, Pallas kernels for 0% -> 0%
where the time goes in v7:
time: 205 us; the launch traced here: 203 us
  starting transfers between devices  78.4 us (38%)
  waiting for transfers between devices  41.6 us (20%)
  blocking collectives  26.5 us (13%)
  other arithmetic  17.7 us (9%)
  matrix products  17.4 us (8%)
  local copies, waits for them, and re-layouts  10.5 us (5%)
  Pallas kernels  8.52 us (4%)
  between operations  2.49 us (1%)
    all_to_all x1, starting transfers between devices, on_device(): lax.all_to_all(packed, 'wide', split_axis=1, concat_axis=1, tiled=True)  27 us
    psum x1, blocking collectives, on_device(): square_total, misfit_total = lax.psum((wide_square, wide_misfit), 'narrow')  26.5 us
    all_to_all x1, starting transfers between devices, on_device(): lax.all_to_all(sent, 'wide', split_axis=0, concat_axis=1, tiled=True)  14.6 us
    all_to_all x1, waiting for transfers between devices, on_device(): lax.all_to_all(returned, 'wide', split_axis=1, concat_axis=0, tiled=True)  14.5 us
    ppermute x4, starting transfers between devices, halo_edges(): edges.append(lax.ppermute(block[2 * index + 1], axis, down))  14.3 us
    ppermute x4, starting transfers between devices, halo_edges(): edges.append(lax.ppermute(block[2 * index], axis, up))  14 us
    all_to_all x1, waiting for transfers between devices, on_device(): lax.all_to_all(packed, 'wide', split_axis=1, concat_axis=1, tiled=True)  10.8 us
    all_to_all x1, waiting for transfers between devices, on_device(): lax.all_to_all(sent, 'wide', split_axis=0, concat_axis=1, tiled=True)  9.03 us
  transfers between devices with their start and end apart: 11, of which 5 were waited for; matrix products, arithmetic and copies ran while one was open for 13% of the time, Pallas kernels for 0%

profile of v7, /device:TPU:6, one launch (start us, length us, event | category | flops | bytes accessed | tf_op | source)
XLA Modules:
  0.0 203.1 jit_solution(10204023374477062566)
XLA Ops:
  0.6 2.1 %fusion.50 = (f32[2,20,1,512]{3,2,1,0:T(1,128)}, f32[2,20,1,512]{3,2,1,0:T(1,128)}) fusion(f32[2,20,16,512]{3,2,1,0:T(8,128)} %adjoint_ref.1), kind=kLoop, calls=%fused_computation.118 | loop fusion | bytes 327680 | tf_op jit(solution)/shard_map/slice | solution.py:142
  2.7 1.9 collective-permute-start
  4.6 5.8 %collective-permute-start.1 = (f32[2,20,1,512]{3,2,1,0:T(1,128)}, f32[2,20,1,512]{3,2,1,0:T(1,128)}, u32[]{:S(2)}, u32[]{:S(2)}) collective-permute-start(f32[2,20,1,512]{3,2,1,0:T(1,128)} %get-tuple-element.32), channel_id=1, source_target_pairs={{8,0},{16,8},{24,16},{32,24},{40,32},{48,40},{56,48},{64,56},{72,6... | collective-permute-start | bytes 245768 | tf_op jit(solution)/shard_map/ppermute | solution.py:153
  19.5 27.0 %all-to-all-start = ((f32[4,64,128]{2,0,1:T(4,128)}), f32[4,64,128]{2,0,1:T(4,128)S(1)}, u32[]{:S(2)}, u32[]{:S(2)}) async-start(f32[4,64,128]{2,0,1:T(4,128)} %copy.18), calls=%async_computation | async-start | bytes 262144 | tf_op jit(solution)/shard_map/all_to_all | solution.py:285
  46.7 2.9 %collective-permute-start.2 = (f32[2,20,16,1]{3,2,1,0:T(8,128)S(1)}, f32[2,20,16,1]{3,2,1,0:T(8,128)S(1)}, u32[]{:S(2)}, u32[]{:S(2)}) collective-permute-start(f32[2,20,16,1]{3,2,1,0:T(8,128)S(1)} %get-tuple-element.31), channel_id=1, source_target_pairs={{0,1},{1,2},{2,3},{3,4},{4,5},{5,6},{6,7},{8,9},{9,10},{10,11},{11... | collective-permute-start | bytes 7688 | tf_op jit(solution)/shard_map/ppermute | solution.py:152
  51.8 10.8 %all-to-all-done = f32[4,64,128]{2,0,1:T(4,128)S(1)} async-done(((f32[4,64,128]{2,0,1:T(4,128)}), f32[4,64,128]{2,0,1:T(4,128)S(1)}, u32[]{:S(2)}, u32[]{:S(2)}) %all-to-all-start) | async-done | bytes 131104 | tf_op jit(solution)/shard_map/all_to_all | solution.py:285
  62.8 3.2 %fusion.1 = f32[96,8192]{1,0:T(8,128)S(1)} fusion(s32[8192]{0:T(1024)S(1)} %get-tuple-element.45, bf16[32,512]{1,0:T(8,128)(2,1)S(1)} %get-tuple-element.42, bf16[32,512]{1,0:T(8,128)(2,1)S(1)} %get-tuple-element.43, bf16[32,512]{1,0:T(8,128)(2,1)S(1)} %get-tuple-element.41), kind=kOutput, calls=%fused_computation.2 | convolution fusion | flops 809795584 | bytes 3276800 | tf_op jit(solution)/shard_map/dot_general | solution.py:225
  67.5 3.2 %fusion = f32[96,512]{1,0:T(8,128)S(1)} fusion(s32[8192]{0:T(1024)S(1)} %get-tuple-element.45, bf16[32,8192]{1,0:T(8,128)(2,1)S(1)} %get-tuple-element.35, bf16[32,8192]{1,0:T(8,128)(2,1)S(1)} %get-tuple-element.36, bf16[32,8192]{1,0:T(8,128)(2,1)S(1)} %get-tuple-element.34), kind=kOutput, calls=%fused_computation.1 | convolution fusion | flops 814219264 | bytes 1802240 | tf_op jit(solution)/shard_map/dot_general | solution.py:225
  72.2 4.4 %shard_map.121 = (f32[2,20,16,512]{3,2,1,0:T(8,128)}, f32[2,20,1,512]{3,2,1,0:T(1,128)}, f32[2,20,1,512]{3,2,1,0:T(1,128)}, f32[2,20,16,1]{3,2,1,0:T(8,128)}, f32[2,20,16,1]{3,2,1,0:T(8,128)}) custom-call(f32[2,20,16,512]{3,2,1,0:T(8,128)} %adjoint_ref.1, f32[2,20,1,512]{3,2,1,0:T(1,128)} %copy-done.10, f32[2,20,1,512]{3,2,1,0:T(1,128)} %collective-permute-done.1.x_next_ref, ...), custom_call_target="tpu_custom_call" | custom-call | flops 6553600 | bytes 3407872 | tf_op jit(solution)/shard_map/pallas_call | solution.py:165
  76.6 1.9 collective-permute-start.4
  78.5 5.8 %collective-permute-start.5 = (f32[2,20,1,512]{3,2,1,0:T(1,128)}, f32[2,20,1,512]{3,2,1,0:T(1,128)S(1)}, u32[]{:S(2)}, u32[]{:S(2)}) collective-permute-start(f32[2,20,1,512]{3,2,1,0:T(1,128)} %get-tuple-element.13), channel_id=1, source_target_pairs={{8,0},{16,8},{24,16},{32,24},{40,32},{48,40},{56,48},{64,56},{72,6... | collective-permute-start | bytes 245768 | tf_op jit(solution)/shard_map/ppermute | solution.py:153
  84.3 7.2 %collective-permute-start.6 = (f32[2,20,16,1]{3,2,1,0:T(8,128)}, f32[2,20,16,1]{3,2,1,0:T(8,128)S(1)}, u32[]{:S(2)}, u32[]{:S(2)}) collective-permute-start(f32[2,20,16,1]{3,2,1,0:T(8,128)} %get-tuple-element.14), channel_id=1, source_target_pairs={{0,1},{1,2},{2,3},{3,4},{4,5},{5,6},{6,7},{8,9},{9,10},{10,11},{11... | collective-permute-start | bytes 7688 | tf_op jit(solution)/shard_map/ppermute | solution.py:152
  93.5 2.9 %collective-permute-done.6.y_prev_ref = f32[2,20,16,1]{3,2,1,0:T(8,128)S(1)} collective-permute-done((f32[2,20,16,1]{3,2,1,0:T(8,128)}, f32[2,20,16,1]{3,2,1,0:T(8,128)S(1)}, u32[]{:S(2)}, u32[]{:S(2)}) %collective-permute-start.6) | collective-permute-done | bytes 2592 | tf_op jit(solution)/shard_map/ppermute | solution.py:152
  96.4 4.3 %collective-permute-done.7.y_next_ref = f32[2,20,16,1]{3,2,1,0:T(8,128)S(1)} collective-permute-done((f32[2,20,16,1]{3,2,1,0:T(8,128)}, f32[2,20,16,1]{3,2,1,0:T(8,128)S(1)}, u32[]{:S(2)}, u32[]{:S(2)}) %collective-permute-start.7) | collective-permute-done | bytes 2592 | tf_op jit(solution)/shard_map/ppermute | solution.py:153
  101.5 4.1 %shard_map.122 = f32[2,20,16,512]{3,2,1,0:T(8,128)} custom-call(f32[2,20,16,512]{3,2,1,0:T(8,128)} %get-tuple-element.11.adjoint_ref, f32[2,20,1,512]{3,2,1,0:T(1,128)} %copy-done.11, f32[2,20,1,512]{3,2,1,0:T(1,128)} %copy-done.12, f32[2,20,16,1]{3,2,1,0:T(8,128)} %copy-done.2, f32[2,20,16,1]{3,2,1,0:T(8,128)} %copy-done.3, f32[19,16,512]{2,1,0:T(8,128)} %coupling_ref.3, ...), custom_call_target="tpu_custom_call" | custom-call | flops 6553600 | bytes 3407872 | tf_op jit(solution)/shard_map/pallas_call | solution.py:165
  107.5 14.6 %all-to-all-start.1 = ((f32[64,1,136]{2,1,0:T(1,128)}), f32[64,1,136]{2,1,0:T(1,128)S(1)}, u32[]{:S(2)}, u32[]{:S(2)}) async-start(f32[64,1,136]{2,1,0:T(1,128)} %reshape.407), calls=%async_computation.1 | async-start | bytes 131072 | tf_op jit(solution)/shard_map/all_to_all | solution.py:317
  123.2 2.7 %multiply_subtract_fusion = (f32[32,32,1024]{2,1,0:T(8,128)S(1)}, f32[32,32,1024]{2,1,0:T(8,128)}) fusion(f32[32,1024]{1,0:T(8,128)S(1)} %get-tuple-element.52, f32[32,1024]{1,0:T(8,128)S(1)} %get-tuple-element.49, f32[32,1024]{1,0:T(8,128)S(1)} %get-tuple-element.53, f32[32,1024]{1,0:T(8,128)S(1)} %get-tuple-element.48, f32[1024]{0:T(1024)S(1)} %bitcast.93), kind=kLoop, calls=%fused_computation.17 | loop fusion | flops 4194304 | bytes 8916992 | tf_op jit(solution)/shard_map/sub | solution.py:191
  125.8 2.5 %bitcast_multiply_fusion = f32[1024,1024]{1,0:T(8,128)} fusion(f32[32,32,1024]{2,1,0:T(8,128)S(1)} %get-tuple-element.37, f32[1024]{0:T(1024)S(1)} %bitcast.94), kind=kLoop, calls=%fused_computation.16 | loop fusion | flops 1048576 | bytes 8392704 | tf_op jit(solution)/shard_map/mul | solution.py:195
  128.3 9.0 %all-to-all-done.1 = f32[64,1,136]{2,1,0:T(1,128)S(1)} async-done(((f32[64,1,136]{2,1,0:T(1,128)}), f32[64,1,136]{2,1,0:T(1,128)S(1)}, u32[]{:S(2)}, u32[]{:S(2)}) %all-to-all-start.1) | async-done | bytes 34848 | tf_op jit(solution)/shard_map/all_to_all | solution.py:317
  139.0 4.4 %convolution_divide_fusion = f32[8,1024]{1,0:T(8,128)S(1)} fusion(f32[8,1024]{1,0:T(8,128)S(1)} %reshape.403, f32[1024,1024]{1,0:T(8,128)} %bitcast.80, f32[1024]{0:T(1024)S(1)} %multiply_add_fusion), kind=kOutput, calls=%fused_computation.30 | convolution fusion | flops 100671488 | bytes 4263936 | tf_op jit(solution)/shard_map/dot_general | solution.py:202
  143.5 4.2 %multiply_reduce_fusion = (f32[]{:T(128)}, f32[8,1024]{1,0:T(8,128)S(1)}) fusion(f32[8,1024]{1,0:T(8,128)S(1)} %convolution_divide_fusion, f32[1024,1024]{1,0:T(8,128)S(1)} %copy-done), kind=kOutput, calls=%fused_computation.99 | convolution fusion | flops 100679680 | bytes 4259844 | tf_op jit(solution)/shard_map/dot_general | solution.py:206
  149.4 8.6 %all-to-all-start.2 = ((f32[64,1,136]{2,1,0:T(1,128)}), f32[64,1,136]{2,1,0:T(1,128)S(1)}, u32[]{:S(2)}, u32[]{:S(2)}) async-start(f32[64,1,136]{2,1,0:T(1,128)} %reshape.409), calls=%async_computation.2 | async-start | bytes 131072 | tf_op jit(solution)/shard_map/all_to_all | solution.py:327
  158.8 14.5 %all-to-all-done.2 = f32[64,1,136]{2,1,0:T(1,128)S(1)} async-done(((f32[64,1,136]{2,1,0:T(1,128)}), f32[64,1,136]{2,1,0:T(1,128)S(1)}, u32[]{:S(2)}, u32[]{:S(2)}) %all-to-all-start.2) | async-done | bytes 34848 | tf_op jit(solution)/shard_map/all_to_all | solution.py:327
  175.1 26.5 %all-reduce.2 = (f32[]{:T(128)}, f32[]{:T(128)}) all-reduce(f32[]{:T(128)} %reduce_sum.84, f32[]{:T(128)} %slice_reduce_fusion.1), channel_id=1, replica_groups=mesh['wide'=64,'narrow'=8] {'narrow'}, use_global_device_ids=true, to_apply=%region_7.8 | all-reduce | flops 2 | bytes 16 | tf_op jit(solution)/shard_map/psum | solution.py:331
  (92 shorter events, 26.0 us)
Async XLA Ops:
  2.7 68.7 %collective-permute-start = (f32[2,20,1,512]{3,2,1,0:T(1,128)}, f32[2,20,1,512]{3,2,1,0:T(1,128)S(1)}, u32[]{:S(2)}, u32[]{:S(2)}) collective-permute-start(f32[2,20,1,512]{3,2,1,0:T(1,128)} %get-tuple-element.33), channel_id=1, source_target_pairs={{0,8},{8,16},{16,24},{24,32},{32,40},{40,48},{48,56},{56,64},{64,7... | collective-permute-start | bytes 245768 | tf_op jit(solution)/shard_map/ppermute | solution.py:152
  4.6 66.8 %collective-permute-start.1 = (f32[2,20,1,512]{3,2,1,0:T(1,128)}, f32[2,20,1,512]{3,2,1,0:T(1,128)}, u32[]{:S(2)}, u32[]{:S(2)}) collective-permute-start(f32[2,20,1,512]{3,2,1,0:T(1,128)} %get-tuple-element.32), channel_id=1, source_target_pairs={{8,0},{16,8},{24,16},{32,24},{40,32},{48,40},{56,48},{64,56},{72,6... | collective-permute-start | bytes 245768 | tf_op jit(solution)/shard_map/ppermute | solution.py:153
  14.0 1.2 copy-start.8
  16.8 29.7 %copy-start.1 = (f32[2,20,16,512]{3,2,1,0:T(8,128)S(1)}, f32[2,20,16,512]{3,2,1,0:T(8,128)}, u32[]{:S(2)}) copy-start(f32[2,20,16,512]{3,2,1,0:T(8,128)} %adjoint_ref.1) | copy-start | bytes 3932164
  16.8 34.3 %copy-start.9 = (s32[16,512]{1,0:T(8,128)S(1)}, s32[16,512]{1,0:T(8,128)}, u32[]{:S(2)}) copy-start(s32[16,512]{1,0:T(8,128)} %param.15) | copy-start | bytes 98308
  16.8 35.0 %slice-start = ((f32[2,20,16,512]{3,2,1,0:T(8,128)}), f32[2,1,16,512]{3,2,1,0:T(8,128)S(1)}, s32[]{:S(2)}) async-start(f32[2,20,16,512]{3,2,1,0:T(8,128)} %param.11), calls=%async_computation.3 | async-start | bytes 131072 | tf_op jit(solution)/shard_map/slice | solution.py:292
  19.5 43.1 %all-to-all-start = ((f32[4,64,128]{2,0,1:T(4,128)}), f32[4,64,128]{2,0,1:T(4,128)S(1)}, u32[]{:S(2)}, u32[]{:S(2)}) async-start(f32[4,64,128]{2,0,1:T(4,128)} %copy.18), calls=%async_computation | async-start | bytes 262144 | tf_op jit(solution)/shard_map/all_to_all | solution.py:285
  46.7 24.7 %collective-permute-start.2 = (f32[2,20,16,1]{3,2,1,0:T(8,128)S(1)}, f32[2,20,16,1]{3,2,1,0:T(8,128)S(1)}, u32[]{:S(2)}, u32[]{:S(2)}) collective-permute-start(f32[2,20,16,1]{3,2,1,0:T(8,128)S(1)} %get-tuple-element.31), channel_id=1, source_target_pairs={{0,1},{1,2},{2,3},{3,4},{4,5},{5,6},{6,7},{8,9},{9,10},{10,11},{11... | collective-permute-start | bytes 7688 | tf_op jit(solution)/shard_map/ppermute | solution.py:152
  49.6 21.8 %collective-permute-start.3 = (f32[2,20,16,1]{3,2,1,0:T(8,128)S(1)}, f32[2,20,16,1]{3,2,1,0:T(8,128)S(1)}, u32[]{:S(2)}, u32[]{:S(2)}) collective-permute-start(f32[2,20,16,1]{3,2,1,0:T(8,128)S(1)} %get-tuple-element.30), channel_id=1, source_target_pairs={{1,0},{2,1},{3,2},{4,3},{5,4},{6,5},{7,6},{9,8},{10,9},{11,10},{12... | collective-permute-start | bytes 7688 | tf_op jit(solution)/shard_map/ppermute | solution.py:153
  70.7 34.9 %copy-start.7 = (f32[2,20,16,512]{3,2,1,0:T(8,128)S(1)}, f32[2,20,16,512]{3,2,1,0:T(8,128)}, u32[]{:S(2)}) copy-start(f32[2,20,16,512]{3,2,1,0:T(8,128)} %param.11) | copy-start | bytes 3932164
  70.7 35.7 %copy-start.6 = (f32[16,512]{1,0:T(8,128)S(1)}, f32[16,512]{1,0:T(8,128)}, u32[]{:S(2)}) copy-start(f32[16,512]{1,0:T(8,128)} %friction_ref.3) | copy-start | bytes 98308
  71.4 0.8 copy-start.5
  71.4 0.8 copy-start.10
  76.6 24.1 %collective-permute-start.4 = (f32[2,20,1,512]{3,2,1,0:T(1,128)}, f32[2,20,1,512]{3,2,1,0:T(1,128)S(1)}, u32[]{:S(2)}, u32[]{:S(2)}) collective-permute-start(f32[2,20,1,512]{3,2,1,0:T(1,128)} %get-tuple-element.12), channel_id=1, source_target_pairs={{0,8},{8,16},{16,24},{24,32},{32,40},{40,48},{48,56},{56,64},{64,7... | collective-permute-start | bytes 245768 | tf_op jit(solution)/shard_map/ppermute | solution.py:152
  78.5 22.2 %collective-permute-start.5 = (f32[2,20,1,512]{3,2,1,0:T(1,128)}, f32[2,20,1,512]{3,2,1,0:T(1,128)S(1)}, u32[]{:S(2)}, u32[]{:S(2)}) collective-permute-start(f32[2,20,1,512]{3,2,1,0:T(1,128)} %get-tuple-element.13), channel_id=1, source_target_pairs={{8,0},{16,8},{24,16},{32,24},{40,32},{48,40},{56,48},{64,56},{72,6... | collective-permute-start | bytes 245768 | tf_op jit(solution)/shard_map/ppermute | solution.py:153
  84.3 12.1 %collective-permute-start.6 = (f32[2,20,16,1]{3,2,1,0:T(8,128)}, f32[2,20,16,1]{3,2,1,0:T(8,128)S(1)}, u32[]{:S(2)}, u32[]{:S(2)}) collective-permute-start(f32[2,20,16,1]{3,2,1,0:T(8,128)} %get-tuple-element.14), channel_id=1, source_target_pairs={{0,1},{1,2},{2,3},{3,4},{4,5},{5,6},{6,7},{8,9},{9,10},{10,11},{11... | collective-permute-start | bytes 7688 | tf_op jit(solution)/shard_map/ppermute | solution.py:152
  91.5 9.2 %collective-permute-start.7 = (f32[2,20,16,1]{3,2,1,0:T(8,128)}, f32[2,20,16,1]{3,2,1,0:T(8,128)S(1)}, u32[]{:S(2)}, u32[]{:S(2)}) collective-permute-start(f32[2,20,16,1]{3,2,1,0:T(8,128)} %get-tuple-element.15), channel_id=1, source_target_pairs={{1,0},{2,1},{3,2},{4,3},{5,4},{6,5},{7,6},{9,8},{10,9},{11,10},{12... | collective-permute-start | bytes 7688 | tf_op jit(solution)/shard_map/ppermute | solution.py:153
  96.4 4.3 %copy-start.2 = (f32[2,20,16,1]{3,2,1,0:T(8,128)}, f32[2,20,16,1]{3,2,1,0:T(8,128)S(1)}, u32[]{:S(2)}) copy-start(f32[2,20,16,1]{3,2,1,0:T(8,128)S(1)} %collective-permute-done.6.y_prev_ref) | copy-start | bytes 7684
  100.7 0.7 copy-start.3
  100.7 0.7 copy-start.11
  100.7 0.8 copy-start.12
  107.5 29.9 %all-to-all-start.1 = ((f32[64,1,136]{2,1,0:T(1,128)}), f32[64,1,136]{2,1,0:T(1,128)S(1)}, u32[]{:S(2)}, u32[]{:S(2)}) async-start(f32[64,1,136]{2,1,0:T(1,128)} %reshape.407), calls=%async_computation.1 | async-start | bytes 131072 | tf_op jit(solution)/shard_map/all_to_all | solution.py:317
  139.0 4.4 %copy-start = (f32[1024,1024]{1,0:T(8,128)S(1)}, f32[1024,1024]{1,0:T(8,128)}, u32[]{:S(2)}) copy-start(f32[1024,1024]{1,0:T(8,128)} %bitcast_multiply_fusion) | copy-start | bytes 12582916
  149.4 23.9 %all-to-all-start.2 = ((f32[64,1,136]{2,1,0:T(1,128)}), f32[64,1,136]{2,1,0:T(1,128)S(1)}, u32[]{:S(2)}, u32[]{:S(2)}) async-start(f32[64,1,136]{2,1,0:T(1,128)} %reshape.409), calls=%async_computation.2 | async-start | bytes 131072 | tf_op jit(solution)/shard_map/all_to_all | solution.py:327
  (1 other events, 0.7 us)

commit v8 on v7

--- a/solution.py
+++ b/solution.py
@@ -200,14 +200,14 @@
     modes = lax.iota(jnp.int32, length).astype(jnp.float32)
     spectrum = 1.0 + kappa_val * (2.0 - 2.0 * jnp.cos(jnp.pi * modes / length))
     coefficients = jnp.dot(
-        lines, table, precision=lax.Precision.HIGHEST, preferred_element_type=jnp.float32
+        lines, table, precision=lax.Precision.HIGH, preferred_element_type=jnp.float32
     )
     coefficients = coefficients / spectrum[None, :]
     return lax.dot_general(
         coefficients,
         table,
         (((1,), (1,)), ((), ())),
-        precision=lax.Precision.HIGHEST,
+        precision=lax.Precision.HIGH,
         preferred_element_type=jnp.float32,
     )
 

time: 205 us -> 202 us (0.985)
  matrix products: 17.4 us -> 14.7 us
where the time goes in v8:
time: 202 us; the launch traced here: 200 us
  starting transfers between devices  78.4 us (39%)
  waiting for transfers between devices  41.6 us (21%)
  blocking collectives  26.5 us (13%)
  other arithmetic  17.7 us (9%)
  matrix products  14.7 us (7%)
  local copies, waits for them, and re-layouts  10.5 us (5%)
  Pallas kernels  8.52 us (4%)
  between operations  2.49 us (1%)
    all_to_all x1, starting transfers between devices, on_device(): lax.all_to_all(packed, 'wide', split_axis=1, concat_axis=1, tiled=True)  27 us
    psum x1, blocking collectives, on_device(): square_total, misfit_total = lax.psum((wide_square, wide_misfit), 'narrow')  26.5 us
    all_to_all x1, starting transfers between devices, on_device(): lax.all_to_all(sent, 'wide', split_axis=0, concat_axis=1, tiled=True)  14.6 us
    all_to_all x1, waiting for transfers between devices, on_device(): lax.all_to_all(returned, 'wide', split_axis=1, concat_axis=0, tiled=True)  14.5 us
    ppermute x4, starting transfers between devices, halo_edges(): edges.append(lax.ppermute(block[2 * index + 1], axis, down))  14.3 us
    ppermute x4, starting transfers between devices, halo_edges(): edges.append(lax.ppermute(block[2 * index], axis, up))  14 us
    all_to_all x1, waiting for transfers between devices, on_device(): lax.all_to_all(packed, 'wide', split_axis=1, concat_axis=1, tiled=True)  10.8 us
    all_to_all x1, waiting for transfers between devices, on_device(): lax.all_to_all(sent, 'wide', split_axis=0, concat_axis=1, tiled=True)  9.03 us
  transfers between devices with their start and end apart: 11, of which 5 were waited for; matrix products, arithmetic and copies ran while one was open for 13% of the time, Pallas kernels for 0%

profile of v8, /device:TPU:6, one launch (start us, length us, event | category | flops | bytes accessed | tf_op | source)
XLA Modules:
  0.0 200.4 jit_solution(185874288291571302)
XLA Ops:
  0.6 2.1 %fusion.50 = (f32[2,20,1,512]{3,2,1,0:T(1,128)}, f32[2,20,1,512]{3,2,1,0:T(1,128)}) fusion(f32[2,20,16,512]{3,2,1,0:T(8,128)} %adjoint_ref.1), kind=kLoop, calls=%fused_computation.118 | loop fusion | bytes 327680 | tf_op jit(solution)/shard_map/slice | solution.py:142
  2.7 1.9 collective-permute-start
  4.6 5.8 %collective-permute-start.1 = (f32[2,20,1,512]{3,2,1,0:T(1,128)}, f32[2,20,1,512]{3,2,1,0:T(1,128)}, u32[]{:S(2)}, u32[]{:S(2)}) collective-permute-start(f32[2,20,1,512]{3,2,1,0:T(1,128)} %get-tuple-element.32), channel_id=1, source_target_pairs={{8,0},{16,8},{24,16},{32,24},{40,32},{48,40},{56,48},{64,56},{72,6... | collective-permute-start | bytes 245768 | tf_op jit(solution)/shard_map/ppermute | solution.py:153
  19.5 27.0 %all-to-all-start = ((f32[4,64,128]{2,0,1:T(4,128)}), f32[4,64,128]{2,0,1:T(4,128)S(1)}, u32[]{:S(2)}, u32[]{:S(2)}) async-start(f32[4,64,128]{2,0,1:T(4,128)} %copy.18), calls=%async_computation | async-start | bytes 262144 | tf_op jit(solution)/shard_map/all_to_all | solution.py:285
  46.7 2.9 %collective-permute-start.2 = (f32[2,20,16,1]{3,2,1,0:T(8,128)S(1)}, f32[2,20,16,1]{3,2,1,0:T(8,128)S(1)}, u32[]{:S(2)}, u32[]{:S(2)}) collective-permute-start(f32[2,20,16,1]{3,2,1,0:T(8,128)S(1)} %get-tuple-element.31), channel_id=1, source_target_pairs={{0,1},{1,2},{2,3},{3,4},{4,5},{5,6},{6,7},{8,9},{9,10},{10,11},{11... | collective-permute-start | bytes 7688 | tf_op jit(solution)/shard_map/ppermute | solution.py:152
  51.8 10.8 %all-to-all-done = f32[4,64,128]{2,0,1:T(4,128)S(1)} async-done(((f32[4,64,128]{2,0,1:T(4,128)}), f32[4,64,128]{2,0,1:T(4,128)S(1)}, u32[]{:S(2)}, u32[]{:S(2)}) %all-to-all-start) | async-done | bytes 131104 | tf_op jit(solution)/shard_map/all_to_all | solution.py:285
  62.8 3.2 %fusion.1 = f32[96,8192]{1,0:T(8,128)S(1)} fusion(s32[8192]{0:T(1024)S(1)} %get-tuple-element.45, bf16[32,512]{1,0:T(8,128)(2,1)S(1)} %get-tuple-element.42, bf16[32,512]{1,0:T(8,128)(2,1)S(1)} %get-tuple-element.43, bf16[32,512]{1,0:T(8,128)(2,1)S(1)} %get-tuple-element.41), kind=kOutput, calls=%fused_computation.2 | convolution fusion | flops 809795584 | bytes 3276800 | tf_op jit(solution)/shard_map/dot_general | solution.py:225
  67.5 3.2 %fusion = f32[96,512]{1,0:T(8,128)S(1)} fusion(s32[8192]{0:T(1024)S(1)} %get-tuple-element.45, bf16[32,8192]{1,0:T(8,128)(2,1)S(1)} %get-tuple-element.35, bf16[32,8192]{1,0:T(8,128)(2,1)S(1)} %get-tuple-element.36, bf16[32,8192]{1,0:T(8,128)(2,1)S(1)} %get-tuple-element.34), kind=kOutput, calls=%fused_computation.1 | convolution fusion | flops 814219264 | bytes 1802240 | tf_op jit(solution)/shard_map/dot_general | solution.py:225
  72.2 4.4 %shard_map.121 = (f32[2,20,16,512]{3,2,1,0:T(8,128)}, f32[2,20,1,512]{3,2,1,0:T(1,128)}, f32[2,20,1,512]{3,2,1,0:T(1,128)}, f32[2,20,16,1]{3,2,1,0:T(8,128)}, f32[2,20,16,1]{3,2,1,0:T(8,128)}) custom-call(f32[2,20,16,512]{3,2,1,0:T(8,128)} %adjoint_ref.1, f32[2,20,1,512]{3,2,1,0:T(1,128)} %copy-done.10, f32[2,20,1,512]{3,2,1,0:T(1,128)} %collective-permute-done.1.x_next_ref, ...), custom_call_target="tpu_custom_call" | custom-call | flops 6553600 | bytes 3407872 | tf_op jit(solution)/shard_map/pallas_call | solution.py:165
  76.6 1.9 collective-permute-start.4
  78.5 5.8 %collective-permute-start.5 = (f32[2,20,1,512]{3,2,1,0:T(1,128)}, f32[2,20,1,512]{3,2,1,0:T(1,128)S(1)}, u32[]{:S(2)}, u32[]{:S(2)}) collective-permute-start(f32[2,20,1,512]{3,2,1,0:T(1,128)} %get-tuple-element.13), channel_id=1, source_target_pairs={{8,0},{16,8},{24,16},{32,24},{40,32},{48,40},{56,48},{64,56},{72,6... | collective-permute-start | bytes 245768 | tf_op jit(solution)/shard_map/ppermute | solution.py:153
  84.3 7.2 %collective-permute-start.6 = (f32[2,20,16,1]{3,2,1,0:T(8,128)}, f32[2,20,16,1]{3,2,1,0:T(8,128)S(1)}, u32[]{:S(2)}, u32[]{:S(2)}) collective-permute-start(f32[2,20,16,1]{3,2,1,0:T(8,128)} %get-tuple-element.14), channel_id=1, source_target_pairs={{0,1},{1,2},{2,3},{3,4},{4,5},{5,6},{6,7},{8,9},{9,10},{10,11},{11... | collective-permute-start | bytes 7688 | tf_op jit(solution)/shard_map/ppermute | solution.py:152
  93.5 2.9 %collective-permute-done.6.y_prev_ref = f32[2,20,16,1]{3,2,1,0:T(8,128)S(1)} collective-permute-done((f32[2,20,16,1]{3,2,1,0:T(8,128)}, f32[2,20,16,1]{3,2,1,0:T(8,128)S(1)}, u32[]{:S(2)}, u32[]{:S(2)}) %collective-permute-start.6) | collective-permute-done | bytes 2592 | tf_op jit(solution)/shard_map/ppermute | solution.py:152
  96.4 4.3 %collective-permute-done.7.y_next_ref = f32[2,20,16,1]{3,2,1,0:T(8,128)S(1)} collective-permute-done((f32[2,20,16,1]{3,2,1,0:T(8,128)}, f32[2,20,16,1]{3,2,1,0:T(8,128)S(1)}, u32[]{:S(2)}, u32[]{:S(2)}) %collective-permute-start.7) | collective-permute-done | bytes 2592 | tf_op jit(solution)/shard_map/ppermute | solution.py:153
  101.5 4.1 %shard_map.122 = f32[2,20,16,512]{3,2,1,0:T(8,128)} custom-call(f32[2,20,16,512]{3,2,1,0:T(8,128)} %get-tuple-element.11.adjoint_ref, f32[2,20,1,512]{3,2,1,0:T(1,128)} %copy-done.11, f32[2,20,1,512]{3,2,1,0:T(1,128)} %copy-done.12, f32[2,20,16,1]{3,2,1,0:T(8,128)} %copy-done.2, f32[2,20,16,1]{3,2,1,0:T(8,128)} %copy-done.3, f32[19,16,512]{2,1,0:T(8,128)} %coupling_ref.3, ...), custom_call_target="tpu_custom_call" | custom-call | flops 6553600 | bytes 3407872 | tf_op jit(solution)/shard_map/pallas_call | solution.py:165
  107.5 14.6 %all-to-all-start.1 = ((f32[64,1,136]{2,1,0:T(1,128)}), f32[64,1,136]{2,1,0:T(1,128)S(1)}, u32[]{:S(2)}, u32[]{:S(2)}) async-start(f32[64,1,136]{2,1,0:T(1,128)} %reshape.407), calls=%async_computation.1 | async-start | bytes 131072 | tf_op jit(solution)/shard_map/all_to_all | solution.py:317
  123.2 2.7 %multiply_subtract_fusion = (f32[32,32,1024]{2,1,0:T(8,128)S(1)}, f32[32,32,1024]{2,1,0:T(8,128)}) fusion(f32[32,1024]{1,0:T(8,128)S(1)} %get-tuple-element.52, f32[32,1024]{1,0:T(8,128)S(1)} %get-tuple-element.49, f32[32,1024]{1,0:T(8,128)S(1)} %get-tuple-element.53, f32[32,1024]{1,0:T(8,128)S(1)} %get-tuple-element.48, f32[1024]{0:T(1024)S(1)} %bitcast.93), kind=kLoop, calls=%fused_computation.17 | loop fusion | flops 4194304 | bytes 8916992 | tf_op jit(solution)/shard_map/sub | solution.py:191
  125.8 2.5 %bitcast_multiply_fusion = f32[1024,1024]{1,0:T(8,128)} fusion(f32[32,32,1024]{2,1,0:T(8,128)S(1)} %get-tuple-element.37, f32[1024]{0:T(1024)S(1)} %bitcast.94), kind=kLoop, calls=%fused_computation.16 | loop fusion | flops 1048576 | bytes 8392704 | tf_op jit(solution)/shard_map/mul | solution.py:195
  128.3 9.0 %all-to-all-done.1 = f32[64,1,136]{2,1,0:T(1,128)S(1)} async-done(((f32[64,1,136]{2,1,0:T(1,128)}), f32[64,1,136]{2,1,0:T(1,128)S(1)}, u32[]{:S(2)}, u32[]{:S(2)}) %all-to-all-start.1) | async-done | bytes 34848 | tf_op jit(solution)/shard_map/all_to_all | solution.py:317
  139.0 3.5 %convolution_divide_fusion = f32[8,1024]{1,0:T(8,128)S(1)} fusion(f32[8,1024]{1,0:T(8,128)S(1)} %reshape.403, f32[1024,1024]{1,0:T(8,128)} %bitcast.80, f32[1024]{0:T(1024)S(1)} %multiply_add_fusion), kind=kOutput, calls=%fused_computation.30 | convolution fusion | flops 50339840 | bytes 4263936 | tf_op jit(solution)/shard_map/dot_general | solution.py:202
  142.5 2.5 %multiply_reduce_fusion = (f32[]{:T(128)}, f32[8,1024]{1,0:T(8,128)S(1)}) fusion(f32[8,1024]{1,0:T(8,128)S(1)} %convolution_divide_fusion, f32[1024,1024]{1,0:T(8,128)S(1)} %copy-done), kind=kOutput, calls=%fused_computation.99 | convolution fusion | flops 50348032 | bytes 4259844 | tf_op jit(solution)/shard_map/dot_general | solution.py:206
  146.8 8.6 %all-to-all-start.2 = ((f32[64,1,136]{2,1,0:T(1,128)}), f32[64,1,136]{2,1,0:T(1,128)S(1)}, u32[]{:S(2)}, u32[]{:S(2)}) async-start(f32[64,1,136]{2,1,0:T(1,128)} %reshape.409), calls=%async_computation.2 | async-start | bytes 131072 | tf_op jit(solution)/shard_map/all_to_all | solution.py:327
  156.2 14.5 %all-to-all-done.2 = f32[64,1,136]{2,1,0:T(1,128)S(1)} async-done(((f32[64,1,136]{2,1,0:T(1,128)}), f32[64,1,136]{2,1,0:T(1,128)S(1)}, u32[]{:S(2)}, u32[]{:S(2)}) %all-to-all-start.2) | async-done | bytes 34848 | tf_op jit(solution)/shard_map/all_to_all | solution.py:327
  172.4 26.5 %all-reduce.2 = (f32[]{:T(128)}, f32[]{:T(128)}) all-reduce(f32[]{:T(128)} %reduce_sum.84, f32[]{:T(128)} %slice_reduce_fusion.1), channel_id=1, replica_groups=mesh['wide'=64,'narrow'=8] {'narrow'}, use_global_device_ids=true, to_apply=%region_7.8 | all-reduce | flops 2 | bytes 16 | tf_op jit(solution)/shard_map/psum | solution.py:331
  (92 shorter events, 26.0 us)
Async XLA Ops:
  2.7 68.7 %collective-permute-start = (f32[2,20,1,512]{3,2,1,0:T(1,128)}, f32[2,20,1,512]{3,2,1,0:T(1,128)S(1)}, u32[]{:S(2)}, u32[]{:S(2)}) collective-permute-start(f32[2,20,1,512]{3,2,1,0:T(1,128)} %get-tuple-element.33), channel_id=1, source_target_pairs={{0,8},{8,16},{16,24},{24,32},{32,40},{40,48},{48,56},{56,64},{64,7... | collective-permute-start | bytes 245768 | tf_op jit(solution)/shard_map/ppermute | solution.py:152
  4.6 66.8 %collective-permute-start.1 = (f32[2,20,1,512]{3,2,1,0:T(1,128)}, f32[2,20,1,512]{3,2,1,0:T(1,128)}, u32[]{:S(2)}, u32[]{:S(2)}) collective-permute-start(f32[2,20,1,512]{3,2,1,0:T(1,128)} %get-tuple-element.32), channel_id=1, source_target_pairs={{8,0},{16,8},{24,16},{32,24},{40,32},{48,40},{56,48},{64,56},{72,6... | collective-permute-start | bytes 245768 | tf_op jit(solution)/shard_map/ppermute | solution.py:153
  14.0 1.2 copy-start.8
  16.8 29.7 %copy-start.1 = (f32[2,20,16,512]{3,2,1,0:T(8,128)S(1)}, f32[2,20,16,512]{3,2,1,0:T(8,128)}, u32[]{:S(2)}) copy-start(f32[2,20,16,512]{3,2,1,0:T(8,128)} %adjoint_ref.1) | copy-start | bytes 3932164
  16.8 34.3 %copy-start.9 = (s32[16,512]{1,0:T(8,128)S(1)}, s32[16,512]{1,0:T(8,128)}, u32[]{:S(2)}) copy-start(s32[16,512]{1,0:T(8,128)} %param.15) | copy-start | bytes 98308
  16.8 35.0 %slice-start = ((f32[2,20,16,512]{3,2,1,0:T(8,128)}), f32[2,1,16,512]{3,2,1,0:T(8,128)S(1)}, s32[]{:S(2)}) async-start(f32[2,20,16,512]{3,2,1,0:T(8,128)} %param.11), calls=%async_computation.3 | async-start | bytes 131072 | tf_op jit(solution)/shard_map/slice | solution.py:292
  19.5 43.1 %all-to-all-start = ((f32[4,64,128]{2,0,1:T(4,128)}), f32[4,64,128]{2,0,1:T(4,128)S(1)}, u32[]{:S(2)}, u32[]{:S(2)}) async-start(f32[4,64,128]{2,0,1:T(4,128)} %copy.18), calls=%async_computation | async-start | bytes 262144 | tf_op jit(solution)/shard_map/all_to_all | solution.py:285
  46.7 24.7 %collective-permute-start.2 = (f32[2,20,16,1]{3,2,1,0:T(8,128)S(1)}, f32[2,20,16,1]{3,2,1,0:T(8,128)S(1)}, u32[]{:S(2)}, u32[]{:S(2)}) collective-permute-start(f32[2,20,16,1]{3,2,1,0:T(8,128)S(1)} %get-tuple-element.31), channel_id=1, source_target_pairs={{0,1},{1,2},{2,3},{3,4},{4,5},{5,6},{6,7},{8,9},{9,10},{10,11},{11... | collective-permute-start | bytes 7688 | tf_op jit(solution)/shard_map/ppermute | solution.py:152
  49.6 21.8 %collective-permute-start.3 = (f32[2,20,16,1]{3,2,1,0:T(8,128)S(1)}, f32[2,20,16,1]{3,2,1,0:T(8,128)S(1)}, u32[]{:S(2)}, u32[]{:S(2)}) collective-permute-start(f32[2,20,16,1]{3,2,1,0:T(8,128)S(1)} %get-tuple-element.30), channel_id=1, source_target_pairs={{1,0},{2,1},{3,2},{4,3},{5,4},{6,5},{7,6},{9,8},{10,9},{11,10},{12... | collective-permute-start | bytes 7688 | tf_op jit(solution)/shard_map/ppermute | solution.py:153
  70.7 34.9 %copy-start.7 = (f32[2,20,16,512]{3,2,1,0:T(8,128)S(1)}, f32[2,20,16,512]{3,2,1,0:T(8,128)}, u32[]{:S(2)}) copy-start(f32[2,20,16,512]{3,2,1,0:T(8,128)} %param.11) | copy-start | bytes 3932164
  70.7 35.7 %copy-start.6 = (f32[16,512]{1,0:T(8,128)S(1)}, f32[16,512]{1,0:T(8,128)}, u32[]{:S(2)}) copy-start(f32[16,512]{1,0:T(8,128)} %friction_ref.3) | copy-start | bytes 98308
  71.4 0.8 copy-start.5
  71.4 0.8 copy-start.10
  76.6 24.1 %collective-permute-start.4 = (f32[2,20,1,512]{3,2,1,0:T(1,128)}, f32[2,20,1,512]{3,2,1,0:T(1,128)S(1)}, u32[]{:S(2)}, u32[]{:S(2)}) collective-permute-start(f32[2,20,1,512]{3,2,1,0:T(1,128)} %get-tuple-element.12), channel_id=1, source_target_pairs={{0,8},{8,16},{16,24},{24,32},{32,40},{40,48},{48,56},{56,64},{64,7... | collective-permute-start | bytes 245768 | tf_op jit(solution)/shard_map/ppermute | solution.py:152
  78.5 22.2 %collective-permute-start.5 = (f32[2,20,1,512]{3,2,1,0:T(1,128)}, f32[2,20,1,512]{3,2,1,0:T(1,128)S(1)}, u32[]{:S(2)}, u32[]{:S(2)}) collective-permute-start(f32[2,20,1,512]{3,2,1,0:T(1,128)} %get-tuple-element.13), channel_id=1, source_target_pairs={{8,0},{16,8},{24,16},{32,24},{40,32},{48,40},{56,48},{64,56},{72,6... | collective-permute-start | bytes 245768 | tf_op jit(solution)/shard_map/ppermute | solution.py:153
  84.3 12.1 %collective-permute-start.6 = (f32[2,20,16,1]{3,2,1,0:T(8,128)}, f32[2,20,16,1]{3,2,1,0:T(8,128)S(1)}, u32[]{:S(2)}, u32[]{:S(2)}) collective-permute-start(f32[2,20,16,1]{3,2,1,0:T(8,128)} %get-tuple-element.14), channel_id=1, source_target_pairs={{0,1},{1,2},{2,3},{3,4},{4,5},{5,6},{6,7},{8,9},{9,10},{10,11},{11... | collective-permute-start | bytes 7688 | tf_op jit(solution)/shard_map/ppermute | solution.py:152
  91.5 9.2 %collective-permute-start.7 = (f32[2,20,16,1]{3,2,1,0:T(8,128)}, f32[2,20,16,1]{3,2,1,0:T(8,128)S(1)}, u32[]{:S(2)}, u32[]{:S(2)}) collective-permute-start(f32[2,20,16,1]{3,2,1,0:T(8,128)} %get-tuple-element.15), channel_id=1, source_target_pairs={{1,0},{2,1},{3,2},{4,3},{5,4},{6,5},{7,6},{9,8},{10,9},{11,10},{12... | collective-permute-start | bytes 7688 | tf_op jit(solution)/shard_map/ppermute | solution.py:153
  96.4 4.3 %copy-start.2 = (f32[2,20,16,1]{3,2,1,0:T(8,128)}, f32[2,20,16,1]{3,2,1,0:T(8,128)S(1)}, u32[]{:S(2)}) copy-start(f32[2,20,16,1]{3,2,1,0:T(8,128)S(1)} %collective-permute-done.6.y_prev_ref) | copy-start | bytes 7684
  100.7 0.7 copy-start.3
  100.7 0.7 copy-start.11
  100.7 0.8 copy-start.12
  107.5 29.9 %all-to-all-start.1 = ((f32[64,1,136]{2,1,0:T(1,128)}), f32[64,1,136]{2,1,0:T(1,128)S(1)}, u32[]{:S(2)}, u32[]{:S(2)}) async-start(f32[64,1,136]{2,1,0:T(1,128)} %reshape.407), calls=%async_computation.1 | async-start | bytes 131072 | tf_op jit(solution)/shard_map/all_to_all | solution.py:317
  139.0 3.5 %copy-start = (f32[1024,1024]{1,0:T(8,128)S(1)}, f32[1024,1024]{1,0:T(8,128)}, u32[]{:S(2)}) copy-start(f32[1024,1024]{1,0:T(8,128)} %bitcast_multiply_fusion) | copy-start | bytes 12582916
  146.8 23.9 %all-to-all-start.2 = ((f32[64,1,136]{2,1,0:T(1,128)}), f32[64,1,136]{2,1,0:T(1,128)S(1)}, u32[]{:S(2)}, u32[]{:S(2)}) async-start(f32[64,1,136]{2,1,0:T(1,128)} %reshape.409), calls=%async_computation.2 | async-start | bytes 131072 | tf_op jit(solution)/shard_map/all_to_all | solution.py:327
  (1 other events, 0.7 us)

commit v9 on v8

--- a/solution.py
+++ b/solution.py
@@ -215,9 +215,7 @@
 def split_parts(value):
     high = lax.reduce_precision(value, exponent_bits=8, mantissa_bits=7)
     rest = value - high
-    middle = lax.reduce_precision(rest, exponent_bits=8, mantissa_bits=7)
-    low = rest - middle
-    return jnp.concatenate([high, middle, low], axis=0).astype(jnp.bfloat16)
+    return jnp.concatenate([high, rest], axis=0).astype(jnp.bfloat16)
 
 
 def exact_dot(value, selector, contract):
@@ -228,8 +226,8 @@
         (((1,), (contract,)), ((), ())),
         preferred_element_type=jnp.float32,
     )
-    parts = parts.reshape(3, rows, parts.shape[-1])
-    return (parts[0] + parts[1]) + parts[2]
+    parts = parts.reshape(2, rows, parts.shape[-1])
+    return parts[0] + parts[1]
 
 
 def owner_ranks(owner_hot):

time: 202 us -> 201 us (level)
  transfers between devices with their start and end apart: 11 -> 11, of which waited for: 5 -> 5; matrix products, arithmetic and copies ran while one was open for 13% -> 12% of each run, Pallas kernels for 0% -> 0%
where the time goes in v9:
time: 201 us; the launch traced here: 199 us
  starting transfers between devices  78.3 us (39%)
  waiting for transfers between devices  41.6 us (21%)
  blocking collectives  26.5 us (13%)
  other arithmetic  17 us (8%)
  matrix products  14 us (7%)
  local copies, waits for them, and re-layouts  10.5 us (5%)
  Pallas kernels  8.52 us (4%)
  between operations  2.49 us (1%)
    all_to_all x1, starting transfers between devices, on_device(): lax.all_to_all(packed, 'wide', split_axis=1, concat_axis=1, tiled=True)  27 us
    psum x1, blocking collectives, on_device(): square_total, misfit_total = lax.psum((wide_square, wide_misfit), 'narrow')  26.5 us
    all_to_all x1, starting transfers between devices, on_device(): lax.all_to_all(sent, 'wide', split_axis=0, concat_axis=1, tiled=True)  14.6 us
    all_to_all x1, waiting for transfers between devices, on_device(): lax.all_to_all(returned, 'wide', split_axis=1, concat_axis=0, tiled=True)  14.5 us
    ppermute x4, starting transfers between devices, halo_edges(): edges.append(lax.ppermute(block[2 * index + 1], axis, down))  14.3 us
    ppermute x4, starting transfers between devices, halo_edges(): edges.append(lax.ppermute(block[2 * index], axis, up))  13.9 us
    all_to_all x1, waiting for transfers between devices, on_device(): lax.all_to_all(packed, 'wide', split_axis=1, concat_axis=1, tiled=True)  10.8 us
    all_to_all x1, waiting for transfers between devices, on_device(): lax.all_to_all(sent, 'wide', split_axis=0, concat_axis=1, tiled=True)  9.03 us
  transfers between devices with their start and end apart: 11, of which 5 were waited for; matrix products, arithmetic and copies ran while one was open for 12% of the time, Pallas kernels for 0%

profile of v9, /device:TPU:6, one launch (start us, length us, event | category | flops | bytes accessed | tf_op | source)
XLA Modules:
  0.0 199.1 jit_solution(9041390259748814389)
XLA Ops:
  0.6 2.1 %fusion.44 = (f32[2,20,1,512]{3,2,1,0:T(1,128)}, f32[2,20,1,512]{3,2,1,0:T(1,128)}) fusion(f32[2,20,16,512]{3,2,1,0:T(8,128)} %adjoint_ref.1), kind=kLoop, calls=%fused_computation.103 | loop fusion | bytes 327680 | tf_op jit(solution)/shard_map/slice | solution.py:142
  2.7 1.9 collective-permute-start
  4.6 5.8 %collective-permute-start.1 = (f32[2,20,1,512]{3,2,1,0:T(1,128)}, f32[2,20,1,512]{3,2,1,0:T(1,128)}, u32[]{:S(2)}, u32[]{:S(2)}) collective-permute-start(f32[2,20,1,512]{3,2,1,0:T(1,128)} %get-tuple-element.31), channel_id=1, source_target_pairs={{8,0},{16,8},{24,16},{32,24},{40,32},{48,40},{56,48},{64,56},{72,6... | collective-permute-start | bytes 245768 | tf_op jit(solution)/shard_map/ppermute | solution.py:153
  18.5 27.0 %all-to-all-start = ((f32[4,64,128]{2,0,1:T(4,128)}), f32[4,64,128]{2,0,1:T(4,128)S(1)}, u32[]{:S(2)}, u32[]{:S(2)}) async-start(f32[4,64,128]{2,0,1:T(4,128)} %copy.18), calls=%async_computation | async-start | bytes 262144 | tf_op jit(solution)/shard_map/all_to_all | solution.py:283
  45.7 2.9 %collective-permute-start.2 = (f32[2,20,16,1]{3,2,1,0:T(8,128)S(1)}, f32[2,20,16,1]{3,2,1,0:T(8,128)S(1)}, u32[]{:S(2)}, u32[]{:S(2)}) collective-permute-start(f32[2,20,16,1]{3,2,1,0:T(8,128)S(1)} %get-tuple-element.30), channel_id=1, source_target_pairs={{0,1},{1,2},{2,3},{3,4},{4,5},{5,6},{6,7},{8,9},{9,10},{10,11},{11... | collective-permute-start | bytes 7688 | tf_op jit(solution)/shard_map/ppermute | solution.py:152
  50.8 10.8 %all-to-all-done = f32[4,64,128]{2,0,1:T(4,128)S(1)} async-done(((f32[4,64,128]{2,0,1:T(4,128)}), f32[4,64,128]{2,0,1:T(4,128)S(1)}, u32[]{:S(2)}, u32[]{:S(2)}) %all-to-all-start) | async-done | bytes 131104 | tf_op jit(solution)/shard_map/all_to_all | solution.py:283
  61.8 3.1 %fusion.1 = f32[64,8192]{1,0:T(8,128)S(1)} fusion(s32[8192]{0:T(1024)S(1)} %get-tuple-element.42, bf16[32,512]{1,0:T(8,128)(2,1)S(1)} %get-tuple-element.40, bf16[32,512]{1,0:T(8,128)(2,1)S(1)} %get-tuple-element.39), kind=kOutput, calls=%fused_computation.2 | convolution fusion | flops 541196288 | bytes 2195456 | tf_op jit(solution)/shard_map/dot_general | solution.py:223
  66.3 3.1 %fusion = f32[64,512]{1,0:T(8,128)S(1)} fusion(s32[8192]{0:T(1024)S(1)} %get-tuple-element.42, bf16[32,8192]{1,0:T(8,128)(2,1)S(1)} %get-tuple-element.34, bf16[32,8192]{1,0:T(8,128)(2,1)S(1)} %get-tuple-element.33), kind=kOutput, calls=%fused_computation.1 | convolution fusion | flops 543162368 | bytes 1212416 | tf_op jit(solution)/shard_map/dot_general | solution.py:223
  70.9 4.4 %shard_map.121 = (f32[2,20,16,512]{3,2,1,0:T(8,128)}, f32[2,20,1,512]{3,2,1,0:T(1,128)}, f32[2,20,1,512]{3,2,1,0:T(1,128)}, f32[2,20,16,1]{3,2,1,0:T(8,128)}, f32[2,20,16,1]{3,2,1,0:T(8,128)}) custom-call(f32[2,20,16,512]{3,2,1,0:T(8,128)} %adjoint_ref.1, f32[2,20,1,512]{3,2,1,0:T(1,128)} %copy-done.10, f32[2,20,1,512]{3,2,1,0:T(1,128)} %collective-permute-done.1.x_next_ref, ...), custom_call_target="tpu_custom_call" | custom-call | flops 6553600 | bytes 3407872 | tf_op jit(solution)/shard_map/pallas_call | solution.py:165
  75.3 1.9 collective-permute-start.4
  77.2 5.8 %collective-permute-start.5 = (f32[2,20,1,512]{3,2,1,0:T(1,128)}, f32[2,20,1,512]{3,2,1,0:T(1,128)S(1)}, u32[]{:S(2)}, u32[]{:S(2)}) collective-permute-start(f32[2,20,1,512]{3,2,1,0:T(1,128)} %get-tuple-element.13), channel_id=1, source_target_pairs={{8,0},{16,8},{24,16},{32,24},{40,32},{48,40},{56,48},{64,56},{72,6... | collective-permute-start | bytes 245768 | tf_op jit(solution)/shard_map/ppermute | solution.py:153
  83.0 7.2 %collective-permute-start.6 = (f32[2,20,16,1]{3,2,1,0:T(8,128)}, f32[2,20,16,1]{3,2,1,0:T(8,128)S(1)}, u32[]{:S(2)}, u32[]{:S(2)}) collective-permute-start(f32[2,20,16,1]{3,2,1,0:T(8,128)} %get-tuple-element.14), channel_id=1, source_target_pairs={{0,1},{1,2},{2,3},{3,4},{4,5},{5,6},{6,7},{8,9},{9,10},{10,11},{11... | collective-permute-start | bytes 7688 | tf_op jit(solution)/shard_map/ppermute | solution.py:152
  92.1 2.9 %collective-permute-done.6.y_prev_ref = f32[2,20,16,1]{3,2,1,0:T(8,128)S(1)} collective-permute-done((f32[2,20,16,1]{3,2,1,0:T(8,128)}, f32[2,20,16,1]{3,2,1,0:T(8,128)S(1)}, u32[]{:S(2)}, u32[]{:S(2)}) %collective-permute-start.6) | collective-permute-done | bytes 2592 | tf_op jit(solution)/shard_map/ppermute | solution.py:152
  95.0 4.3 %collective-permute-done.7.y_next_ref = f32[2,20,16,1]{3,2,1,0:T(8,128)S(1)} collective-permute-done((f32[2,20,16,1]{3,2,1,0:T(8,128)}, f32[2,20,16,1]{3,2,1,0:T(8,128)S(1)}, u32[]{:S(2)}, u32[]{:S(2)}) %collective-permute-start.7) | collective-permute-done | bytes 2592 | tf_op jit(solution)/shard_map/ppermute | solution.py:153
  100.1 4.1 %shard_map.122 = f32[2,20,16,512]{3,2,1,0:T(8,128)} custom-call(f32[2,20,16,512]{3,2,1,0:T(8,128)} %get-tuple-element.11.adjoint_ref, f32[2,20,1,512]{3,2,1,0:T(1,128)} %copy-done.11, f32[2,20,1,512]{3,2,1,0:T(1,128)} %copy-done.12, f32[2,20,16,1]{3,2,1,0:T(8,128)} %copy-done.2, f32[2,20,16,1]{3,2,1,0:T(8,128)} %copy-done.3, f32[19,16,512]{2,1,0:T(8,128)} %coupling_ref.3, ...), custom_call_target="tpu_custom_call" | custom-call | flops 6553600 | bytes 3407872 | tf_op jit(solution)/shard_map/pallas_call | solution.py:165
  106.1 14.6 %all-to-all-start.1 = ((f32[64,1,136]{2,1,0:T(1,128)}), f32[64,1,136]{2,1,0:T(1,128)S(1)}, u32[]{:S(2)}, u32[]{:S(2)}) async-start(f32[64,1,136]{2,1,0:T(1,128)} %reshape.395), calls=%async_computation.1 | async-start | bytes 131072 | tf_op jit(solution)/shard_map/all_to_all | solution.py:315
  121.8 2.7 %multiply_subtract_fusion = (f32[32,32,1024]{2,1,0:T(8,128)S(1)}, f32[32,32,1024]{2,1,0:T(8,128)}) fusion(f32[32,1024]{1,0:T(8,128)S(1)} %get-tuple-element.49, f32[32,1024]{1,0:T(8,128)S(1)} %get-tuple-element.46, f32[32,1024]{1,0:T(8,128)S(1)} %get-tuple-element.50, f32[32,1024]{1,0:T(8,128)S(1)} %get-tuple-element.45, f32[1024]{0:T(1024)S(1)} %bitcast.81), kind=kLoop, calls=%fused_computation.13 | loop fusion | flops 4194304 | bytes 8916992 | tf_op jit(solution)/shard_map/sub | solution.py:191
  124.5 2.5 %bitcast_multiply_fusion = f32[1024,1024]{1,0:T(8,128)} fusion(f32[32,32,1024]{2,1,0:T(8,128)S(1)} %get-tuple-element.35, f32[1024]{0:T(1024)S(1)} %bitcast.82), kind=kLoop, calls=%fused_computation.12 | loop fusion | flops 1048576 | bytes 8392704 | tf_op jit(solution)/shard_map/mul | solution.py:195
  127.0 9.0 %all-to-all-done.1 = f32[64,1,136]{2,1,0:T(1,128)S(1)} async-done(((f32[64,1,136]{2,1,0:T(1,128)}), f32[64,1,136]{2,1,0:T(1,128)S(1)}, u32[]{:S(2)}, u32[]{:S(2)}) %all-to-all-start.1) | async-done | bytes 34848 | tf_op jit(solution)/shard_map/all_to_all | solution.py:315
  137.7 3.5 %convolution_divide_fusion = f32[8,1024]{1,0:T(8,128)S(1)} fusion(f32[8,1024]{1,0:T(8,128)S(1)} %reshape.391, f32[1024,1024]{1,0:T(8,128)} %bitcast.68, f32[1024]{0:T(1024)S(1)} %multiply_add_fusion), kind=kOutput, calls=%fused_computation.19 | convolution fusion | flops 50339840 | bytes 4263936 | tf_op jit(solution)/shard_map/dot_general | solution.py:202
  141.2 2.5 %multiply_reduce_fusion = (f32[]{:T(128)}, f32[8,1024]{1,0:T(8,128)S(1)}) fusion(f32[8,1024]{1,0:T(8,128)S(1)} %convolution_divide_fusion, f32[1024,1024]{1,0:T(8,128)S(1)} %copy-done), kind=kOutput, calls=%fused_computation.84 | convolution fusion | flops 50348032 | bytes 4259844 | tf_op jit(solution)/shard_map/dot_general | solution.py:206
  145.5 8.6 %all-to-all-start.2 = ((f32[64,1,136]{2,1,0:T(1,128)}), f32[64,1,136]{2,1,0:T(1,128)S(1)}, u32[]{:S(2)}, u32[]{:S(2)}) async-start(f32[64,1,136]{2,1,0:T(1,128)} %reshape.397), calls=%async_computation.2 | async-start | bytes 131072 | tf_op jit(solution)/shard_map/all_to_all | solution.py:325
  154.8 14.5 %all-to-all-done.2 = f32[64,1,136]{2,1,0:T(1,128)S(1)} async-done(((f32[64,1,136]{2,1,0:T(1,128)}), f32[64,1,136]{2,1,0:T(1,128)S(1)}, u32[]{:S(2)}, u32[]{:S(2)}) %all-to-all-start.2) | async-done | bytes 34848 | tf_op jit(solution)/shard_map/all_to_all | solution.py:325
  171.1 26.5 %all-reduce.2 = (f32[]{:T(128)}, f32[]{:T(128)}) all-reduce(f32[]{:T(128)} %reduce_sum.84, f32[]{:T(128)} %slice_reduce_fusion.1), channel_id=1, replica_groups=mesh['wide'=64,'narrow'=8] {'narrow'}, use_global_device_ids=true, to_apply=%region_7.8 | all-reduce | flops 2 | bytes 16 | tf_op jit(solution)/shard_map/psum | solution.py:329
  (92 shorter events, 24.9 us)
Async XLA Ops:
  2.7 67.3 %collective-permute-start = (f32[2,20,1,512]{3,2,1,0:T(1,128)}, f32[2,20,1,512]{3,2,1,0:T(1,128)S(1)}, u32[]{:S(2)}, u32[]{:S(2)}) collective-permute-start(f32[2,20,1,512]{3,2,1,0:T(1,128)} %get-tuple-element.32), channel_id=1, source_target_pairs={{0,8},{8,16},{16,24},{24,32},{32,40},{40,48},{48,56},{56,64},{64,7... | collective-permute-start | bytes 245768 | tf_op jit(solution)/shard_map/ppermute | solution.py:152
  4.6 65.4 %collective-permute-start.1 = (f32[2,20,1,512]{3,2,1,0:T(1,128)}, f32[2,20,1,512]{3,2,1,0:T(1,128)}, u32[]{:S(2)}, u32[]{:S(2)}) collective-permute-start(f32[2,20,1,512]{3,2,1,0:T(1,128)} %get-tuple-element.31), channel_id=1, source_target_pairs={{8,0},{16,8},{24,16},{32,24},{40,32},{48,40},{56,48},{64,56},{72,6... | collective-permute-start | bytes 245768 | tf_op jit(solution)/shard_map/ppermute | solution.py:153
  14.0 0.8 copy-start.8
  16.3 29.2 %copy-start.1 = (f32[2,20,16,512]{3,2,1,0:T(8,128)S(1)}, f32[2,20,16,512]{3,2,1,0:T(8,128)}, u32[]{:S(2)}) copy-start(f32[2,20,16,512]{3,2,1,0:T(8,128)} %adjoint_ref.1) | copy-start | bytes 3932164
  16.3 33.8 %copy-start.9 = (s32[16,512]{1,0:T(8,128)S(1)}, s32[16,512]{1,0:T(8,128)}, u32[]{:S(2)}) copy-start(s32[16,512]{1,0:T(8,128)} %param.15) | copy-start | bytes 98308
  16.3 34.4 %slice-start = ((f32[2,20,16,512]{3,2,1,0:T(8,128)}), f32[2,1,16,512]{3,2,1,0:T(8,128)S(1)}, s32[]{:S(2)}) async-start(f32[2,20,16,512]{3,2,1,0:T(8,128)} %param.11), calls=%async_computation.3 | async-start | bytes 131072 | tf_op jit(solution)/shard_map/slice | solution.py:290
  18.5 43.1 %all-to-all-start = ((f32[4,64,128]{2,0,1:T(4,128)}), f32[4,64,128]{2,0,1:T(4,128)S(1)}, u32[]{:S(2)}, u32[]{:S(2)}) async-start(f32[4,64,128]{2,0,1:T(4,128)} %copy.18), calls=%async_computation | async-start | bytes 262144 | tf_op jit(solution)/shard_map/all_to_all | solution.py:283
  45.7 24.4 %collective-permute-start.2 = (f32[2,20,16,1]{3,2,1,0:T(8,128)S(1)}, f32[2,20,16,1]{3,2,1,0:T(8,128)S(1)}, u32[]{:S(2)}, u32[]{:S(2)}) collective-permute-start(f32[2,20,16,1]{3,2,1,0:T(8,128)S(1)} %get-tuple-element.30), channel_id=1, source_target_pairs={{0,1},{1,2},{2,3},{3,4},{4,5},{5,6},{6,7},{8,9},{9,10},{10,11},{11... | collective-permute-start | bytes 7688 | tf_op jit(solution)/shard_map/ppermute | solution.py:152
  48.6 21.4 %collective-permute-start.3 = (f32[2,20,16,1]{3,2,1,0:T(8,128)S(1)}, f32[2,20,16,1]{3,2,1,0:T(8,128)S(1)}, u32[]{:S(2)}, u32[]{:S(2)}) collective-permute-start(f32[2,20,16,1]{3,2,1,0:T(8,128)S(1)} %get-tuple-element.29), channel_id=1, source_target_pairs={{1,0},{2,1},{3,2},{4,3},{5,4},{6,5},{7,6},{9,8},{10,9},{11,10},{12... | collective-permute-start | bytes 7688 | tf_op jit(solution)/shard_map/ppermute | solution.py:153
  69.4 34.8 %copy-start.7 = (f32[2,20,16,512]{3,2,1,0:T(8,128)S(1)}, f32[2,20,16,512]{3,2,1,0:T(8,128)}, u32[]{:S(2)}) copy-start(f32[2,20,16,512]{3,2,1,0:T(8,128)} %param.11) | copy-start | bytes 3932164
  69.4 35.7 %copy-start.6 = (f32[16,512]{1,0:T(8,128)S(1)}, f32[16,512]{1,0:T(8,128)}, u32[]{:S(2)}) copy-start(f32[16,512]{1,0:T(8,128)} %friction_ref.3) | copy-start | bytes 98308
  70.1 0.8 copy-start.5
  70.1 0.8 copy-start.10
  75.3 24.0 %collective-permute-start.4 = (f32[2,20,1,512]{3,2,1,0:T(1,128)}, f32[2,20,1,512]{3,2,1,0:T(1,128)S(1)}, u32[]{:S(2)}, u32[]{:S(2)}) collective-permute-start(f32[2,20,1,512]{3,2,1,0:T(1,128)} %get-tuple-element.12), channel_id=1, source_target_pairs={{0,8},{8,16},{16,24},{24,32},{32,40},{40,48},{48,56},{56,64},{64,7... | collective-permute-start | bytes 245768 | tf_op jit(solution)/shard_map/ppermute | solution.py:152
  77.2 22.1 %collective-permute-start.5 = (f32[2,20,1,512]{3,2,1,0:T(1,128)}, f32[2,20,1,512]{3,2,1,0:T(1,128)S(1)}, u32[]{:S(2)}, u32[]{:S(2)}) collective-permute-start(f32[2,20,1,512]{3,2,1,0:T(1,128)} %get-tuple-element.13), channel_id=1, source_target_pairs={{8,0},{16,8},{24,16},{32,24},{40,32},{48,40},{56,48},{64,56},{72,6... | collective-permute-start | bytes 245768 | tf_op jit(solution)/shard_map/ppermute | solution.py:153
  83.0 12.1 %collective-permute-start.6 = (f32[2,20,16,1]{3,2,1,0:T(8,128)}, f32[2,20,16,1]{3,2,1,0:T(8,128)S(1)}, u32[]{:S(2)}, u32[]{:S(2)}) collective-permute-start(f32[2,20,16,1]{3,2,1,0:T(8,128)} %get-tuple-element.14), channel_id=1, source_target_pairs={{0,1},{1,2},{2,3},{3,4},{4,5},{5,6},{6,7},{8,9},{9,10},{10,11},{11... | collective-permute-start | bytes 7688 | tf_op jit(solution)/shard_map/ppermute | solution.py:152
  90.2 9.2 %collective-permute-start.7 = (f32[2,20,16,1]{3,2,1,0:T(8,128)}, f32[2,20,16,1]{3,2,1,0:T(8,128)S(1)}, u32[]{:S(2)}, u32[]{:S(2)}) collective-permute-start(f32[2,20,16,1]{3,2,1,0:T(8,128)} %get-tuple-element.15), channel_id=1, source_target_pairs={{1,0},{2,1},{3,2},{4,3},{5,4},{6,5},{7,6},{9,8},{10,9},{11,10},{12... | collective-permute-start | bytes 7688 | tf_op jit(solution)/shard_map/ppermute | solution.py:153
  95.0 4.3 %copy-start.2 = (f32[2,20,16,1]{3,2,1,0:T(8,128)}, f32[2,20,16,1]{3,2,1,0:T(8,128)S(1)}, u32[]{:S(2)}) copy-start(f32[2,20,16,1]{3,2,1,0:T(8,128)S(1)} %collective-permute-done.6.y_prev_ref) | copy-start | bytes 7684
  99.3 0.7 copy-start.3
  99.3 0.7 copy-start.11
  99.4 0.8 copy-start.12
  106.1 29.9 %all-to-all-start.1 = ((f32[64,1,136]{2,1,0:T(1,128)}), f32[64,1,136]{2,1,0:T(1,128)S(1)}, u32[]{:S(2)}, u32[]{:S(2)}) async-start(f32[64,1,136]{2,1,0:T(1,128)} %reshape.395), calls=%async_computation.1 | async-start | bytes 131072 | tf_op jit(solution)/shard_map/all_to_all | solution.py:315
  137.7 3.5 %copy-start = (f32[1024,1024]{1,0:T(8,128)S(1)}, f32[1024,1024]{1,0:T(8,128)}, u32[]{:S(2)}) copy-start(f32[1024,1024]{1,0:T(8,128)} %bitcast_multiply_fusion) | copy-start | bytes 12582916
  145.5 23.9 %all-to-all-start.2 = ((f32[64,1,136]{2,1,0:T(1,128)}), f32[64,1,136]{2,1,0:T(1,128)S(1)}, u32[]{:S(2)}, u32[]{:S(2)}) async-start(f32[64,1,136]{2,1,0:T(1,128)} %reshape.397), calls=%async_computation.2 | async-start | bytes 131072 | tf_op jit(solution)/shard_map/all_to_all | solution.py:325
  (1 other events, 0.7 us)
